TPU v7x, 512 devices: a whole 4x4x16 slice. The times are simulated.
512 devices in a mesh: rows: 64 (over x_hi, z, core), chan: 8 (over x_lo, y).
Axes of the slice: x: 4 (x_hi: 2, x_lo: 2; x = x_hi * 2 + x_lo), y: 4, z: 16, core: 2. Of those that a mesh axis runs over, the one named last changes fastest.
Arguments:
- hidden: float32 [32, 2048, 2048], P('chan', 'rows'), may hold values from -6 to 6
- front: float32 [2048, 2048], P('rows', 'chan'), may hold values from -6 to 6
- spectral_weight: float32 [2, 128, 128, 32, 32], P(None, 'rows', 'chan'), may hold values from -0.5 to 0.5
- skip_gain: float32 [32], P('chan'), may hold values from 0.5 to 1.5
- skip_bias: float32 [32], P('chan'), may hold values from -3 to 3
- project_weight: float32 [2, 32], P(None, 'chan'), may hold values from -1 to 1
- project_bias: float32 [2], replicated, may hold values from -3 to 3
- ice_mask: int32 [2048, 2048], P('rows', 'chan'), may hold values 0 or 1
- front_flags: int32 [2048, 2048], P('rows', 'chan'), may hold values 0 or 1
Outputs:
- velocity: float32 [2, 2048, 2048], P(None, 'rows', 'chan')
- front_next: float32 [2048, 2048], P('rows', 'chan')
All inputs are finite; a program needn't handle non-finite values. No bound on the sum of `ice_mask` or of `front_flags` on one device may be relied on, other than what follows from the above.
Results may differ from a plain program's by a relative error of at most 0.0003.
Values sent between devices are 32-bit elements; how exact they have to be, the bound alone decides.
No kernel may reach another device: no remote copies, remote signals or barrier semaphores. Data moves between devices by JAX's collectives and lax.ppermute only.
A program may use at most 128 MiB of HBM per device.

v0:
```python
import math

import jax
import jax.numpy as jnp
from jax import lax
from jax.sharding import PartitionSpec as P

LS_STEPS = 4


time_step = 0.25
highest = lax.Precision.HIGHEST


def with_halo(block, sides, width):
    for axis, dim in sides:
        count = lax.axis_size(axis)
        forward = [(i, i + 1) for i in range(count - 1)]
        backward = [(target, source) for source, target in forward]
        low = lax.ppermute(
            lax.slice_in_dim(block, block.shape[dim] - width, None, axis=dim), axis, forward
        )
        high = lax.ppermute(lax.slice_in_dim(block, 0, width, axis=dim), axis, backward)
        block = jnp.concatenate([low, block, high], axis=dim)
    return block


def angles(freqs, places, length):
    product = freqs[:, None] * places[None, :] % length
    return 2.0 * math.pi / length * product.astype(jnp.float32)


def base_table(modes, length):
    phase = angles(jnp.arange(modes, dtype=jnp.int32), jnp.arange(length, dtype=jnp.int32), length)
    return jnp.concatenate([jnp.cos(phase), -jnp.sin(phase)])


def fold_modes(vec, half):
    pos = jnp.pad(vec[..., :half], [(0, 0)] * (vec.ndim - 1) + [(0, 1)])
    neg = jnp.pad(jnp.flip(vec[..., half:], -1), [(0, 0)] * (vec.ndim - 1) + [(1, 0)])
    return pos, neg


def unfold_modes(plus, minus, half):
    return jnp.concatenate([plus[..., :half], jnp.flip(minus[..., 1 : half + 1], -1)], axis=-1)


def windows(block, count, size, halo):
    padded = jnp.pad(block, [(0, 0)] * (block.ndim - 1) + [(halo, size)])
    lead = block.shape[:-1]
    main = padded[..., : count * size].reshape(lead + (count, size))
    tail = padded[..., size : size + count * size].reshape(lead + (count, size))
    return jnp.concatenate([main, tail[..., : 2 * halo]], axis=-1)


def halo_2d(block, width):
    n_rows = lax.axis_size("rows")
    n_chan = lax.axis_size("chan")

    def shifted(piece, d_row, d_chan):
        pairs = [
            (r * n_chan + c, (r + d_row) * n_chan + c + d_chan)
            for r in range(n_rows)
            for c in range(n_chan)
            if 0 <= r + d_row < n_rows and 0 <= c + d_chan < n_chan
        ]
        return lax.ppermute(piece, ("rows", "chan"), pairs)

    lo, hi = slice(-width, None), slice(0, width)
    every = slice(None)
    parts = {}
    for d_row, rows in ((1, lo), (0, every), (-1, hi)):
        for d_chan, cols in ((1, lo), (0, every), (-1, hi)):
            piece = block[..., rows, cols]
            parts[d_row, d_chan] = piece if d_row == d_chan == 0 else shifted(piece, d_row, d_chan)
    bands = [
        jnp.concatenate([parts[d_row, 1], parts[d_row, 0], parts[d_row, -1]], axis=-1)
        for d_row in (1, 0, -1)
    ]
    return jnp.concatenate(bands, axis=-2)


def advance(padded, speed_x, speed_y, band):
    center = padded[1:-1, 1:-1]
    back_x = center - padded[:-2, 1:-1]
    ahead_x = padded[2:, 1:-1] - center
    back_y = center - padded[1:-1, :-2]
    ahead_y = padded[1:-1, 2:] - center
    transport = jnp.maximum(speed_x, 0.0) * back_x + jnp.minimum(speed_x, 0.0) * ahead_x
    transport = transport + jnp.maximum(speed_y, 0.0) * back_y + jnp.minimum(speed_y, 0.0) * ahead_y
    return center - time_step * band * transport


def on_device(
    hidden,
    front,
    spectral_weight,
    skip_gain,
    skip_bias,
    project_weight,
    project_bias,
    ice_mask,
    front_flags,
):
    halo = LS_STEPS
    local_chan, row_count, columns = hidden.shape
    row_devices = lax.axis_size("rows")
    chan_devices = lax.axis_size("chan")
    local_ymodes = spectral_weight.shape[1]
    all_rows = row_count * row_devices
    all_xmodes = spectral_weight.shape[2] * chan_devices
    all_ymodes = local_ymodes * row_devices
    tile_cols = columns // chan_devices
    win_rows = row_count + 2 * halo
    norm_scale = 1.0 / math.sqrt(all_rows * columns * all_xmodes * all_ymodes)

    fields = jnp.stack(
        [front, front_flags.astype(jnp.float32), ice_mask.astype(jnp.float32)]
    )
    fields = halo_2d(fields, halo)
    hidden_win = with_halo(hidden, (("rows", 1),), halo)

    table = base_table(all_ymodes, columns)
    half = all_xmodes // 2
    if all_rows == columns and all_ymodes > half:
        x_table = table
    else:
        x_table = base_table(half + 1, all_rows)
    x_modes = x_table.shape[0] // 2

    spec_y = jnp.einsum("cxy,ky->ckx", hidden, table, precision=highest)
    spec_y = spec_y.reshape(local_chan, 2, all_ymodes, row_count)
    by_freq = lax.all_to_all(spec_y, "rows", split_axis=2, concat_axis=3, tiled=True)
    parts = jnp.einsum("caqx,kx->caqk", by_freq, x_table, precision=highest)
    cos_part = parts[..., :x_modes]
    sin_part = parts[..., x_modes:]
    real_in = unfold_modes(
        cos_part[:, 0] - sin_part[:, 1], cos_part[:, 0] + sin_part[:, 1], half
    )
    imag_in = unfold_modes(
        cos_part[:, 1] + sin_part[:, 0], cos_part[:, 1] - sin_part[:, 0], half
    )
    spectra = jnp.stack([real_in, imag_in], axis=2)

    gathered = lax.all_to_all(spectra, "chan", split_axis=3, concat_axis=0, tiled=True)
    real_in = gathered[:, :, 0]
    imag_in = gathered[:, :, 1]
    real_out = jnp.einsum(
        "qpio,iqp->oqp", spectral_weight[0], real_in, precision=highest
    ) - jnp.einsum("qpio,iqp->oqp", spectral_weight[1], imag_in, precision=highest)
    imag_out = jnp.einsum(
        "qpio,iqp->oqp", spectral_weight[0], imag_in, precision=highest
    ) + jnp.einsum("qpio,iqp->oqp", spectral_weight[1], real_in, precision=highest)
    mixed = lax.all_to_all(
        jnp.stack([real_out, imag_out], axis=2), "chan", split_axis=0, concat_axis=3, tiled=True
    )

    real_pos, real_neg = fold_modes(mixed[:, :, 0], half)
    imag_pos, imag_neg = fold_modes(mixed[:, :, 1], half)
    pad = [(0, 0), (0, 0), (0, x_modes - half - 1)]
    coef_real = jnp.concatenate(
        [jnp.pad(real_pos + real_neg, pad), jnp.pad(imag_pos - imag_neg, pad)], axis=-1
    )
    coef_imag = jnp.concatenate(
        [jnp.pad(imag_pos + imag_neg, pad), jnp.pad(real_neg - real_pos, pad)], axis=-1
    )
    coef = jnp.stack([coef_real, coef_imag], axis=1)
    inverted = jnp.einsum("otqk,kx->otqx", coef, x_table, precision=highest)
    inverted = windows(inverted, row_devices, row_count, halo)
    inverted = lax.all_to_all(inverted, "rows", split_axis=3, concat_axis=2, tiled=True)
    y_weights = jnp.where(jnp.arange(all_ymodes) == 0, 1.0, 2.0).astype(jnp.float32) * norm_scale
    inverted = inverted.reshape(local_chan, 2, all_ymodes, win_rows) * y_weights[:, None]
    inverted = inverted.reshape(local_chan, 2 * all_ymodes, win_rows)

    spectral = jnp.einsum("ckx,ky->cxy", inverted, table, precision=highest)
    activated = jax.nn.gelu(
        spectral + skip_gain[:, None, None] * hidden_win + skip_bias[:, None, None],
        approximate=False,
    )
    partial_speed = jnp.einsum("jc,cxy->jxy", project_weight, activated, precision=highest)
    sent = windows(partial_speed, chan_devices, tile_cols, halo)
    received = lax.all_to_all(sent, "chan", split_axis=2, concat_axis=2, tiled=True)
    speed = jnp.sum(received, axis=2) + project_bias[:, None, None]
    speed = speed * fields[2][None]
    velocity = speed[:, halo : halo + row_count, halo : halo + tile_cols]

    level = fields[0]
    band = fields[1]
    for level_step in range(LS_STEPS):
        inner = level_step + 1
        rows_end = win_rows - inner
        cols_end = tile_cols + 2 * halo - inner
        level = advance(
            level,
            speed[0, inner:rows_end, inner:cols_end],
            speed[1, inner:rows_end, inner:cols_end],
            band[inner:rows_end, inner:cols_end],
        )
    return (velocity, level)


def solution(mesh):
    return jax.shard_map(
        on_device,
        mesh=mesh,
        in_specs=(
            P("chan", "rows", None),
            P("rows", "chan"),
            P(None, "rows", "chan", None, None),
            P("chan"),
            P("chan"),
            P(None, "chan"),
            P(),
            P("rows", "chan"),
            P("rows", "chan"),
        ),
        out_specs=(P(None, "rows", "chan"), P("rows", "chan")),
        check_vma=False,
    )
```

profile of v0, /device:TPU:6, one launch (start us, length us, event | category | flops | bytes accessed | tf_op | source)
XLA Modules:
  0.0 177.8 jit_solution(9341766292547779368)
XLA Ops:
  0.7 4.1 %sine_negate_fusion = (f32[128,2048]{1,0:T(8,128)S(1)}, f32[128,2048]{1,0:T(8,128)S(1)}) fusion(), kind=kLoop, calls=%fused_computation.39 | loop fusion | flops 3932160 | bytes 2097152 | tf_op jit(solution)/shard_map/neg | solution.py:35
  4.8 2.2 %fusion.20 = f32[4,256,32]{1,2,0:T(8,128)S(1)} fusion(f32[4,32,2048]{2,1,0:T(8,128)S(1)} %copy-done.1, f32[128,2048]{1,0:T(8,128)S(1)} %get-tuple-element.40, f32[128,2048]{1,0:T(8,128)S(1)} %get-tuple-element.41), kind=kOutput, calls=%fused_computation.35 | convolution fusion | flops 805830656 | bytes 3276800 | tf_op jit(solution)/shard_map/cxy,ky->ckx/dot_general | solution.py:131
  8.0 34.2 %all_to_all.74 = f32[64,1,512]{2,1,0:T(1,128)S(1)} all-to-all(f32[64,1,512]{2,1,0:T(1,128)S(1)} %reshape.88), channel_id=1, replica_groups=mesh['rows'=64,'chan'=8] {'rows'}, dimensions={0} | all-to-all | bytes 262144 | tf_op jit(solution)/shard_map/all_to_all | solution.py:133
  42.7 1.0 reduce.8
  44.6 1.9 %fusion.2 = f32[4,2,2,256]{3,2,1,0:T(2,128)S(1)} fusion(f32[4,2,2,2048]{3,2,1,0:T(2,128)S(1)} %all_to_all.56, f32[128,2048]{1,0:T(8,128)S(1)} %get-tuple-element.40, f32[128,2048]{1,0:T(8,128)S(1)} %get-tuple-element.41), kind=kOutput, calls=%fused_computation.4 | convolution fusion | flops 101187584 | bytes 2244608 | tf_op jit(solution)/shard_map/caqx,kx->caqk/dot_general | solution.py:134
  47.7 10.5 %all_to_all.75 = f32[8,1,256]{2,1,0:T(1,128)S(1)} all-to-all(f32[8,1,256]{2,1,0:T(1,128)S(1)} %reshape.90), channel_id=1, replica_groups=mesh['rows'=64,'chan'=8] {'chan'}, dimensions={0} | all-to-all | bytes 16384 | tf_op jit(solution)/shard_map/all_to_all | solution.py:145
  61.4 4.7 %all-to-all-start.2 = ((f32[8,1,256]{2,1,0:T(1,128)}), f32[8,1,256]{2,1,0:T(1,128)S(1)}, u32[]{:S(2)}, u32[]{:S(2)}) async-start(f32[8,1,256]{2,1,0:T(1,128)} %reshape.92), calls=%async_computation.2 | async-start | bytes 16384 | tf_op jit(solution)/shard_map/all_to_all | solution.py:154
  66.1 1.1 fusion.89
  67.2 1.9 %collective-permute-start = (f32[4,4,2048]{2,1,0:T(4,128)S(1)}, f32[4,4,2048]{2,1,0:T(4,128)}, u32[]{:S(2)}, u32[]{:S(2)}) collective-permute-start(f32[4,4,2048]{2,1,0:T(4,128)S(1)} %get-tuple-element.10), channel_id=1, source_target_pairs={{0,8},{8,16},{16,24},{24,32},{32,40},{40,48},{48,56},{56,64},{64,7... | collective-permute-start | bytes 393224 | tf_op jit(solution)/shard_map/ppermute | solution.py:20
  69.1 7.3 %collective-permute-start.1 = (f32[4,4,2048]{2,1,0:T(4,128)S(1)}, f32[4,4,2048]{2,1,0:T(4,128)}, u32[]{:S(2)}, u32[]{:S(2)}) collective-permute-start(f32[4,4,2048]{2,1,0:T(4,128)S(1)} %get-tuple-element.11), channel_id=1, source_target_pairs={{8,0},{16,8},{24,16},{32,24},{40,32},{48,40},{56,48},{64,56},{72,6... | collective-permute-start | bytes 393224 | tf_op jit(solution)/shard_map/ppermute | solution.py:23
  77.8 1.1 fusion
  80.5 1.6 reshape.94
  82.1 5.5 %all-to-all-start.3 = ((f32[64,1,640]{2,1,0:T(1,128)}), f32[64,1,640]{2,1,0:T(1,128)S(1)}, u32[]{:S(2)}, u32[]{:S(2)}) async-start(f32[64,1,640]{2,1,0:T(1,128)} %reshape.94), calls=%async_computation.3 | async-start | bytes 327680 | tf_op jit(solution)/shard_map/all_to_all | solution.py:170
  87.7 16.8 %all-to-all-done.3 = f32[64,1,640]{2,1,0:T(1,128)S(1)} async-done(((f32[64,1,640]{2,1,0:T(1,128)}), f32[64,1,640]{2,1,0:T(1,128)S(1)}, u32[]{:S(2)}, u32[]{:S(2)}) %all-to-all-start.3) | async-done | bytes 163872 | tf_op jit(solution)/shard_map/all_to_all | solution.py:170
  104.5 1.0 reduce.11
  107.7 5.5 %fusion.9 = f32[4,40,2048]{2,1,0:T(8,128)S(1)} fusion(f32[4,4,2048]{2,1,0:T(4,128)} %collective-permute-done.1, f32[4,32,2048]{2,1,0:T(8,128)S(1)} %copy-done.2, f32[4,4,2048]{2,1,0:T(4,128)} %collective-permute-done, f32[4]{0:T(128)S(1)} %copy-done.9, f32[4]{0:T(128)S(1)} %copy-done.10, f32[128,2048]{1,0:T(8,128)S(1)} %get-tuple-element.40, ...), kind=kOutput, calls=%fused_computation.15 | convolution fusion | flops 1029808128 | bytes 4883488 | tf_op jit(solution)/shard_map/ckx,ky->cxy/dot_general | solution.py:175
  113.2 3.1 %convolution_bitcast_fusion = f32[2,40,2048]{2,0,1:T(2,128)S(1)} fusion(f32[4,40,2048]{2,1,0:T(8,128)S(1)} %fusion.9, f32[2,4]{1,0:T(2,128)S(1)} %copy-done), kind=kOutput, calls=%fused_computation | convolution fusion | flops 7864320 | bytes 1966112 | tf_op jit(solution)/shard_map/jc,cxy->jxy/dot_general | solution.py:180
  116.3 1.4 pad_slice_fusion.1
  118.7 1.4 pad_maximum_fusion.1
  120.1 5.7 %all-to-all-start.4 = ((f32[2,40,8,264]{3,0,1,2:T(2,128)}), f32[2,40,8,264]{3,0,1,2:T(2,128)S(1)}, u32[]{:S(2)}, u32[]{:S(2)}) async-start(f32[2,40,8,264]{3,0,1,2:T(2,128)} %pad_maximum_fusion.1), calls=%async_computation.4 | async-start | bytes 1966080 | tf_op jit(solution)/shard_map/all_to_all | solution.py:182
  125.9 3.4 %collective-permute-start.5 = (f32[3,32,4]{2,1,0:T(8,128)S(1)}, f32[3,32,4]{2,1,0:T(8,128)S(1)}, u32[]{:S(2)}, u32[]{:S(2)}) collective-permute-start(f32[3,32,4]{2,1,0:T(8,128)S(1)} %get-tuple-element.25), channel_id=1, source_target_pairs={{0,1},{1,2},{2,3},{3,4},{4,5},{5,6},{6,7},{8,9},{9,10},{10,11},{11... | collective-permute-start | bytes 4616 | tf_op jit(solution)/shard_map/ppermute | solution.py:67
  129.3 4.6 %collective-permute-start.6 = (f32[3,32,4]{2,1,0:T(8,128)S(1)}, f32[3,32,4]{2,1,0:T(8,128)S(1)}, u32[]{:S(2)}, u32[]{:S(2)}) collective-permute-start(f32[3,32,4]{2,1,0:T(8,128)S(1)} %get-tuple-element.26), channel_id=1, source_target_pairs={{1,0},{2,1},{3,2},{4,3},{5,4},{6,5},{7,6},{9,8},{10,9},{11,10},{12... | collective-permute-start | bytes 4616 | tf_op jit(solution)/shard_map/ppermute | solution.py:67
  133.9 1.9 %collective-permute-start.3 = (f32[3,4,256]{2,1,0:T(4,128)S(1)}, f32[3,4,256]{2,1,0:T(4,128)S(1)}, u32[]{:S(2)}, u32[]{:S(2)}) collective-permute-start(f32[3,4,256]{2,1,0:T(4,128)S(1)} %get-tuple-element.23), channel_id=1, source_target_pairs={{0,8},{1,9},{2,10},{3,11},{4,12},{5,13},{6,14},{7,15},{8,16},{9,17... | collective-permute-start | bytes 36872 | tf_op jit(solution)/shard_map/ppermute | solution.py:67
  135.8 7.3 %collective-permute-start.8 = (f32[3,4,256]{2,1,0:T(4,128)S(1)}, f32[3,4,256]{2,1,0:T(4,128)S(1)}, u32[]{:S(2)}, u32[]{:S(2)}) collective-permute-start(f32[3,4,256]{2,1,0:T(4,128)S(1)} %get-tuple-element.24), channel_id=1, source_target_pairs={{8,0},{9,1},{10,2},{11,3},{12,4},{13,5},{14,6},{15,7},{16,8},{17,9... | collective-permute-start | bytes 36872 | tf_op jit(solution)/shard_map/ppermute | solution.py:67
  143.2 1.9 %collective-permute-start.2 = (f32[3,4,4]{2,1,0:T(4,128)S(1)}, f32[3,4,4]{2,1,0:T(4,128)S(1)}, u32[]{:S(2)}, u32[]{:S(2)}) collective-permute-start(f32[3,4,4]{2,1,0:T(4,128)S(1)} %get-tuple-element.19), channel_id=1, source_target_pairs={{0,9},{1,10},{2,11},{3,12},{4,13},{5,14},{6,15},{8,17},{9,18},{10,... | collective-permute-start | bytes 584 | tf_op jit(solution)/shard_map/ppermute | solution.py:67
  145.1 8.4 %collective-permute-done.2 = f32[3,4,4]{2,1,0:T(4,128)S(1)} collective-permute-done((f32[3,4,4]{2,1,0:T(4,128)S(1)}, f32[3,4,4]{2,1,0:T(4,128)S(1)}, u32[]{:S(2)}, u32[]{:S(2)}) %collective-permute-start.2) | collective-permute-done | bytes 224 | tf_op jit(solution)/shard_map/ppermute | solution.py:67
  153.5 1.9 %collective-permute-start.4 = (f32[3,4,4]{2,1,0:T(4,128)S(1)}, f32[3,4,4]{2,1,0:T(4,128)S(1)}, u32[]{:S(2)}, u32[]{:S(2)}) collective-permute-start(f32[3,4,4]{2,1,0:T(4,128)S(1)} %get-tuple-element.22), channel_id=1, source_target_pairs={{1,8},{2,9},{3,10},{4,11},{5,12},{6,13},{7,14},{9,16},{10,17},{11,... | collective-permute-start | bytes 584 | tf_op jit(solution)/shard_map/ppermute | solution.py:67
  155.5 7.5 %collective-permute-done.4 = f32[3,4,4]{2,1,0:T(4,128)S(1)} collective-permute-done((f32[3,4,4]{2,1,0:T(4,128)S(1)}, f32[3,4,4]{2,1,0:T(4,128)S(1)}, u32[]{:S(2)}, u32[]{:S(2)}) %collective-permute-start.4) | collective-permute-done | bytes 224 | tf_op jit(solution)/shard_map/ppermute | solution.py:67
  163.0 1.9 %collective-permute-start.7 = (f32[3,4,4]{2,1,0:T(4,128)S(1)}, f32[3,4,4]{2,1,0:T(4,128)S(1)}, u32[]{:S(2)}, u32[]{:S(2)}) collective-permute-start(f32[3,4,4]{2,1,0:T(4,128)S(1)} %get-tuple-element.21), channel_id=1, source_target_pairs={{8,1},{9,2},{10,3},{11,4},{12,5},{13,6},{14,7},{16,9},{17,10},{18,... | collective-permute-start | bytes 584 | tf_op jit(solution)/shard_map/ppermute | solution.py:67
  164.9 5.1 %collective-permute-done.7 = f32[3,4,4]{2,1,0:T(4,128)S(1)} collective-permute-done((f32[3,4,4]{2,1,0:T(4,128)S(1)}, f32[3,4,4]{2,1,0:T(4,128)S(1)}, u32[]{:S(2)}, u32[]{:S(2)}) %collective-permute-start.7) | collective-permute-done | bytes 224 | tf_op jit(solution)/shard_map/ppermute | solution.py:67
  170.0 2.5 %collective-permute-start.9 = (f32[3,4,4]{2,1,0:T(4,128)S(1)}, f32[3,4,4]{2,1,0:T(4,128)S(1)}, u32[]{:S(2)}, u32[]{:S(2)}) collective-permute-start(f32[3,4,4]{2,1,0:T(4,128)S(1)} %get-tuple-element.20), channel_id=1, source_target_pairs={{9,0},{10,1},{11,2},{12,3},{13,4},{14,5},{15,6},{17,8},{18,9},{19,... | collective-permute-start | bytes 584 | tf_op jit(solution)/shard_map/ppermute | solution.py:67
  172.5 2.4 %collective-permute-done.9 = f32[3,4,4]{2,1,0:T(4,128)S(1)} collective-permute-done((f32[3,4,4]{2,1,0:T(4,128)S(1)}, f32[3,4,4]{2,1,0:T(4,128)S(1)}, u32[]{:S(2)}, u32[]{:S(2)}) %collective-permute-start.9) | collective-permute-done | bytes 224 | tf_op jit(solution)/shard_map/ppermute | solution.py:67
  (107 shorter events, 15.6 us)
Async XLA Ops:
  0.6 112.6 %copy-start = (f32[2,4]{1,0:T(2,128)S(1)}, f32[2,4]{1,0:T(2,128)}, u32[]{:S(2)}) copy-start(f32[2,4]{1,0:T(2,128)} %param.14) | copy-start | bytes 100
  0.6 4.1 %copy-start.1 = (f32[4,32,2048]{2,1,0:T(8,128)S(1)}, f32[4,32,2048]{2,1,0:T(8,128)}, u32[]{:S(2)}) copy-start(f32[4,32,2048]{2,1,0:T(8,128)} %param.9) | copy-start | bytes 3145732
  46.5 13.1 %copy-start.3 = (f32[2,2,16,32,32]{4,3,2,1,0:T(8,128)S(1)}, f32[2,2,16,32,32]{4,3,2,1,0:T(8,128)}, u32[]{:S(2)}) copy-start(f32[2,2,16,32,32]{4,3,2,1,0:T(8,128)} %param.11) | copy-start | bytes 786436
  59.7 18.0 %copy-start.8 = (pred[65]{0:T(512)(128)(4,1)S(1)}, pred[65]{0:T(512)(128)(4,1)}, u32[]{:S(2)}) copy-start(pred[65]{0:T(512)(128)(4,1)} %constant.37.clone.1) | copy-start | bytes 199
  61.4 15.0 %all-to-all-start.2 = ((f32[8,1,256]{2,1,0:T(1,128)}), f32[8,1,256]{2,1,0:T(1,128)S(1)}, u32[]{:S(2)}, u32[]{:S(2)}) async-start(f32[8,1,256]{2,1,0:T(1,128)} %reshape.92), calls=%async_computation.2 | async-start | bytes 16384 | tf_op jit(solution)/shard_map/all_to_all | solution.py:154
  67.2 39.7 %collective-permute-start = (f32[4,4,2048]{2,1,0:T(4,128)S(1)}, f32[4,4,2048]{2,1,0:T(4,128)}, u32[]{:S(2)}, u32[]{:S(2)}) collective-permute-start(f32[4,4,2048]{2,1,0:T(4,128)S(1)} %get-tuple-element.10), channel_id=1, source_target_pairs={{0,8},{8,16},{16,24},{24,32},{32,40},{40,48},{48,56},{56,64},{64,7... | collective-permute-start | bytes 393224 | tf_op jit(solution)/shard_map/ppermute | solution.py:20
  69.1 37.8 %collective-permute-start.1 = (f32[4,4,2048]{2,1,0:T(4,128)S(1)}, f32[4,4,2048]{2,1,0:T(4,128)}, u32[]{:S(2)}, u32[]{:S(2)}) collective-permute-start(f32[4,4,2048]{2,1,0:T(4,128)S(1)} %get-tuple-element.11), channel_id=1, source_target_pairs={{8,0},{16,8},{24,16},{32,24},{40,32},{48,40},{56,48},{64,56},{72,6... | collective-permute-start | bytes 393224 | tf_op jit(solution)/shard_map/ppermute | solution.py:23
  80.0 7.6 %copy-start.5 = (s32[32,256]{1,0:T(8,128)S(1)}, s32[32,256]{1,0:T(8,128)}, u32[]{:S(2)}) copy-start(s32[32,256]{1,0:T(8,128)} %param.16) | copy-start | bytes 98308
  80.1 7.6 %copy-start.6 = (s32[32,256]{1,0:T(8,128)S(1)}, s32[32,256]{1,0:T(8,128)}, u32[]{:S(2)}) copy-start(s32[32,256]{1,0:T(8,128)} %param.17) | copy-start | bytes 98308
  80.1 7.6 %copy-start.4 = (f32[32,256]{1,0:T(8,128)S(1)}, f32[32,256]{1,0:T(8,128)}, u32[]{:S(2)}) copy-start(f32[32,256]{1,0:T(8,128)} %param.10) | copy-start | bytes 98308
  82.1 22.4 %all-to-all-start.3 = ((f32[64,1,640]{2,1,0:T(1,128)}), f32[64,1,640]{2,1,0:T(1,128)S(1)}, u32[]{:S(2)}, u32[]{:S(2)}) async-start(f32[64,1,640]{2,1,0:T(1,128)} %reshape.94), calls=%async_computation.3 | async-start | bytes 327680 | tf_op jit(solution)/shard_map/all_to_all | solution.py:170
  105.5 1.4 copy-start.9
  105.6 1.4 copy-start.10
  106.5 1.2 copy-start.2
  120.1 55.1 %all-to-all-start.4 = ((f32[2,40,8,264]{3,0,1,2:T(2,128)}), f32[2,40,8,264]{3,0,1,2:T(2,128)S(1)}, u32[]{:S(2)}, u32[]{:S(2)}) async-start(f32[2,40,8,264]{3,0,1,2:T(2,128)} %pad_maximum_fusion.1), calls=%async_computation.4 | async-start | bytes 1966080 | tf_op jit(solution)/shard_map/all_to_all | solution.py:182
  125.8 49.8 %copy-start.7 = (f32[2]{0:T(128)S(1)}, f32[2]{0:T(128)}, u32[]{:S(2)}) copy-start(f32[2]{0:T(128)} %param.15) | copy-start | bytes 28
  125.9 49.1 %collective-permute-start.5 = (f32[3,32,4]{2,1,0:T(8,128)S(1)}, f32[3,32,4]{2,1,0:T(8,128)S(1)}, u32[]{:S(2)}, u32[]{:S(2)}) collective-permute-start(f32[3,32,4]{2,1,0:T(8,128)S(1)} %get-tuple-element.25), channel_id=1, source_target_pairs={{0,1},{1,2},{2,3},{3,4},{4,5},{5,6},{6,7},{8,9},{9,10},{10,11},{11... | collective-permute-start | bytes 4616 | tf_op jit(solution)/shard_map/ppermute | solution.py:67
  129.3 45.7 %collective-permute-start.6 = (f32[3,32,4]{2,1,0:T(8,128)S(1)}, f32[3,32,4]{2,1,0:T(8,128)S(1)}, u32[]{:S(2)}, u32[]{:S(2)}) collective-permute-start(f32[3,32,4]{2,1,0:T(8,128)S(1)} %get-tuple-element.26), channel_id=1, source_target_pairs={{1,0},{2,1},{3,2},{4,3},{5,4},{6,5},{7,6},{9,8},{10,9},{11,10},{12... | collective-permute-start | bytes 4616 | tf_op jit(solution)/shard_map/ppermute | solution.py:67
  133.9 41.1 %collective-permute-start.3 = (f32[3,4,256]{2,1,0:T(4,128)S(1)}, f32[3,4,256]{2,1,0:T(4,128)S(1)}, u32[]{:S(2)}, u32[]{:S(2)}) collective-permute-start(f32[3,4,256]{2,1,0:T(4,128)S(1)} %get-tuple-element.23), channel_id=1, source_target_pairs={{0,8},{1,9},{2,10},{3,11},{4,12},{5,13},{6,14},{7,15},{8,16},{9,17... | collective-permute-start | bytes 36872 | tf_op jit(solution)/shard_map/ppermute | solution.py:67
  135.8 39.2 %collective-permute-start.8 = (f32[3,4,256]{2,1,0:T(4,128)S(1)}, f32[3,4,256]{2,1,0:T(4,128)S(1)}, u32[]{:S(2)}, u32[]{:S(2)}) collective-permute-start(f32[3,4,256]{2,1,0:T(4,128)S(1)} %get-tuple-element.24), channel_id=1, source_target_pairs={{8,0},{9,1},{10,2},{11,3},{12,4},{13,5},{14,6},{15,7},{16,8},{17,9... | collective-permute-start | bytes 36872 | tf_op jit(solution)/shard_map/ppermute | solution.py:67
  143.2 10.4 %collective-permute-start.2 = (f32[3,4,4]{2,1,0:T(4,128)S(1)}, f32[3,4,4]{2,1,0:T(4,128)S(1)}, u32[]{:S(2)}, u32[]{:S(2)}) collective-permute-start(f32[3,4,4]{2,1,0:T(4,128)S(1)} %get-tuple-element.19), channel_id=1, source_target_pairs={{0,9},{1,10},{2,11},{3,12},{4,13},{5,14},{6,15},{8,17},{9,18},{10,... | collective-permute-start | bytes 584 | tf_op jit(solution)/shard_map/ppermute | solution.py:67
  153.5 9.4 %collective-permute-start.4 = (f32[3,4,4]{2,1,0:T(4,128)S(1)}, f32[3,4,4]{2,1,0:T(4,128)S(1)}, u32[]{:S(2)}, u32[]{:S(2)}) collective-permute-start(f32[3,4,4]{2,1,0:T(4,128)S(1)} %get-tuple-element.22), channel_id=1, source_target_pairs={{1,8},{2,9},{3,10},{4,11},{5,12},{6,13},{7,14},{9,16},{10,17},{11,... | collective-permute-start | bytes 584 | tf_op jit(solution)/shard_map/ppermute | solution.py:67
  163.0 7.0 %collective-permute-start.7 = (f32[3,4,4]{2,1,0:T(4,128)S(1)}, f32[3,4,4]{2,1,0:T(4,128)S(1)}, u32[]{:S(2)}, u32[]{:S(2)}) collective-permute-start(f32[3,4,4]{2,1,0:T(4,128)S(1)} %get-tuple-element.21), channel_id=1, source_target_pairs={{8,1},{9,2},{10,3},{11,4},{12,5},{13,6},{14,7},{16,9},{17,10},{18,... | collective-permute-start | bytes 584 | tf_op jit(solution)/shard_map/ppermute | solution.py:67
  170.0 4.9 %collective-permute-start.9 = (f32[3,4,4]{2,1,0:T(4,128)S(1)}, f32[3,4,4]{2,1,0:T(4,128)S(1)}, u32[]{:S(2)}, u32[]{:S(2)}) collective-permute-start(f32[3,4,4]{2,1,0:T(4,128)S(1)} %get-tuple-element.20), channel_id=1, source_target_pairs={{9,0},{10,1},{11,2},{12,3},{13,4},{14,5},{15,6},{17,8},{18,9},{19,... | collective-permute-start | bytes 584 | tf_op jit(solution)/shard_map/ppermute | solution.py:67
where the time goes:
time: 179 us; the launch traced here: 178 us
  starting transfers between devices  50.4 us (28%)
  blocking collectives  44.7 us (25%)
  waiting for transfers between devices  40.4 us (23%)
  local copies, waits for them, and re-layouts  15.1 us (8%)
  matrix products  13.9 us (8%)
  other arithmetic  12.1 us (7%)
    all_to_all x1, blocking collectives, on_device(): lax.all_to_all(spec_y, 'rows', split_axis=2, concat_axis=3, tiled=True)  34.2 us
    ppermute x8, starting transfers between devices, shifted(): return lax.ppermute(piece, ('rows', 'chan'), pairs)  25.3 us
    ppermute x8, waiting for transfers between devices, shifted(): return lax.ppermute(piece, ('rows', 'chan'), pairs)  23.6 us
    all_to_all x1, waiting for transfers between devices, on_device(): lax.all_to_all(inverted, 'rows', split_axis=3, concat_axis=2, tiled=True)  16.8 us
    all_to_all x1, blocking collectives, on_device(): lax.all_to_all(spectra, 'chan', split_axis=3, concat_axis=0, tiled=True)  10.5 us
    ppermute x1, starting transfers between devices, with_halo(): lax.ppermute(lax.slice_in_dim(block, 0, width, axis=dim), axis, backward)  7.26 us
    unnamed x34, local copies, waits for them, and re-layouts  6.36 us
    all_to_all x1, starting transfers between devices, on_device(): lax.all_to_all(sent, 'chan', split_axis=2, concat_axis=2, tiled=True)  5.72 us
  transfers between devices with their start and end apart: 13, of which 5 were waited for; matrix products, arithmetic and copies ran while one was open for 5% of the time, Pallas kernels for 0%

commit v1 on v0

--- a/solution.py
+++ b/solution.py
@@ -78,6 +78,29 @@
         for d_row in (1, 0, -1)
     ]
     return jnp.concatenate(bands, axis=-2)
+
+
+def rows_halo_pair(first, second, width):
+    count = lax.axis_size("rows")
+    forward = [(i, i + 1) for i in range(count - 1)]
+    backward = [(target, source) for source, target in forward]
+
+    def packed(rows):
+        a, b = first[..., rows, :], second[..., rows, :]
+        return jnp.concatenate([a.reshape(-1), b.reshape(-1)]), a.shape, b.shape
+
+    def unpacked(flat, a_shape, b_shape):
+        split = math.prod(a_shape)
+        return flat[:split].reshape(a_shape), flat[split:].reshape(b_shape)
+
+    low, a_shape, b_shape = packed(slice(-width, None))
+    high, _, _ = packed(slice(0, width))
+    low_a, low_b = unpacked(lax.ppermute(low, "rows", forward), a_shape, b_shape)
+    high_a, high_b = unpacked(lax.ppermute(high, "rows", backward), a_shape, b_shape)
+    return (
+        jnp.concatenate([low_a, first, high_a], axis=-2),
+        jnp.concatenate([low_b, second, high_b], axis=-2),
+    )
 
 
 def advance(padded, speed_x, speed_y, band):
@@ -117,8 +140,9 @@
     fields = jnp.stack(
         [front, front_flags.astype(jnp.float32), ice_mask.astype(jnp.float32)]
     )
-    fields = halo_2d(fields, halo)
-    hidden_win = with_halo(hidden, (("rows", 1),), halo)
+    hidden_win, fields = rows_halo_pair(hidden, fields, halo)
+    fields = with_halo(fields, (("chan", 2),), halo)
+    fields, hidden_win = lax.optimization_barrier((fields, hidden_win))
 
     table = base_table(all_ymodes, columns)
     half = all_xmodes // 2

time: 179 us -> 160 us (0.89)
  the two profiles are of different devices: /device:TPU:6 before, /device:TPU:1 now
where the time goes in v1:
time: 160 us; the launch traced here: 158 us
  starting transfers between devices  46.6 us (29%)
  waiting for transfers between devices  43.7 us (27%)
  local copies, waits for them, and re-layouts  33.9 us (21%)
  other arithmetic  20.2 us (13%)
  matrix products  12.7 us (8%)
    all_to_all x1, waiting for transfers between devices, on_device(): lax.all_to_all(spec_y, 'rows', split_axis=2, concat_axis=3, tiled=True)  14.8 us
    all_to_all x1, waiting for transfers between devices, on_device(): lax.all_to_all(sent, 'chan', split_axis=2, concat_axis=2, tiled=True)  14.2 us
    all_to_all x1, starting transfers between devices, on_device(): lax.all_to_all(spec_y, 'rows', split_axis=2, concat_axis=3, tiled=True)  12.9 us
    unnamed x47, local copies, waits for them, and re-layouts  11.7 us
    ppermute x1, starting transfers between devices, rows_halo_pair(): lax.ppermute(high, 'rows', backward)  8.74 us
    all_to_all x1, starting transfers between devices, on_device(): lax.all_to_all(inverted, 'rows', split_axis=3, concat_axis=2, tiled=True)  6.78 us
    all_to_all x1, waiting for transfers between devices, on_device(): lax.all_to_all(spectra, 'chan', split_axis=3, concat_axis=0, tiled=True)  5.04 us
    all_to_all x1, waiting for transfers between devices, on_device(): lax.all_to_all(inverted, 'rows', split_axis=3, concat_axis=2, tiled=True)  4.97 us
  transfers between devices with their start and end apart: 9, of which 6 were waited for; matrix products, arithmetic and copies ran while one was open for 22% of the time, Pallas kernels for 0%

profile of v1, /device:TPU:1, one launch (start us, length us, event | category | flops | bytes accessed | tf_op | source)
XLA Modules:
  0.0 158.4 jit_solution(13685357048287546316)
XLA Ops:
  4.0 8.7 %collective-permute-start.1 = (f32[35840]{0:T(1024)}, f32[35840]{0:T(1024)}, u32[]{:S(2)}, u32[]{:S(2)}) collective-permute-start(f32[35840]{0:T(1024)} %pad_maximum_fusion.10), channel_id=1, source_target_pairs={{8,0},{16,8},{24,16},{32,24},{40,32},{48,40},{56,48},{64,56},{72,6... | collective-permute-start | bytes 430088 | tf_op jit(solution)/shard_map/ppermute | solution.py:99
  12.8 4.1 %sine_negate_fusion = (f32[128,2048]{1,0:T(8,128)S(1)}, f32[128,2048]{1,0:T(8,128)S(1)}) fusion(), kind=kLoop, calls=%fused_computation.38 | loop fusion | flops 3932160 | bytes 2097152 | tf_op jit(solution)/shard_map/neg | solution.py:35
  16.9 2.2 %fusion.18 = f32[4,256,32]{1,2,0:T(8,128)S(1)} fusion(f32[4,32,2048]{2,1,0:T(8,128)S(1)} %copy-done.1, f32[128,2048]{1,0:T(8,128)S(1)} %get-tuple-element.42, f32[128,2048]{1,0:T(8,128)S(1)} %get-tuple-element.43), kind=kOutput, calls=%fused_computation.34 | convolution fusion | flops 805830656 | bytes 3276800 | tf_op jit(solution)/shard_map/cxy,ky->ckx/dot_general | solution.py:155
  20.2 2.2 %reshape.130 = f32[64,1,512]{2,1,0:T(1,128)} reshape(f32[128,4,2,32]{3,2,1,0:T(2,128)} %bitcast.198) | data formatting | bytes 262144
  22.4 12.9 %all-to-all-start = ((f32[64,1,512]{2,1,0:T(1,128)}), f32[64,1,512]{2,1,0:T(1,128)S(1)}, u32[]{:S(2)}, u32[]{:S(2)}) async-start(f32[64,1,512]{2,1,0:T(1,128)} %reshape.130), calls=%async_computation | async-start | bytes 262144 | tf_op jit(solution)/shard_map/all_to_all | solution.py:157
  36.0 3.5 %collective-permute-start = (f32[35840]{0:T(1024)}, f32[35840]{0:T(1024)}, u32[]{:S(2)}, u32[]{:S(2)}) collective-permute-start(f32[35840]{0:T(1024)} %pad_maximum_fusion.9), channel_id=1, source_target_pairs={{0,8},{8,16},{16,24},{24,32},{32,40},{40,48},{48,56},{56,64},{64,7... | collective-permute-start | bytes 430088 | tf_op jit(solution)/shard_map/ppermute | solution.py:98
  39.5 14.8 %all-to-all-done = f32[64,1,512]{2,1,0:T(1,128)S(1)} async-done(((f32[64,1,512]{2,1,0:T(1,128)}), f32[64,1,512]{2,1,0:T(1,128)S(1)}, u32[]{:S(2)}, u32[]{:S(2)}) %all-to-all-start) | async-done | bytes 131104 | tf_op jit(solution)/shard_map/all_to_all | solution.py:157
  55.9 1.2 reshape.131
  59.1 1.3 all_to_all.56
  60.4 1.9 %fusion.3 = f32[4,2,2,256]{3,2,1,0:T(2,128)S(1)} fusion(f32[4,2,2,2048]{3,2,1,0:T(2,128)S(1)} %all_to_all.56, f32[128,2048]{1,0:T(8,128)S(1)} %get-tuple-element.42, f32[128,2048]{1,0:T(8,128)S(1)} %get-tuple-element.43), kind=kOutput, calls=%fused_computation.6 | convolution fusion | flops 101187584 | bytes 2244608 | tf_op jit(solution)/shard_map/caqx,kx->caqk/dot_general | solution.py:158
  64.1 4.2 %all-to-all-start.1 = ((f32[8,1,256]{2,1,0:T(1,128)}), f32[8,1,256]{2,1,0:T(1,128)S(1)}, u32[]{:S(2)}, u32[]{:S(2)}) async-start(f32[8,1,256]{2,1,0:T(1,128)} %reshape.132), calls=%async_computation.1 | async-start | bytes 16384 | tf_op jit(solution)/shard_map/all_to_all | solution.py:169
  68.3 5.0 %all-to-all-done.1 = f32[8,1,256]{2,1,0:T(1,128)S(1)} async-done(((f32[8,1,256]{2,1,0:T(1,128)}), f32[8,1,256]{2,1,0:T(1,128)S(1)}, u32[]{:S(2)}, u32[]{:S(2)}) %all-to-all-start.1) | async-done | bytes 8224 | tf_op jit(solution)/shard_map/all_to_all | solution.py:169
  74.9 1.7 %fusion.29 = (f32[2,16,32]{2,1,0:T(8,128)S(1)}, f32[2,16,32]{2,1,0:T(8,128)S(1)}, f32[2,16,32]{2,1,0:T(8,128)S(1)}, f32[2,16,32]{2,1,0:T(8,128)S(1)}) fusion(f32[2,2,16,32,32]{4,3,2,1,0:T(8,128)} %param.11, f32[2,16,32]{2,1,0:T(8,128)S(1)} %copy.109, f32[2,16,32]{2,1,0:T(8,128)S(1)} %copy.108), kind=kLoop, calls=%fused_computation.49 | loop fusion | flops 258048 | bytes 286720
  77.9 3.3 %all-to-all-start.2 = ((f32[8,1,256]{2,1,0:T(1,128)}), f32[8,1,256]{2,1,0:T(1,128)S(1)}, u32[]{:S(2)}, u32[]{:S(2)}) async-start(f32[8,1,256]{2,1,0:T(1,128)} %reshape.134), calls=%async_computation.2 | async-start | bytes 16384 | tf_op jit(solution)/shard_map/all_to_all | solution.py:178
  83.2 3.0 %all-to-all-done.2 = f32[8,1,256]{2,1,0:T(1,128)S(1)} async-done(((f32[8,1,256]{2,1,0:T(1,128)}), f32[8,1,256]{2,1,0:T(1,128)S(1)}, u32[]{:S(2)}, u32[]{:S(2)}) %all-to-all-start.2) | async-done | bytes 8224 | tf_op jit(solution)/shard_map/all_to_all | solution.py:178
  91.2 1.4 pad_maximum_fusion.7
  93.9 2.7 %reshape.136 = f32[64,1,640]{2,1,0:T(1,128)} reshape(f32[64,4,2,2,40]{4,3,2,1,0:T(2,128)} %bitcast.201) | data formatting | bytes 327680
  96.5 6.8 %all-to-all-start.3 = ((f32[64,1,640]{2,1,0:T(1,128)}), f32[64,1,640]{2,1,0:T(1,128)S(1)}, u32[]{:S(2)}, u32[]{:S(2)}) async-start(f32[64,1,640]{2,1,0:T(1,128)} %reshape.136), calls=%async_computation.3 | async-start | bytes 327680 | tf_op jit(solution)/shard_map/all_to_all | solution.py:194
  104.0 1.6 slice.338
  106.5 1.6 slice.337
  108.1 1.6 %reshape.115 = f32[4,4,2048]{2,1,0:T(4,128)} reshape(f32[32768]{0:T(1024)} %slice.337) | data formatting | bytes 262144 | tf_op jit(solution)/shard_map/reshape | solution.py:94
  110.7 2.2 %collective-permute-start.2 = (f32[3,40,4]{2,1,0:T(8,128)S(1)}, f32[3,40,4]{2,1,0:T(8,128)S(1)}, u32[]{:S(2)}, u32[]{:S(2)}) collective-permute-start(f32[3,40,4]{2,1,0:T(8,128)S(1)} %get-tuple-element.23), channel_id=1, source_target_pairs={{0,1},{1,2},{2,3},{3,4},{4,5},{5,6},{6,7},{8,9},{9,10},{10,11},{11... | collective-permute-start | bytes 5768 | tf_op jit(solution)/shard_map/ppermute | solution.py:20
  112.9 1.3 collective-permute-start.3
  114.2 2.2 %pad_maximum_fusion.1 = f32[4,40,2048]{2,1,0:T(8,128)} fusion(f32[4,4,2048]{2,1,0:T(4,128)S(1)} %reshape.116, f32[4,32,2048]{2,1,0:T(8,128)S(1)} %copy-done.1, f32[4,4,2048]{2,1,0:T(4,128)} %reshape.115), kind=kLoop, calls=%fused_computation.17 | loop fusion | flops 655360 | bytes 2621440 | tf_op jit(solution)/shard_map/concatenate | solution.py:101
  116.3 1.8 %collective-permute-done.3 = f32[3,40,4]{2,1,0:T(8,128)S(1)} collective-permute-done((f32[3,40,4]{2,1,0:T(8,128)S(1)}, f32[3,40,4]{2,1,0:T(8,128)S(1)}, u32[]{:S(2)}, u32[]{:S(2)}) %collective-permute-start.3) | collective-permute-done | bytes 1952 | tf_op jit(solution)/shard_map/ppermute | solution.py:23
  118.3 5.0 %all-to-all-done.3 = f32[64,1,640]{2,1,0:T(1,128)S(1)} async-done(((f32[64,1,640]{2,1,0:T(1,128)}), f32[64,1,640]{2,1,0:T(1,128)S(1)}, u32[]{:S(2)}, u32[]{:S(2)}) %all-to-all-start.3) | async-done | bytes 163872 | tf_op jit(solution)/shard_map/all_to_all | solution.py:194
  126.6 4.4 %fusion.9 = f32[4,40,2048]{2,1,0:T(8,128)S(1)} fusion(f32[4]{0:T(128)S(1)} %copy-done.12, f32[4,40,2048]{2,1,0:T(8,128)S(1)} %copy-done.2, f32[128,2048]{1,0:T(8,128)S(1)} %get-tuple-element.42, f32[128,2048]{1,0:T(8,128)S(1)} %get-tuple-element.43, f32[4]{0:T(128)S(1)} %copy-done.13, f32[4,256,40]{2,1,0:T(8,128)S(1)} %bitcast.204, f32[256]{0:T(256)S(1)} %copy-done.14), kind=kOutput, calls=%fused_computation.16 | convolution fusion | flops 1029152768 | bytes 4883488 | tf_op jit(solution)/shard_map/ckx,ky->cxy/dot_general | solution.py:199
  131.0 3.1 %convolution_bitcast_fusion = f32[2,40,2048]{2,0,1:T(2,128)S(1)} fusion(f32[4,40,2048]{2,1,0:T(8,128)S(1)} %fusion.9, f32[2,4]{1,0:T(2,128)S(1)} %copy-done), kind=kOutput, calls=%fused_computation.2 | convolution fusion | flops 7864320 | bytes 1966112 | tf_op jit(solution)/shard_map/jc,cxy->jxy/dot_general | solution.py:204
  134.1 1.4 pad_slice_fusion.1
  136.5 1.4 pad_maximum_fusion.2
  137.9 3.7 %all-to-all-start.4 = ((f32[2,40,8,264]{3,0,1,2:T(2,128)}), f32[2,40,8,264]{3,0,1,2:T(2,128)S(1)}, u32[]{:S(2)}, u32[]{:S(2)}) async-start(f32[2,40,8,264]{3,0,1,2:T(2,128)} %pad_maximum_fusion.2), calls=%async_computation.4 | async-start | bytes 1966080 | tf_op jit(solution)/shard_map/all_to_all | solution.py:206
  141.6 14.2 %all-to-all-done.4 = f32[2,40,8,264]{3,0,1,2:T(2,128)S(1)} async-done(((f32[2,40,8,264]{3,0,1,2:T(2,128)}), f32[2,40,8,264]{3,0,1,2:T(2,128)S(1)}, u32[]{:S(2)}, u32[]{:S(2)}) %all-to-all-start.4) | async-done | bytes 675872 | tf_op jit(solution)/shard_map/all_to_all | solution.py:206
  (119 shorter events, 30.8 us)
Async XLA Ops:
  0.6 130.4 %copy-start = (f32[2,4]{1,0:T(2,128)S(1)}, f32[2,4]{1,0:T(2,128)}, u32[]{:S(2)}) copy-start(f32[2,4]{1,0:T(2,128)} %param.14) | copy-start | bytes 100
  1.4 1.9 %copy-start.3 = (f32[1,32,256]{2,1,0:T(8,128)}, f32[1,32,256]{2,1,0:T(8,128)S(1)}, u32[]{:S(2)}) copy-start(f32[1,32,256]{2,1,0:T(8,128)S(1)} %get-tuple-element.40) | copy-start | bytes 98308
  1.4 1.9 %copy-start.5 = (f32[1,32,256]{2,1,0:T(8,128)}, f32[1,32,256]{2,1,0:T(8,128)S(1)}, u32[]{:S(2)}) copy-start(f32[1,32,256]{2,1,0:T(8,128)S(1)} %get-tuple-element.41) | copy-start | bytes 98308
  3.3 13.6 %copy-start.1 = (f32[4,32,2048]{2,1,0:T(8,128)S(1)}, f32[4,32,2048]{2,1,0:T(8,128)}, u32[]{:S(2)}) copy-start(f32[4,32,2048]{2,1,0:T(8,128)} %param.9) | copy-start | bytes 3145732
  4.0 77.8 %collective-permute-start.1 = (f32[35840]{0:T(1024)}, f32[35840]{0:T(1024)}, u32[]{:S(2)}, u32[]{:S(2)}) collective-permute-start(f32[35840]{0:T(1024)} %pad_maximum_fusion.10), channel_id=1, source_target_pairs={{8,0},{16,8},{24,16},{32,24},{40,32},{48,40},{56,48},{64,56},{72,6... | collective-permute-start | bytes 430088 | tf_op jit(solution)/shard_map/ppermute | solution.py:99
  22.4 31.9 %all-to-all-start = ((f32[64,1,512]{2,1,0:T(1,128)}), f32[64,1,512]{2,1,0:T(1,128)S(1)}, u32[]{:S(2)}, u32[]{:S(2)}) async-start(f32[64,1,512]{2,1,0:T(1,128)} %reshape.130), calls=%async_computation | async-start | bytes 262144 | tf_op jit(solution)/shard_map/all_to_all | solution.py:157
  36.0 46.5 %collective-permute-start = (f32[35840]{0:T(1024)}, f32[35840]{0:T(1024)}, u32[]{:S(2)}, u32[]{:S(2)}) collective-permute-start(f32[35840]{0:T(1024)} %pad_maximum_fusion.9), channel_id=1, source_target_pairs={{0,8},{8,16},{16,24},{24,32},{32,40},{40,48},{48,56},{56,64},{64,7... | collective-permute-start | bytes 430088 | tf_op jit(solution)/shard_map/ppermute | solution.py:98
  64.1 9.3 %all-to-all-start.1 = ((f32[8,1,256]{2,1,0:T(1,128)}), f32[8,1,256]{2,1,0:T(1,128)S(1)}, u32[]{:S(2)}, u32[]{:S(2)}) async-start(f32[8,1,256]{2,1,0:T(1,128)} %reshape.132), calls=%async_computation.1 | async-start | bytes 16384 | tf_op jit(solution)/shard_map/all_to_all | solution.py:169
  74.8 12.7 %copy-start.11 = (pred[65]{0:T(512)(128)(4,1)S(1)}, pred[65]{0:T(512)(128)(4,1)}, u32[]{:S(2)}) copy-start(pred[65]{0:T(512)(128)(4,1)} %constant.37.clone.1) | copy-start | bytes 199
  77.9 8.3 %all-to-all-start.2 = ((f32[8,1,256]{2,1,0:T(1,128)}), f32[8,1,256]{2,1,0:T(1,128)S(1)}, u32[]{:S(2)}, u32[]{:S(2)}) async-start(f32[8,1,256]{2,1,0:T(1,128)} %reshape.134), calls=%async_computation.2 | async-start | bytes 16384 | tf_op jit(solution)/shard_map/all_to_all | solution.py:178
  92.6 10.7 %copy-start.4 = (f32[1,32,256]{2,1,0:T(8,128)S(1)}, f32[1,32,256]{2,1,0:T(8,128)}, u32[]{:S(2)}) copy-start(f32[1,32,256]{2,1,0:T(8,128)} %copy-done.3) | copy-start | bytes 98308
  92.6 10.7 %copy-start.6 = (f32[1,32,256]{2,1,0:T(8,128)S(1)}, f32[1,32,256]{2,1,0:T(8,128)}, u32[]{:S(2)}) copy-start(f32[1,32,256]{2,1,0:T(8,128)} %copy-done.5) | copy-start | bytes 98308
  92.7 10.7 %copy-start.8 = (f32[32,256]{1,0:T(8,128)S(1)}, f32[32,256]{1,0:T(8,128)}, u32[]{:S(2)}) copy-start(f32[32,256]{1,0:T(8,128)} %param.10) | copy-start | bytes 98308
  96.5 26.7 %all-to-all-start.3 = ((f32[64,1,640]{2,1,0:T(1,128)}), f32[64,1,640]{2,1,0:T(1,128)S(1)}, u32[]{:S(2)}, u32[]{:S(2)}) async-start(f32[64,1,640]{2,1,0:T(1,128)} %reshape.136), calls=%async_computation.3 | async-start | bytes 327680 | tf_op jit(solution)/shard_map/all_to_all | solution.py:194
  110.7 5.7 %collective-permute-start.2 = (f32[3,40,4]{2,1,0:T(8,128)S(1)}, f32[3,40,4]{2,1,0:T(8,128)S(1)}, u32[]{:S(2)}, u32[]{:S(2)}) collective-permute-start(f32[3,40,4]{2,1,0:T(8,128)S(1)} %get-tuple-element.23), channel_id=1, source_target_pairs={{0,1},{1,2},{2,3},{3,4},{4,5},{5,6},{6,7},{8,9},{9,10},{10,11},{11... | collective-permute-start | bytes 5768 | tf_op jit(solution)/shard_map/ppermute | solution.py:20
  112.9 5.3 %copy-start.7 = (f32[1,32,256]{2,1,0:T(8,128)S(1)}, f32[1,32,256]{2,1,0:T(8,128)}, u32[]{:S(2)}) copy-start(f32[1,32,256]{2,1,0:T(8,128)} %copy-done.5) | copy-start | bytes 98308
  112.9 5.3 %copy-start.9 = (f32[32,256]{1,0:T(8,128)S(1)}, f32[32,256]{1,0:T(8,128)}, u32[]{:S(2)}) copy-start(f32[32,256]{1,0:T(8,128)} %param.10) | copy-start | bytes 98308
  112.9 5.3 %collective-permute-start.3 = (f32[3,40,4]{2,1,0:T(8,128)S(1)}, f32[3,40,4]{2,1,0:T(8,128)S(1)}, u32[]{:S(2)}, u32[]{:S(2)}) collective-permute-start(f32[3,40,4]{2,1,0:T(8,128)S(1)} %get-tuple-element.24), channel_id=1, source_target_pairs={{1,0},{2,1},{3,2},{4,3},{5,4},{6,5},{7,6},{9,8},{10,9},{11,10},{12... | collective-permute-start | bytes 5768 | tf_op jit(solution)/shard_map/ppermute | solution.py:23
  124.3 1.4 copy-start.12
  124.4 1.4 copy-start.13
  124.4 1.4 copy-start.14
  125.3 1.3 copy-start.2
  137.9 18.3 %copy-start.10 = (f32[2]{0:T(128)S(1)}, f32[2]{0:T(128)}, u32[]{:S(2)}) copy-start(f32[2]{0:T(128)} %param.15) | copy-start | bytes 28
  137.9 17.9 %all-to-all-start.4 = ((f32[2,40,8,264]{3,0,1,2:T(2,128)}), f32[2,40,8,264]{3,0,1,2:T(2,128)S(1)}, u32[]{:S(2)}, u32[]{:S(2)}) async-start(f32[2,40,8,264]{3,0,1,2:T(2,128)} %pad_maximum_fusion.2), calls=%async_computation.4 | async-start | bytes 1966080 | tf_op jit(solution)/shard_map/all_to_all | solution.py:206

commit v2 on v1

--- a/solution.py
+++ b/solution.py
@@ -154,6 +154,8 @@
 
     spec_y = jnp.einsum("cxy,ky->ckx", hidden, table, precision=highest)
     spec_y = spec_y.reshape(local_chan, 2, all_ymodes, row_count)
+    weights = lax.all_to_all(spectral_weight, "chan", split_axis=3, concat_axis=2, tiled=True)
+    weights, spec_y = lax.optimization_barrier((weights, spec_y))
     by_freq = lax.all_to_all(spec_y, "rows", split_axis=2, concat_axis=3, tiled=True)
     parts = jnp.einsum("caqx,kx->caqk", by_freq, x_table, precision=highest)
     cos_part = parts[..., :x_modes]
@@ -166,17 +168,19 @@
     )
     spectra = jnp.stack([real_in, imag_in], axis=2)
 
-    gathered = lax.all_to_all(spectra, "chan", split_axis=3, concat_axis=0, tiled=True)
-    real_in = gathered[:, :, 0]
-    imag_in = gathered[:, :, 1]
+    real_in = spectra[:, :, 0]
+    imag_in = spectra[:, :, 1]
     real_out = jnp.einsum(
-        "qpio,iqp->oqp", spectral_weight[0], real_in, precision=highest
-    ) - jnp.einsum("qpio,iqp->oqp", spectral_weight[1], imag_in, precision=highest)
+        "qpio,iqp->oqp", weights[0], real_in, precision=highest
+    ) - jnp.einsum("qpio,iqp->oqp", weights[1], imag_in, precision=highest)
     imag_out = jnp.einsum(
-        "qpio,iqp->oqp", spectral_weight[0], imag_in, precision=highest
-    ) + jnp.einsum("qpio,iqp->oqp", spectral_weight[1], real_in, precision=highest)
-    mixed = lax.all_to_all(
-        jnp.stack([real_out, imag_out], axis=2), "chan", split_axis=0, concat_axis=3, tiled=True
+        "qpio,iqp->oqp", weights[0], imag_in, precision=highest
+    ) + jnp.einsum("qpio,iqp->oqp", weights[1], real_in, precision=highest)
+    partial_mixed = jnp.stack([real_out, imag_out], axis=2).reshape(
+        (chan_devices, local_chan) + real_out.shape[1:2] + (2,) + real_out.shape[2:]
+    )
+    mixed = jnp.sum(
+        lax.all_to_all(partial_mixed, "chan", split_axis=0, concat_axis=0, tiled=True), axis=0
     )
 
     real_pos, real_neg = fold_modes(mixed[:, :, 0], half)

time: 160 us -> 169 us (1.056)
  local copies, waits for them, and re-layouts: 33.9 us -> 43.6 us
  waiting for transfers between devices: 43.7 us -> 37.9 us
  other arithmetic: 20.2 us -> 22.7 us
  starting transfers between devices: 46.6 us -> 48.5 us
    ppermute x1, starting transfers between devices: 8.74 us -> 2.53 us  [rows_halo_pair(): lax.ppermute(high, 'rows', backward)]
    all_to_all x2, waiting for transfers between devices: 7.99 us -> 3.18 us  [the longest x1 3.18 us: on_device(): lax.all_to_all(partial_mixed, 'chan', split_axis=0, concat_axis=0, tiled=...]
    unnamed x47 -> x51, local copies, waits for them, and re-layouts: 11.7 us -> 16.3 us
    all_to_all x1, starting transfers between devices: 12.9 us -> 17 us  [on_device(): lax.all_to_all(spec_y, 'rows', split_axis=2, concat_axis=3, tiled=True)]
    all_to_all x2, starting transfers between devices: 7.52 us -> 10.7 us  [the longest x1 5.94 us: on_device(): lax.all_to_all(spectral_weight, 'chan', split_axis=3, concat_axis=2, tile...]
    all_to_all x4 -> x2, local copies, waits for them, and re-layouts: 0.41 us -> 2.82 us  [on_device(): lax.all_to_all(spectral_weight, 'chan', split_axis=3, concat_axis=2, tile...]
    dot_general x4, local copies, waits for them, and re-layouts: 0.33 us -> 2.42 us  [the longest x1 1.59 us: on_device(): jnp.einsum('qpio,iqp->oqp', weights[0], real_in, precision=highest)]
    ppermute x1, waiting for transfers between devices: 1.79 us -> 0.01 us  [with_halo(): lax.ppermute(lax.slice_in_dim(block, 0, width, axis=dim), axis, backward)]
  transfers between devices with their start and end apart: 9 -> 9, of which waited for: 6 -> 4; matrix products, arithmetic and copies ran while one was open for 22% -> 28% of each run, Pallas kernels for 0% -> 0%
where the time goes in v2:
time: 169 us; the launch traced here: 167 us
  starting transfers between devices  48.5 us (29%)
  local copies, waits for them, and re-layouts  43.6 us (26%)
  waiting for transfers between devices  37.9 us (22%)
  other arithmetic  22.7 us (13%)
  matrix products  13.4 us (8%)
    all_to_all x1, starting transfers between devices, on_device(): lax.all_to_all(spec_y, 'rows', split_axis=2, concat_axis=3, tiled=True)  17 us
    unnamed x51, local copies, waits for them, and re-layouts  16.3 us
    all_to_all x1, waiting for transfers between devices, on_device(): lax.all_to_all(spec_y, 'rows', split_axis=2, concat_axis=3, tiled=True)  15.4 us
    all_to_all x1, waiting for transfers between devices, on_device(): lax.all_to_all(sent, 'chan', split_axis=2, concat_axis=2, tiled=True)  14.2 us
    all_to_all x1, starting transfers between devices, on_device(): lax.all_to_all(spectral_weight, 'chan', split_axis=3, concat_axis=2, tile...  5.94 us
    all_to_all x1, starting transfers between devices, on_device(): lax.all_to_all(inverted, 'rows', split_axis=3, concat_axis=2, tiled=True)  5.86 us
    all_to_all x1, waiting for transfers between devices, on_device(): lax.all_to_all(inverted, 'rows', split_axis=3, concat_axis=2, tiled=True)  5.21 us
    all_to_all x1, starting transfers between devices, on_device(): lax.all_to_all(partial_mixed, 'chan', split_axis=0, concat_axis=0, tiled=...  4.81 us
  transfers between devices with their start and end apart: 9, of which 4 were waited for; matrix products, arithmetic and copies ran while one was open for 28% of the time, Pallas kernels for 0%

profile of v2, /device:TPU:1, one launch (start us, length us, event | category | flops | bytes accessed | tf_op | source)
XLA Modules:
  0.0 167.3 jit_solution(5456913930387555221)
XLA Ops:
  0.6 1.8 %copy.128 = f32[2,2,16,32,32]{4,2,1,0,3:T(8,128)S(1)} copy(f32[2,2,16,32,32]{4,3,2,1,0:T(8,128)} %param.11) | data formatting | bytes 524288 | tf_op args[2]
  3.7 5.9 %all-to-all-start = ((f32[8,1,8192]{2,1,0:T(1,128)}), f32[8,1,8192]{2,1,0:T(1,128)S(1)}, u32[]{:S(2)}, u32[]{:S(2)}) async-start(f32[8,1,8192]{2,1,0:T(1,128)} %reshape.135), calls=%async_computation | async-start | bytes 524288 | tf_op jit(solution)/shard_map/all_to_all | solution.py:157
  11.7 4.4 %collective-permute-start = (f32[35840]{0:T(1024)}, f32[35840]{0:T(1024)}, u32[]{:S(2)}, u32[]{:S(2)}) collective-permute-start(f32[35840]{0:T(1024)} %pad_maximum_fusion.9), channel_id=1, source_target_pairs={{0,8},{8,16},{16,24},{24,32},{32,40},{40,48},{48,56},{56,64},{64,7... | collective-permute-start | bytes 430088 | tf_op jit(solution)/shard_map/ppermute | solution.py:98
  16.1 4.1 %sine_negate_fusion = (f32[128,2048]{1,0:T(8,128)S(1)}, f32[128,2048]{1,0:T(8,128)S(1)}) fusion(), kind=kLoop, calls=%fused_computation.38 | loop fusion | flops 3932160 | bytes 2097152 | tf_op jit(solution)/shard_map/neg | solution.py:35
  20.2 2.9 %fusion.18 = f32[4,256,32]{1,2,0:T(8,128)} fusion(f32[4,32,2048]{2,1,0:T(8,128)S(1)} %copy-done.1, f32[128,2048]{1,0:T(8,128)S(1)} %get-tuple-element.45, f32[128,2048]{1,0:T(8,128)S(1)} %get-tuple-element.46), kind=kOutput, calls=%fused_computation.34 | convolution fusion | flops 805830656 | bytes 3276800 | tf_op jit(solution)/shard_map/cxy,ky->ckx/dot_general | solution.py:155
  24.7 1.6 copy.117
  27.5 2.1 %reduce.8 = f32[8,8192]{1,0:T(8,128)S(1)} reduce(f32[8,1,8192]{2,1,0:T(1,128)} %copy-done.3, f32[]{:T(128)} %broadcast.130), dimensions={1}, to_apply=%all_to_all.43.reduce_sub_computation | reduce | bytes 524292 | tf_op jit(solution)/shard_map/all_to_all | solution.py:157
  31.0 2.3 %copy.55 = f32[2,2,16,8,4,32]{5,2,3,4,1,0:T(8,128)} copy(f32[2,2,16,8,4,32]{5,2,1,0,4,3:T(8,128)} %bitcast.176) | data formatting | bytes 524288 | tf_op jit(solution)/shard_map/all_to_all | solution.py:157
  34.4 2.2 %reshape.137 = f32[64,1,512]{2,1,0:T(1,128)} reshape(f32[128,4,2,32]{3,2,1,0:T(2,128)} %bitcast.182) | data formatting | bytes 262144
  36.6 17.0 %all-to-all-start.1 = ((f32[64,1,512]{2,1,0:T(1,128)}), f32[64,1,512]{2,1,0:T(1,128)S(1)}, u32[]{:S(2)}, u32[]{:S(2)}) async-start(f32[64,1,512]{2,1,0:T(1,128)} %reshape.137), calls=%async_computation.1 | async-start | bytes 262144 | tf_op jit(solution)/shard_map/all_to_all | solution.py:159
  54.3 2.5 %collective-permute-start.1 = (f32[35840]{0:T(1024)}, f32[35840]{0:T(1024)}, u32[]{:S(2)}, u32[]{:S(2)}) collective-permute-start(f32[35840]{0:T(1024)} %pad_maximum_fusion.10), channel_id=1, source_target_pairs={{8,0},{16,8},{24,16},{32,24},{40,32},{48,40},{56,48},{64,56},{72,6... | collective-permute-start | bytes 430088 | tf_op jit(solution)/shard_map/ppermute | solution.py:99
  56.9 15.4 %all-to-all-done.1 = f32[64,1,512]{2,1,0:T(1,128)S(1)} async-done(((f32[64,1,512]{2,1,0:T(1,128)}), f32[64,1,512]{2,1,0:T(1,128)S(1)}, u32[]{:S(2)}, u32[]{:S(2)}) %all-to-all-start.1) | async-done | bytes 131104 | tf_op jit(solution)/shard_map/all_to_all | solution.py:159
  77.7 1.9 %fusion.3 = f32[4,2,2,256]{3,2,1,0:T(2,128)S(1)} fusion(f32[4,2,2,2048]{3,2,1,0:T(2,128)S(1)} %all_to_all.50, f32[128,2048]{1,0:T(8,128)S(1)} %get-tuple-element.45, f32[128,2048]{1,0:T(8,128)S(1)} %get-tuple-element.46), kind=kOutput, calls=%fused_computation.6 | convolution fusion | flops 101187584 | bytes 2244608 | tf_op jit(solution)/shard_map/caqx,kx->caqk/dot_general | solution.py:160
  80.2 2.3 %fusion.29 = (f32[2,128,32]{2,1,0:T(8,128)S(1)}, f32[2,128,32]{2,1,0:T(8,128)S(1)}, f32[2,128,32]{2,1,0:T(8,128)S(1)}, f32[2,128,32]{2,1,0:T(8,128)}) fusion(f32[2,2,128,4,32]{4,2,3,1,0:T(8,128)} %bitcast.178, f32[2,128,4]{1,2,0:T(4,128)S(1)} %copy.111, f32[2,128,4]{1,2,0:T(4,128)S(1)} %copy.110), kind=kLoop, calls=%fused_computation.49 | loop fusion | flops 229376 | bytes 401408
  82.5 1.6 copy.83
  86.4 4.8 %all-to-all-start.2 = ((f32[8,4,2,2,128]{4,1,2,3,0:T(4,128)}), f32[8,4,2,2,128]{4,1,2,3,0:T(4,128)S(1)}, u32[]{:S(2)}, u32[]{:S(2)}) async-start(f32[8,4,2,2,128]{4,1,2,3,0:T(4,128)} %copy.65), calls=%async_computation.2 | async-start | bytes 131072 | tf_op jit(solution)/shard_map/all_to_all | solution.py:183
  93.2 3.2 %all-to-all-done.2 = f32[8,4,2,2,128]{4,1,2,3,0:T(4,128)S(1)} async-done(((f32[8,4,2,2,128]{4,1,2,3,0:T(4,128)}), f32[8,4,2,2,128]{4,1,2,3,0:T(4,128)S(1)}, u32[]{:S(2)}, u32[]{:S(2)}) %all-to-all-start.2) | async-done | bytes 65568 | tf_op jit(solution)/shard_map/all_to_all | solution.py:183
  101.1 1.4 pad_maximum_fusion.7
  103.8 2.7 %reshape.139 = f32[64,1,640]{2,1,0:T(1,128)} reshape(f32[64,4,2,2,40]{4,3,2,1,0:T(2,128)} %bitcast.185) | data formatting | bytes 327680
  106.5 5.9 %all-to-all-start.3 = ((f32[64,1,640]{2,1,0:T(1,128)}), f32[64,1,640]{2,1,0:T(1,128)S(1)}, u32[]{:S(2)}, u32[]{:S(2)}) async-start(f32[64,1,640]{2,1,0:T(1,128)} %reshape.139), calls=%async_computation.3 | async-start | bytes 327680 | tf_op jit(solution)/shard_map/all_to_all | solution.py:198
  113.9 2.8 %collective-permute-start.2 = (f32[3,40,4]{2,1,0:T(8,128)}, f32[3,40,4]{2,1,0:T(8,128)}, u32[]{:S(2)}, u32[]{:S(2)}) collective-permute-start(f32[3,40,4]{2,1,0:T(8,128)} %get-tuple-element.27), channel_id=1, source_target_pairs={{0,1},{1,2},{2,3},{3,4},{4,5},{5,6},{6,7},{8,9},{9,10},{10,11},{11... | collective-permute-start | bytes 5768 | tf_op jit(solution)/shard_map/ppermute | solution.py:20
  116.7 1.5 collective-permute-start.3
  118.2 1.6 slice.327
  120.7 1.6 slice.328
  122.3 1.6 reshape.121
  123.9 2.2 %pad_maximum_fusion.1 = f32[4,40,2048]{2,1,0:T(8,128)} fusion(f32[4,4,2048]{2,1,0:T(4,128)} %reshape.121, f32[4,32,2048]{2,1,0:T(8,128)S(1)} %copy-done.1, f32[4,4,2048]{2,1,0:T(4,128)S(1)} %reshape.120), kind=kLoop, calls=%fused_computation.17 | loop fusion | flops 655360 | bytes 2621440 | tf_op jit(solution)/shard_map/concatenate | solution.py:101
  127.1 5.2 %all-to-all-done.3 = f32[64,1,640]{2,1,0:T(1,128)S(1)} async-done(((f32[64,1,640]{2,1,0:T(1,128)}), f32[64,1,640]{2,1,0:T(1,128)S(1)}, u32[]{:S(2)}, u32[]{:S(2)}) %all-to-all-start.3) | async-done | bytes 163872 | tf_op jit(solution)/shard_map/all_to_all | solution.py:198
  135.5 4.4 %fusion.9 = f32[4,40,2048]{2,1,0:T(8,128)S(1)} fusion(f32[4]{0:T(128)S(1)} %copy-done.15, f32[4,40,2048]{2,1,0:T(8,128)S(1)} %copy-done.2, f32[128,2048]{1,0:T(8,128)S(1)} %get-tuple-element.45, f32[128,2048]{1,0:T(8,128)S(1)} %get-tuple-element.46, f32[4]{0:T(128)S(1)} %copy-done.16, f32[4,256,40]{2,1,0:T(8,128)S(1)} %bitcast.186, f32[256]{0:T(256)S(1)} %copy-done.17), kind=kOutput, calls=%fused_computation.16 | convolution fusion | flops 1029152768 | bytes 4883488 | tf_op jit(solution)/shard_map/ckx,ky->cxy/dot_general | solution.py:203
  139.9 3.1 %convolution_bitcast_fusion = f32[2,40,2048]{2,0,1:T(2,128)S(1)} fusion(f32[4,40,2048]{2,1,0:T(8,128)S(1)} %fusion.9, f32[2,4]{1,0:T(2,128)S(1)} %copy-done), kind=kOutput, calls=%fused_computation.2 | convolution fusion | flops 7864320 | bytes 1966112 | tf_op jit(solution)/shard_map/jc,cxy->jxy/dot_general | solution.py:208
  145.4 1.4 pad_maximum_fusion.2
  146.8 3.7 %all-to-all-start.4 = ((f32[2,40,8,264]{3,0,1,2:T(2,128)}), f32[2,40,8,264]{3,0,1,2:T(2,128)S(1)}, u32[]{:S(2)}, u32[]{:S(2)}) async-start(f32[2,40,8,264]{3,0,1,2:T(2,128)} %pad_maximum_fusion.2), calls=%async_computation.4 | async-start | bytes 1966080 | tf_op jit(solution)/shard_map/all_to_all | solution.py:210
  150.5 14.2 %all-to-all-done.4 = f32[2,40,8,264]{3,0,1,2:T(2,128)S(1)} async-done(((f32[2,40,8,264]{3,0,1,2:T(2,128)}), f32[2,40,8,264]{3,0,1,2:T(2,128)S(1)}, u32[]{:S(2)}, u32[]{:S(2)}) %all-to-all-start.4) | async-done | bytes 675872 | tf_op jit(solution)/shard_map/all_to_all | solution.py:210
  (119 shorter events, 36.9 us)
Async XLA Ops:
  0.6 139.3 %copy-start = (f32[2,4]{1,0:T(2,128)S(1)}, f32[2,4]{1,0:T(2,128)}, u32[]{:S(2)}) copy-start(f32[2,4]{1,0:T(2,128)} %param.14) | copy-start | bytes 100
  2.5 7.1 %copy-start.12 = (s32[32,256]{1,0:T(8,128)S(1)}, s32[32,256]{1,0:T(8,128)}, u32[]{:S(2)}) copy-start(s32[32,256]{1,0:T(8,128)} %param.16) | copy-start | bytes 98308
  2.5 7.1 %copy-start.13 = (s32[32,256]{1,0:T(8,128)S(1)}, s32[32,256]{1,0:T(8,128)}, u32[]{:S(2)}) copy-start(s32[32,256]{1,0:T(8,128)} %param.17) | copy-start | bytes 98308
  2.5 7.2 %copy-start.10 = (f32[32,256]{1,0:T(8,128)S(1)}, f32[32,256]{1,0:T(8,128)}, u32[]{:S(2)}) copy-start(f32[32,256]{1,0:T(8,128)} %param.10) | copy-start | bytes 98308
  2.5 7.8 %copy-start.1 = (f32[4,32,2048]{2,1,0:T(8,128)S(1)}, f32[4,32,2048]{2,1,0:T(8,128)}, u32[]{:S(2)}) copy-start(f32[4,32,2048]{2,1,0:T(8,128)} %param.9) | copy-start | bytes 3145732
  3.7 22.6 %all-to-all-start = ((f32[8,1,8192]{2,1,0:T(1,128)}), f32[8,1,8192]{2,1,0:T(1,128)S(1)}, u32[]{:S(2)}, u32[]{:S(2)}) async-start(f32[8,1,8192]{2,1,0:T(1,128)} %reshape.135), calls=%async_computation | async-start | bytes 524288 | tf_op jit(solution)/shard_map/all_to_all | solution.py:157
  9.7 1.4 copy-start.5
  9.7 1.3 copy-start.7
  11.7 80.0 %collective-permute-start = (f32[35840]{0:T(1024)}, f32[35840]{0:T(1024)}, u32[]{:S(2)}, u32[]{:S(2)}) collective-permute-start(f32[35840]{0:T(1024)} %pad_maximum_fusion.9), channel_id=1, source_target_pairs={{0,8},{8,16},{16,24},{24,32},{32,40},{40,48},{48,56},{56,64},{64,7... | collective-permute-start | bytes 430088 | tf_op jit(solution)/shard_map/ppermute | solution.py:98
  26.3 0.7 copy-start.3
  33.3 20.3 %copy-start.4 = (f32[4,16,4,128]{3,1,2,0:T(8,128)S(1)}, f32[4,16,4,128]{3,1,2,0:T(8,128)}, u32[]{:S(2)}) copy-start(f32[4,16,4,128]{3,1,2,0:T(8,128)} %copy.117) | copy-start | bytes 393220
  36.6 35.6 %all-to-all-start.1 = ((f32[64,1,512]{2,1,0:T(1,128)}), f32[64,1,512]{2,1,0:T(1,128)S(1)}, u32[]{:S(2)}, u32[]{:S(2)}) async-start(f32[64,1,512]{2,1,0:T(1,128)} %reshape.137), calls=%async_computation.1 | async-start | bytes 262144 | tf_op jit(solution)/shard_map/all_to_all | solution.py:159
  54.3 38.1 %collective-permute-start.1 = (f32[35840]{0:T(1024)}, f32[35840]{0:T(1024)}, u32[]{:S(2)}, u32[]{:S(2)}) collective-permute-start(f32[35840]{0:T(1024)} %pad_maximum_fusion.10), channel_id=1, source_target_pairs={{8,0},{16,8},{24,16},{32,24},{40,32},{48,40},{56,48},{64,56},{72,6... | collective-permute-start | bytes 430088 | tf_op jit(solution)/shard_map/ppermute | solution.py:99
  86.4 10.0 %all-to-all-start.2 = ((f32[8,4,2,2,128]{4,1,2,3,0:T(4,128)}), f32[8,4,2,2,128]{4,1,2,3,0:T(4,128)S(1)}, u32[]{:S(2)}, u32[]{:S(2)}) async-start(f32[8,4,2,2,128]{4,1,2,3,0:T(4,128)} %copy.65), calls=%async_computation.2 | async-start | bytes 131072 | tf_op jit(solution)/shard_map/all_to_all | solution.py:183
  102.6 9.8 %copy-start.6 = (f32[1,32,256]{2,1,0:T(8,128)S(1)}, f32[1,32,256]{2,1,0:T(8,128)}, u32[]{:S(2)}) copy-start(f32[1,32,256]{2,1,0:T(8,128)} %copy-done.5) | copy-start | bytes 98308
  102.6 9.8 %copy-start.8 = (f32[1,32,256]{2,1,0:T(8,128)S(1)}, f32[1,32,256]{2,1,0:T(8,128)}, u32[]{:S(2)}) copy-start(f32[1,32,256]{2,1,0:T(8,128)} %copy-done.7) | copy-start | bytes 98308
  106.5 25.8 %all-to-all-start.3 = ((f32[64,1,640]{2,1,0:T(1,128)}), f32[64,1,640]{2,1,0:T(1,128)S(1)}, u32[]{:S(2)}, u32[]{:S(2)}) async-start(f32[64,1,640]{2,1,0:T(1,128)} %reshape.139), calls=%async_computation.3 | async-start | bytes 327680 | tf_op jit(solution)/shard_map/all_to_all | solution.py:198
  113.9 12.2 %collective-permute-start.2 = (f32[3,40,4]{2,1,0:T(8,128)}, f32[3,40,4]{2,1,0:T(8,128)}, u32[]{:S(2)}, u32[]{:S(2)}) collective-permute-start(f32[3,40,4]{2,1,0:T(8,128)} %get-tuple-element.27), channel_id=1, source_target_pairs={{0,1},{1,2},{2,3},{3,4},{4,5},{5,6},{6,7},{8,9},{9,10},{10,11},{11... | collective-permute-start | bytes 5768 | tf_op jit(solution)/shard_map/ppermute | solution.py:20
  116.7 9.4 %collective-permute-start.3 = (f32[3,40,4]{2,1,0:T(8,128)}, f32[3,40,4]{2,1,0:T(8,128)}, u32[]{:S(2)}, u32[]{:S(2)}) collective-permute-start(f32[3,40,4]{2,1,0:T(8,128)} %get-tuple-element.28), channel_id=1, source_target_pairs={{1,0},{2,1},{3,2},{4,3},{5,4},{6,5},{7,6},{9,8},{10,9},{11,10},{12... | collective-permute-start | bytes 5768 | tf_op jit(solution)/shard_map/ppermute | solution.py:23
  123.9 2.2 %copy-start.9 = (f32[1,32,256]{2,1,0:T(8,128)S(1)}, f32[1,32,256]{2,1,0:T(8,128)}, u32[]{:S(2)}) copy-start(f32[1,32,256]{2,1,0:T(8,128)} %copy-done.7) | copy-start | bytes 98308
  123.9 2.2 %copy-start.11 = (f32[32,256]{1,0:T(8,128)S(1)}, f32[32,256]{1,0:T(8,128)}, u32[]{:S(2)}) copy-start(f32[32,256]{1,0:T(8,128)} %param.10) | copy-start | bytes 98308
  133.2 1.4 copy-start.15
  133.2 1.4 copy-start.16
  133.3 1.4 copy-start.17
  134.2 1.3 copy-start.2
  146.8 18.3 %copy-start.14 = (f32[2]{0:T(128)S(1)}, f32[2]{0:T(128)}, u32[]{:S(2)}) copy-start(f32[2]{0:T(128)} %param.15) | copy-start | bytes 28
  146.8 17.9 %all-to-all-start.4 = ((f32[2,40,8,264]{3,0,1,2:T(2,128)}), f32[2,40,8,264]{3,0,1,2:T(2,128)S(1)}, u32[]{:S(2)}, u32[]{:S(2)}) async-start(f32[2,40,8,264]{3,0,1,2:T(2,128)} %pad_maximum_fusion.2), calls=%async_computation.4 | async-start | bytes 1966080 | tf_op jit(solution)/shard_map/all_to_all | solution.py:210

commit v3 on v1

--- a/solution.py
+++ b/solution.py
@@ -10,6 +10,7 @@
 
 time_step = 0.25
 highest = lax.Precision.HIGHEST
+high = lax.Precision.HIGH
 
 
 def with_halo(block, sides, width):
@@ -152,10 +153,10 @@
         x_table = base_table(half + 1, all_rows)
     x_modes = x_table.shape[0] // 2
 
-    spec_y = jnp.einsum("cxy,ky->ckx", hidden, table, precision=highest)
+    spec_y = jnp.einsum("cxy,ky->ckx", hidden, table, precision=high)
     spec_y = spec_y.reshape(local_chan, 2, all_ymodes, row_count)
     by_freq = lax.all_to_all(spec_y, "rows", split_axis=2, concat_axis=3, tiled=True)
-    parts = jnp.einsum("caqx,kx->caqk", by_freq, x_table, precision=highest)
+    parts = jnp.einsum("caqx,kx->caqk", by_freq, x_table, precision=high)
     cos_part = parts[..., :x_modes]
     sin_part = parts[..., x_modes:]
     real_in = unfold_modes(
@@ -189,19 +190,19 @@
         [jnp.pad(imag_pos + imag_neg, pad), jnp.pad(real_neg - real_pos, pad)], axis=-1
     )
     coef = jnp.stack([coef_real, coef_imag], axis=1)
-    inverted = jnp.einsum("otqk,kx->otqx", coef, x_table, precision=highest)
+    inverted = jnp.einsum("otqk,kx->otqx", coef, x_table, precision=high)
     inverted = windows(inverted, row_devices, row_count, halo)
     inverted = lax.all_to_all(inverted, "rows", split_axis=3, concat_axis=2, tiled=True)
     y_weights = jnp.where(jnp.arange(all_ymodes) == 0, 1.0, 2.0).astype(jnp.float32) * norm_scale
     inverted = inverted.reshape(local_chan, 2, all_ymodes, win_rows) * y_weights[:, None]
     inverted = inverted.reshape(local_chan, 2 * all_ymodes, win_rows)
 
-    spectral = jnp.einsum("ckx,ky->cxy", inverted, table, precision=highest)
+    spectral = jnp.einsum("ckx,ky->cxy", inverted, table, precision=high)
     activated = jax.nn.gelu(
         spectral + skip_gain[:, None, None] * hidden_win + skip_bias[:, None, None],
         approximate=False,
     )
-    partial_speed = jnp.einsum("jc,cxy->jxy", project_weight, activated, precision=highest)
+    partial_speed = jnp.sum(project_weight[:, :, None, None] * activated[None], axis=1)
     sent = windows(partial_speed, chan_devices, tile_cols, halo)
     received = lax.all_to_all(sent, "chan", split_axis=2, concat_axis=2, tiled=True)
     speed = jnp.sum(received, axis=2) + project_bias[:, None, None]

time: 160 us -> 151 us (0.944)
  matrix products: 12.7 us -> 6.61 us
  other arithmetic: 20.2 us -> 18.3 us
    dot_general x5 -> x4, matrix products: 12.7 us -> 6.61 us  [the longest x1 3.84 us: on_device(): spectral = jnp.einsum('ckx,ky->cxy', inverted, table, precision=high)]
    unnamed x47 -> x46, local copies, waits for them, and re-layouts: 11.7 us -> 11.9 us
  transfers between devices with their start and end apart: 9 -> 9, of which waited for: 6 -> 6; matrix products, arithmetic and copies ran while one was open for 22% -> 21% of each run, Pallas kernels for 0% -> 0%
where the time goes in v3:
time: 151 us; the launch traced here: 150 us
  starting transfers between devices  46.8 us (31%)
  waiting for transfers between devices  44.1 us (29%)
  local copies, waits for them, and re-layouts  32.8 us (22%)
  other arithmetic  18.3 us (12%)
  matrix products  6.61 us (4%)
    all_to_all x1, waiting for transfers between devices, on_device(): lax.all_to_all(spec_y, 'rows', split_axis=2, concat_axis=3, tiled=True)  14.8 us
    all_to_all x1, waiting for transfers between devices, on_device(): lax.all_to_all(sent, 'chan', split_axis=2, concat_axis=2, tiled=True)  14.2 us
    all_to_all x1, starting transfers between devices, on_device(): lax.all_to_all(spec_y, 'rows', split_axis=2, concat_axis=3, tiled=True)  12.9 us
    unnamed x46, local copies, waits for them, and re-layouts  11.9 us
    ppermute x1, starting transfers between devices, rows_halo_pair(): lax.ppermute(high, 'rows', backward)  8.74 us
    all_to_all x1, starting transfers between devices, on_device(): lax.all_to_all(inverted, 'rows', split_axis=3, concat_axis=2, tiled=True)  6.78 us
    all_to_all x1, waiting for transfers between devices, on_device(): lax.all_to_all(spectra, 'chan', split_axis=3, concat_axis=0, tiled=True)  5.04 us
    all_to_all x1, waiting for transfers between devices, on_device(): lax.all_to_all(inverted, 'rows', split_axis=3, concat_axis=2, tiled=True)  5.03 us
  transfers between devices with their start and end apart: 9, of which 6 were waited for; matrix products, arithmetic and copies ran while one was open for 21% of the time, Pallas kernels for 0%

profile of v3, /device:TPU:1, one launch (start us, length us, event | category | flops | bytes accessed | tf_op | source)
XLA Modules:
  0.0 149.8 jit_solution(13124099951658667160)
XLA Ops:
  2.2 1.1 slice_bitcast_fusion.1
  4.0 8.7 %collective-permute-start.1 = (f32[35840]{0:T(1024)}, f32[35840]{0:T(1024)}, u32[]{:S(2)}, u32[]{:S(2)}) collective-permute-start(f32[35840]{0:T(1024)} %pad_maximum_fusion.10), channel_id=1, source_target_pairs={{8,0},{16,8},{24,16},{32,24},{40,32},{48,40},{56,48},{64,56},{72,6... | collective-permute-start | bytes 430088 | tf_op jit(solution)/shard_map/ppermute | solution.py:100
  12.7 4.1 %sine_negate_fusion = (f32[128,2048]{1,0:T(8,128)S(1)}, f32[128,2048]{1,0:T(8,128)S(1)}) fusion(), kind=kLoop, calls=%fused_computation.37 | loop fusion | flops 3932160 | bytes 2097152 | tf_op jit(solution)/shard_map/neg | solution.py:36
  16.8 1.2 fusion.17
  19.1 2.2 %reshape.131 = f32[64,1,512]{2,1,0:T(1,128)} reshape(f32[128,4,2,32]{3,2,1,0:T(2,128)} %bitcast.196) | data formatting | bytes 262144
  21.3 12.9 %all-to-all-start = ((f32[64,1,512]{2,1,0:T(1,128)}), f32[64,1,512]{2,1,0:T(1,128)S(1)}, u32[]{:S(2)}, u32[]{:S(2)}) async-start(f32[64,1,512]{2,1,0:T(1,128)} %reshape.131), calls=%async_computation | async-start | bytes 262144 | tf_op jit(solution)/shard_map/all_to_all | solution.py:158
  34.9 3.5 %collective-permute-start = (f32[35840]{0:T(1024)}, f32[35840]{0:T(1024)}, u32[]{:S(2)}, u32[]{:S(2)}) collective-permute-start(f32[35840]{0:T(1024)} %pad_maximum_fusion.9), channel_id=1, source_target_pairs={{0,8},{8,16},{16,24},{24,32},{32,40},{40,48},{48,56},{56,64},{64,7... | collective-permute-start | bytes 430088 | tf_op jit(solution)/shard_map/ppermute | solution.py:99
  38.4 14.8 %all-to-all-done = f32[64,1,512]{2,1,0:T(1,128)S(1)} async-done(((f32[64,1,512]{2,1,0:T(1,128)}), f32[64,1,512]{2,1,0:T(1,128)S(1)}, u32[]{:S(2)}, u32[]{:S(2)}) %all-to-all-start) | async-done | bytes 131104 | tf_op jit(solution)/shard_map/all_to_all | solution.py:158
  54.6 1.2 reshape.132
  55.9 1.1 copy.58
  57.8 1.3 all_to_all.56
  61.9 4.2 %all-to-all-start.1 = ((f32[8,1,256]{2,1,0:T(1,128)}), f32[8,1,256]{2,1,0:T(1,128)S(1)}, u32[]{:S(2)}, u32[]{:S(2)}) async-start(f32[8,1,256]{2,1,0:T(1,128)} %reshape.133), calls=%async_computation.1 | async-start | bytes 16384 | tf_op jit(solution)/shard_map/all_to_all | solution.py:170
  66.1 5.0 %all-to-all-done.1 = f32[8,1,256]{2,1,0:T(1,128)S(1)} async-done(((f32[8,1,256]{2,1,0:T(1,128)}), f32[8,1,256]{2,1,0:T(1,128)S(1)}, u32[]{:S(2)}, u32[]{:S(2)}) %all-to-all-start.1) | async-done | bytes 8224 | tf_op jit(solution)/shard_map/all_to_all | solution.py:170
  72.6 1.7 %fusion.28 = (f32[2,16,32]{2,1,0:T(8,128)S(1)}, f32[2,16,32]{2,1,0:T(8,128)S(1)}, f32[2,16,32]{2,1,0:T(8,128)S(1)}, f32[2,16,32]{2,1,0:T(8,128)S(1)}) fusion(f32[2,2,16,32,32]{4,3,2,1,0:T(8,128)} %param.11, f32[2,16,32]{2,1,0:T(8,128)S(1)} %copy.105, f32[2,16,32]{2,1,0:T(8,128)S(1)} %copy.104), kind=kLoop, calls=%fused_computation.47 | loop fusion | flops 258048 | bytes 286720
  75.6 3.4 %all-to-all-start.2 = ((f32[8,1,256]{2,1,0:T(1,128)}), f32[8,1,256]{2,1,0:T(1,128)S(1)}, u32[]{:S(2)}, u32[]{:S(2)}) async-start(f32[8,1,256]{2,1,0:T(1,128)} %reshape.135), calls=%async_computation.2 | async-start | bytes 16384 | tf_op jit(solution)/shard_map/all_to_all | solution.py:179
  80.5 3.3 %all-to-all-done.2 = f32[8,1,256]{2,1,0:T(1,128)S(1)} async-done(((f32[8,1,256]{2,1,0:T(1,128)}), f32[8,1,256]{2,1,0:T(1,128)S(1)}, u32[]{:S(2)}, u32[]{:S(2)}) %all-to-all-start.2) | async-done | bytes 8224 | tf_op jit(solution)/shard_map/all_to_all | solution.py:179
  88.2 1.4 pad_maximum_fusion.7
  89.7 1.2 copy.115
  90.9 2.7 %reshape.137 = f32[64,1,640]{2,1,0:T(1,128)} reshape(f32[64,4,2,2,40]{4,3,2,1,0:T(2,128)} %bitcast.199) | data formatting | bytes 327680
  93.5 6.8 %all-to-all-start.3 = ((f32[64,1,640]{2,1,0:T(1,128)}), f32[64,1,640]{2,1,0:T(1,128)S(1)}, u32[]{:S(2)}, u32[]{:S(2)}) async-start(f32[64,1,640]{2,1,0:T(1,128)} %reshape.137), calls=%async_computation.3 | async-start | bytes 327680 | tf_op jit(solution)/shard_map/all_to_all | solution.py:195
  101.0 1.5 %slice.338 = f32[32768]{0:T(1024)} slice(f32[35840]{0:T(1024)} %collective-permute-done.1), slice={[0:32768]} | slice | bytes 262144 | tf_op jit(solution)/shard_map/slice | solution.py:95
  103.5 1.5 %slice.337 = f32[32768]{0:T(1024)} slice(f32[35840]{0:T(1024)} %collective-permute-done), slice={[0:32768]} | slice | bytes 262144 | tf_op jit(solution)/shard_map/slice | solution.py:95
  105.1 1.6 %reshape.117 = f32[4,4,2048]{2,1,0:T(4,128)} reshape(f32[32768]{0:T(1024)} %slice.337) | data formatting | bytes 262144 | tf_op jit(solution)/shard_map/reshape | solution.py:95
  107.6 2.2 %collective-permute-start.2 = (f32[3,40,4]{2,1,0:T(8,128)S(1)}, f32[3,40,4]{2,1,0:T(8,128)S(1)}, u32[]{:S(2)}, u32[]{:S(2)}) collective-permute-start(f32[3,40,4]{2,1,0:T(8,128)S(1)} %get-tuple-element.21), channel_id=1, source_target_pairs={{0,1},{1,2},{2,3},{3,4},{4,5},{5,6},{6,7},{8,9},{9,10},{10,11},{11... | collective-permute-start | bytes 5768 | tf_op jit(solution)/shard_map/ppermute | solution.py:21
  109.8 1.3 collective-permute-start.3
  111.1 2.2 %pad_maximum_fusion.1 = f32[4,40,2048]{2,1,0:T(8,128)} fusion(f32[4,4,2048]{2,1,0:T(4,128)S(1)} %reshape.118, f32[4,32,2048]{2,1,0:T(8,128)S(1)} %copy-done, f32[4,4,2048]{2,1,0:T(4,128)} %reshape.117), kind=kLoop, calls=%fused_computation.17 | loop fusion | flops 655360 | bytes 2621440 | tf_op jit(solution)/shard_map/concatenate | solution.py:102
  113.3 1.8 %collective-permute-done.3 = f32[3,40,4]{2,1,0:T(8,128)S(1)} collective-permute-done((f32[3,40,4]{2,1,0:T(8,128)S(1)}, f32[3,40,4]{2,1,0:T(8,128)S(1)}, u32[]{:S(2)}, u32[]{:S(2)}) %collective-permute-start.3) | collective-permute-done | bytes 1952 | tf_op jit(solution)/shard_map/ppermute | solution.py:24
  115.2 5.0 %all-to-all-done.3 = f32[64,1,640]{2,1,0:T(1,128)S(1)} async-done(((f32[64,1,640]{2,1,0:T(1,128)}), f32[64,1,640]{2,1,0:T(1,128)S(1)}, u32[]{:S(2)}, u32[]{:S(2)}) %all-to-all-start.3) | async-done | bytes 163872 | tf_op jit(solution)/shard_map/all_to_all | solution.py:195
  123.5 3.8 %fusion.9 = f32[4,40,2048]{2,1,0:T(8,128)S(1)} fusion(f32[4]{0:T(128)S(1)} %copy-done.12, f32[4,40,2048]{2,1,0:T(8,128)S(1)} %copy-done.1, f32[128,2048]{1,0:T(8,128)S(1)} %get-tuple-element.40, f32[128,2048]{1,0:T(8,128)S(1)} %get-tuple-element.41, f32[4]{0:T(128)S(1)} %copy-done.13, f32[4,256,40]{2,1,0:T(8,128)S(1)} %bitcast.203, ...), kind=kOutput, calls=%fused_computation.16 | convolution fusion | flops 525836288 | bytes 4883488 | tf_op jit(solution)/shard_map/ckx,ky->cxy/dot_general | solution.py:200
  128.6 1.1 copy.74
  129.7 3.7 %all-to-all-start.4 = ((f32[2,40,8,264]{3,1,0,2:T(8,128)}), f32[2,40,8,264]{3,1,0,2:T(8,128)S(1)}, u32[]{:S(2)}, u32[]{:S(2)}) async-start(f32[2,40,8,264]{3,1,0,2:T(8,128)} %copy.74), calls=%async_computation.4 | async-start | bytes 1966080 | tf_op jit(solution)/shard_map/all_to_all | solution.py:207
  133.4 14.2 %all-to-all-done.4 = f32[2,40,8,264]{3,1,0,2:T(8,128)S(1)} async-done(((f32[2,40,8,264]{3,1,0,2:T(8,128)}), f32[2,40,8,264]{3,1,0,2:T(8,128)S(1)}, u32[]{:S(2)}, u32[]{:S(2)}) %all-to-all-start.4) | async-done | bytes 675872 | tf_op jit(solution)/shard_map/all_to_all | solution.py:207
  (117 shorter events, 26.6 us)
Async XLA Ops:
  1.4 0.8 copy-start.2
  1.4 0.8 copy-start.4
  3.3 13.6 %copy-start = (f32[4,32,2048]{2,1,0:T(8,128)S(1)}, f32[4,32,2048]{2,1,0:T(8,128)}, u32[]{:S(2)}) copy-start(f32[4,32,2048]{2,1,0:T(8,128)} %param.9) | copy-start | bytes 3145732
  4.0 75.0 %collective-permute-start.1 = (f32[35840]{0:T(1024)}, f32[35840]{0:T(1024)}, u32[]{:S(2)}, u32[]{:S(2)}) collective-permute-start(f32[35840]{0:T(1024)} %pad_maximum_fusion.10), channel_id=1, source_target_pairs={{8,0},{16,8},{24,16},{32,24},{40,32},{48,40},{56,48},{64,56},{72,6... | collective-permute-start | bytes 430088 | tf_op jit(solution)/shard_map/ppermute | solution.py:100
  21.3 31.9 %all-to-all-start = ((f32[64,1,512]{2,1,0:T(1,128)}), f32[64,1,512]{2,1,0:T(1,128)S(1)}, u32[]{:S(2)}, u32[]{:S(2)}) async-start(f32[64,1,512]{2,1,0:T(1,128)} %reshape.131), calls=%async_computation | async-start | bytes 262144 | tf_op jit(solution)/shard_map/all_to_all | solution.py:158
  34.9 44.8 %collective-permute-start = (f32[35840]{0:T(1024)}, f32[35840]{0:T(1024)}, u32[]{:S(2)}, u32[]{:S(2)}) collective-permute-start(f32[35840]{0:T(1024)} %pad_maximum_fusion.9), channel_id=1, source_target_pairs={{0,8},{8,16},{16,24},{24,32},{32,40},{40,48},{48,56},{56,64},{64,7... | collective-permute-start | bytes 430088 | tf_op jit(solution)/shard_map/ppermute | solution.py:99
  61.9 9.3 %all-to-all-start.1 = ((f32[8,1,256]{2,1,0:T(1,128)}), f32[8,1,256]{2,1,0:T(1,128)S(1)}, u32[]{:S(2)}, u32[]{:S(2)}) async-start(f32[8,1,256]{2,1,0:T(1,128)} %reshape.133), calls=%async_computation.1 | async-start | bytes 16384 | tf_op jit(solution)/shard_map/all_to_all | solution.py:170
  72.5 12.5 %copy-start.11 = (pred[65]{0:T(512)(128)(4,1)S(1)}, pred[65]{0:T(512)(128)(4,1)}, u32[]{:S(2)}) copy-start(pred[65]{0:T(512)(128)(4,1)} %constant.37.clone.1) | copy-start | bytes 199
  75.6 8.2 %all-to-all-start.2 = ((f32[8,1,256]{2,1,0:T(1,128)}), f32[8,1,256]{2,1,0:T(1,128)S(1)}, u32[]{:S(2)}, u32[]{:S(2)}) async-start(f32[8,1,256]{2,1,0:T(1,128)} %reshape.135), calls=%async_computation.2 | async-start | bytes 16384 | tf_op jit(solution)/shard_map/all_to_all | solution.py:179
  80.5 19.8 %copy-start.7 = (f32[3,4,256]{2,1,0:T(4,128)}, f32[3,4,256]{2,1,0:T(4,128)S(1)}, u32[]{:S(2)}) copy-start(f32[3,4,256]{2,1,0:T(4,128)S(1)} %slice.268) | copy-start | bytes 36868
  89.6 10.7 %copy-start.3 = (f32[1,32,256]{2,1,0:T(8,128)S(1)}, f32[1,32,256]{2,1,0:T(8,128)}, u32[]{:S(2)}) copy-start(f32[1,32,256]{2,1,0:T(8,128)} %copy-done.2) | copy-start | bytes 98308
  89.6 10.7 %copy-start.5 = (f32[1,32,256]{2,1,0:T(8,128)S(1)}, f32[1,32,256]{2,1,0:T(8,128)}, u32[]{:S(2)}) copy-start(f32[1,32,256]{2,1,0:T(8,128)} %copy-done.4) | copy-start | bytes 98308
  89.6 10.7 %copy-start.6 = (f32[32,256]{1,0:T(8,128)S(1)}, f32[32,256]{1,0:T(8,128)}, u32[]{:S(2)}) copy-start(f32[32,256]{1,0:T(8,128)} %param.10) | copy-start | bytes 98308
  93.5 26.7 %all-to-all-start.3 = ((f32[64,1,640]{2,1,0:T(1,128)}), f32[64,1,640]{2,1,0:T(1,128)S(1)}, u32[]{:S(2)}, u32[]{:S(2)}) async-start(f32[64,1,640]{2,1,0:T(1,128)} %reshape.137), calls=%async_computation.3 | async-start | bytes 327680 | tf_op jit(solution)/shard_map/all_to_all | solution.py:195
  107.6 5.7 %collective-permute-start.2 = (f32[3,40,4]{2,1,0:T(8,128)S(1)}, f32[3,40,4]{2,1,0:T(8,128)S(1)}, u32[]{:S(2)}, u32[]{:S(2)}) collective-permute-start(f32[3,40,4]{2,1,0:T(8,128)S(1)} %get-tuple-element.21), channel_id=1, source_target_pairs={{0,1},{1,2},{2,3},{3,4},{4,5},{5,6},{6,7},{8,9},{9,10},{10,11},{11... | collective-permute-start | bytes 5768 | tf_op jit(solution)/shard_map/ppermute | solution.py:21
  109.8 5.3 %copy-start.8 = (f32[3,4,256]{2,1,0:T(4,128)S(1)}, f32[3,4,256]{2,1,0:T(4,128)}, u32[]{:S(2)}) copy-start(f32[3,4,256]{2,1,0:T(4,128)} %copy-done.7) | copy-start | bytes 36868
  109.8 5.3 %collective-permute-start.3 = (f32[3,40,4]{2,1,0:T(8,128)S(1)}, f32[3,40,4]{2,1,0:T(8,128)S(1)}, u32[]{:S(2)}, u32[]{:S(2)}) collective-permute-start(f32[3,40,4]{2,1,0:T(8,128)S(1)} %get-tuple-element.22), channel_id=1, source_target_pairs={{1,0},{2,1},{3,2},{4,3},{5,4},{6,5},{7,6},{9,8},{10,9},{11,10},{12... | collective-permute-start | bytes 5768 | tf_op jit(solution)/shard_map/ppermute | solution.py:24
  121.2 1.4 copy-start.12
  121.2 1.4 copy-start.13
  122.2 1.3 copy-start.1
  123.5 3.8 %copy-start.9 = (f32[2,4]{1,0:T(2,128)S(1)}, f32[2,4]{1,0:T(2,128)}, u32[]{:S(2)}) copy-start(f32[2,4]{1,0:T(2,128)} %param.14) | copy-start | bytes 100
  129.7 17.9 %copy-start.10 = (f32[2]{0:T(128)S(1)}, f32[2]{0:T(128)}, u32[]{:S(2)}) copy-start(f32[2]{0:T(128)} %param.15) | copy-start | bytes 28
  129.7 17.9 %all-to-all-start.4 = ((f32[2,40,8,264]{3,1,0,2:T(8,128)}), f32[2,40,8,264]{3,1,0,2:T(8,128)S(1)}, u32[]{:S(2)}, u32[]{:S(2)}) async-start(f32[2,40,8,264]{3,1,0,2:T(8,128)} %copy.74), calls=%async_computation.4 | async-start | bytes 1966080 | tf_op jit(solution)/shard_map/all_to_all | solution.py:207

commit v4 on v3

--- a/solution.py
+++ b/solution.py
@@ -204,8 +204,16 @@
     )
     partial_speed = jnp.sum(project_weight[:, :, None, None] * activated[None], axis=1)
     sent = windows(partial_speed, chan_devices, tile_cols, halo)
-    received = lax.all_to_all(sent, "chan", split_axis=2, concat_axis=2, tiled=True)
-    speed = jnp.sum(received, axis=2) + project_bias[:, None, None]
+    sent = jnp.moveaxis(sent, 2, 0)
+    chunk_shape = sent.shape[1:]
+    chunk = math.prod(chunk_shape)
+    lanes = 128
+    flat_len = -(-chunk // lanes) * lanes
+    flat = jnp.pad(sent.reshape(chan_devices, chunk), ((0, 0), (0, flat_len - chunk)))
+    flat = flat.reshape(chan_devices, flat_len // lanes, lanes)
+    received = lax.all_to_all(flat, "chan", split_axis=0, concat_axis=0, tiled=True)
+    speed = jnp.sum(received, axis=0).reshape(-1)[:chunk].reshape(chunk_shape)
+    speed = speed + project_bias[:, None, None]
     speed = speed * fields[2][None]
     velocity = speed[:, halo : halo + row_count, halo : halo + tile_cols]
 

time: 151 us -> 148 us (0.980)
  waiting for transfers between devices: 44.1 us -> 40.7 us
    all_to_all x1, waiting for transfers between devices: 14.2 us -> 10.7 us  [on_device(): lax.all_to_all(flat, 'chan', split_axis=0, concat_axis=0, tiled=True)]
    reshape x0 -> x1, local copies, waits for them, and re-layouts: none -> 1.58 us  [on_device(): flat = flat.reshape(chan_devices, flat_len // lanes, lanes)]
  transfers between devices with their start and end apart: 9 -> 9, of which waited for: 6 -> 6; matrix products, arithmetic and copies ran while one was open for 21% -> 22% of each run, Pallas kernels for 0% -> 0%
where the time goes in v4:
time: 148 us; the launch traced here: 147 us
  starting transfers between devices  46.7 us (32%)
  waiting for transfers between devices  40.7 us (28%)
  local copies, waits for them, and re-layouts  33.6 us (23%)
  other arithmetic  18.2 us (12%)
  matrix products  6.61 us (4%)
    all_to_all x1, waiting for transfers between devices, on_device(): lax.all_to_all(spec_y, 'rows', split_axis=2, concat_axis=3, tiled=True)  14.8 us
    all_to_all x1, starting transfers between devices, on_device(): lax.all_to_all(spec_y, 'rows', split_axis=2, concat_axis=3, tiled=True)  12.9 us
    unnamed x46, local copies, waits for them, and re-layouts  11.9 us
    all_to_all x1, waiting for transfers between devices, on_device(): lax.all_to_all(flat, 'chan', split_axis=0, concat_axis=0, tiled=True)  10.7 us
    ppermute x1, starting transfers between devices, rows_halo_pair(): lax.ppermute(high, 'rows', backward)  8.74 us
    all_to_all x1, starting transfers between devices, on_device(): lax.all_to_all(inverted, 'rows', split_axis=3, concat_axis=2, tiled=True)  6.78 us
    all_to_all x1, waiting for transfers between devices, on_device(): lax.all_to_all(spectra, 'chan', split_axis=3, concat_axis=0, tiled=True)  5.04 us
    all_to_all x1, waiting for transfers between devices, on_device(): lax.all_to_all(inverted, 'rows', split_axis=3, concat_axis=2, tiled=True)  5.02 us
  transfers between devices with their start and end apart: 9, of which 6 were waited for; matrix products, arithmetic and copies ran while one was open for 22% of the time, Pallas kernels for 0%

profile of v4, /device:TPU:1, one launch (start us, length us, event | category | flops | bytes accessed | tf_op | source)
XLA Modules:
  0.0 147.1 jit_solution(13804513456609999441)
XLA Ops:
  2.2 1.1 slice_bitcast_fusion.1
  4.0 8.7 %collective-permute-start.1 = (f32[35840]{0:T(1024)}, f32[35840]{0:T(1024)}, u32[]{:S(2)}, u32[]{:S(2)}) collective-permute-start(f32[35840]{0:T(1024)} %pad_maximum_fusion.9), channel_id=1, source_target_pairs={{8,0},{16,8},{24,16},{32,24},{40,32},{48,40},{56,48},{64,56},{72,6... | collective-permute-start | bytes 430088 | tf_op jit(solution)/shard_map/ppermute | solution.py:100
  12.7 4.1 %sine_negate_fusion = (f32[128,2048]{1,0:T(8,128)S(1)}, f32[128,2048]{1,0:T(8,128)S(1)}) fusion(), kind=kLoop, calls=%fused_computation.37 | loop fusion | flops 3932160 | bytes 2097152 | tf_op jit(solution)/shard_map/neg | solution.py:36
  16.8 1.2 fusion.17
  19.1 2.2 %reshape.137 = f32[64,1,512]{2,1,0:T(1,128)} reshape(f32[128,4,2,32]{3,2,1,0:T(2,128)} %bitcast.200) | data formatting | bytes 262144
  21.3 12.9 %all-to-all-start = ((f32[64,1,512]{2,1,0:T(1,128)}), f32[64,1,512]{2,1,0:T(1,128)S(1)}, u32[]{:S(2)}, u32[]{:S(2)}) async-start(f32[64,1,512]{2,1,0:T(1,128)} %reshape.137), calls=%async_computation | async-start | bytes 262144 | tf_op jit(solution)/shard_map/all_to_all | solution.py:158
  34.9 3.5 %collective-permute-start = (f32[35840]{0:T(1024)}, f32[35840]{0:T(1024)}, u32[]{:S(2)}, u32[]{:S(2)}) collective-permute-start(f32[35840]{0:T(1024)} %pad_maximum_fusion.8), channel_id=1, source_target_pairs={{0,8},{8,16},{16,24},{24,32},{32,40},{40,48},{48,56},{56,64},{64,7... | collective-permute-start | bytes 430088 | tf_op jit(solution)/shard_map/ppermute | solution.py:99
  38.4 14.8 %all-to-all-done = f32[64,1,512]{2,1,0:T(1,128)S(1)} async-done(((f32[64,1,512]{2,1,0:T(1,128)}), f32[64,1,512]{2,1,0:T(1,128)S(1)}, u32[]{:S(2)}, u32[]{:S(2)}) %all-to-all-start) | async-done | bytes 131104 | tf_op jit(solution)/shard_map/all_to_all | solution.py:158
  54.6 1.2 reshape.138
  55.8 1.1 copy.73
  57.8 1.3 all_to_all.56
  61.9 4.2 %all-to-all-start.1 = ((f32[8,1,256]{2,1,0:T(1,128)}), f32[8,1,256]{2,1,0:T(1,128)S(1)}, u32[]{:S(2)}, u32[]{:S(2)}) async-start(f32[8,1,256]{2,1,0:T(1,128)} %reshape.139), calls=%async_computation.1 | async-start | bytes 16384 | tf_op jit(solution)/shard_map/all_to_all | solution.py:170
  66.1 5.0 %all-to-all-done.1 = f32[8,1,256]{2,1,0:T(1,128)S(1)} async-done(((f32[8,1,256]{2,1,0:T(1,128)}), f32[8,1,256]{2,1,0:T(1,128)S(1)}, u32[]{:S(2)}, u32[]{:S(2)}) %all-to-all-start.1) | async-done | bytes 8224 | tf_op jit(solution)/shard_map/all_to_all | solution.py:170
  72.6 1.7 %fusion.28 = (f32[2,16,32]{2,1,0:T(8,128)S(1)}, f32[2,16,32]{2,1,0:T(8,128)S(1)}, f32[2,16,32]{2,1,0:T(8,128)S(1)}, f32[2,16,32]{2,1,0:T(8,128)S(1)}) fusion(f32[2,2,16,32,32]{4,3,2,1,0:T(8,128)} %param.11, f32[2,16,32]{2,1,0:T(8,128)S(1)} %copy.120, f32[2,16,32]{2,1,0:T(8,128)S(1)} %copy.119), kind=kLoop, calls=%fused_computation.47 | loop fusion | flops 258048 | bytes 286720
  75.5 3.4 %all-to-all-start.2 = ((f32[8,1,256]{2,1,0:T(1,128)}), f32[8,1,256]{2,1,0:T(1,128)S(1)}, u32[]{:S(2)}, u32[]{:S(2)}) async-start(f32[8,1,256]{2,1,0:T(1,128)} %reshape.141), calls=%async_computation.2 | async-start | bytes 16384 | tf_op jit(solution)/shard_map/all_to_all | solution.py:179
  80.5 3.3 %all-to-all-done.2 = f32[8,1,256]{2,1,0:T(1,128)S(1)} async-done(((f32[8,1,256]{2,1,0:T(1,128)}), f32[8,1,256]{2,1,0:T(1,128)S(1)}, u32[]{:S(2)}, u32[]{:S(2)}) %all-to-all-start.2) | async-done | bytes 8224 | tf_op jit(solution)/shard_map/all_to_all | solution.py:179
  88.2 1.4 pad_maximum_fusion.6
  89.6 1.2 copy.130
  90.8 2.7 %reshape.143 = f32[64,1,640]{2,1,0:T(1,128)} reshape(f32[64,4,2,2,40]{4,3,2,1,0:T(2,128)} %bitcast.203) | data formatting | bytes 327680
  93.5 6.8 %all-to-all-start.3 = ((f32[64,1,640]{2,1,0:T(1,128)}), f32[64,1,640]{2,1,0:T(1,128)S(1)}, u32[]{:S(2)}, u32[]{:S(2)}) async-start(f32[64,1,640]{2,1,0:T(1,128)} %reshape.143), calls=%async_computation.3 | async-start | bytes 327680 | tf_op jit(solution)/shard_map/all_to_all | solution.py:195
  101.0 1.5 %slice.338 = f32[32768]{0:T(1024)} slice(f32[35840]{0:T(1024)} %collective-permute-done.1), slice={[0:32768]} | slice | bytes 262144 | tf_op jit(solution)/shard_map/slice | solution.py:95
  103.5 1.5 %slice.337 = f32[32768]{0:T(1024)} slice(f32[35840]{0:T(1024)} %collective-permute-done), slice={[0:32768]} | slice | bytes 262144 | tf_op jit(solution)/shard_map/slice | solution.py:95
  105.0 1.6 %reshape.122 = f32[4,4,2048]{2,1,0:T(4,128)} reshape(f32[32768]{0:T(1024)} %slice.337) | data formatting | bytes 262144 | tf_op jit(solution)/shard_map/reshape | solution.py:95
  107.6 2.2 %collective-permute-start.2 = (f32[3,40,4]{2,1,0:T(8,128)S(1)}, f32[3,40,4]{2,1,0:T(8,128)S(1)}, u32[]{:S(2)}, u32[]{:S(2)}) collective-permute-start(f32[3,40,4]{2,1,0:T(8,128)S(1)} %get-tuple-element.21), channel_id=1, source_target_pairs={{0,1},{1,2},{2,3},{3,4},{4,5},{5,6},{6,7},{8,9},{9,10},{10,11},{11... | collective-permute-start | bytes 5768 | tf_op jit(solution)/shard_map/ppermute | solution.py:21
  109.8 1.3 collective-permute-start.3
  111.1 2.2 %pad_maximum_fusion.1 = f32[4,40,2048]{2,1,0:T(8,128)} fusion(f32[4,4,2048]{2,1,0:T(4,128)S(1)} %reshape.123, f32[4,32,2048]{2,1,0:T(8,128)S(1)} %copy-done, f32[4,4,2048]{2,1,0:T(4,128)} %reshape.122), kind=kLoop, calls=%fused_computation.17 | loop fusion | flops 655360 | bytes 2621440 | tf_op jit(solution)/shard_map/concatenate | solution.py:102
  113.3 1.8 %collective-permute-done.3 = f32[3,40,4]{2,1,0:T(8,128)S(1)} collective-permute-done((f32[3,40,4]{2,1,0:T(8,128)S(1)}, f32[3,40,4]{2,1,0:T(8,128)S(1)}, u32[]{:S(2)}, u32[]{:S(2)}) %collective-permute-start.3) | collective-permute-done | bytes 1952 | tf_op jit(solution)/shard_map/ppermute | solution.py:24
  115.2 5.0 %all-to-all-done.3 = f32[64,1,640]{2,1,0:T(1,128)S(1)} async-done(((f32[64,1,640]{2,1,0:T(1,128)}), f32[64,1,640]{2,1,0:T(1,128)S(1)}, u32[]{:S(2)}, u32[]{:S(2)}) %all-to-all-start.3) | async-done | bytes 163872 | tf_op jit(solution)/shard_map/all_to_all | solution.py:195
  123.5 3.8 %fusion.9 = f32[4,40,2048]{2,1,0:T(8,128)S(1)} fusion(f32[4]{0:T(128)S(1)} %copy-done.12, f32[4,40,2048]{2,1,0:T(8,128)S(1)} %copy-done.1, f32[128,2048]{1,0:T(8,128)S(1)} %get-tuple-element.40, f32[128,2048]{1,0:T(8,128)S(1)} %get-tuple-element.41, f32[4]{0:T(128)S(1)} %copy-done.13, f32[4,256,40]{2,1,0:T(8,128)S(1)} %bitcast.207, ...), kind=kOutput, calls=%fused_computation.16 | convolution fusion | flops 525836288 | bytes 4883488 | tf_op jit(solution)/shard_map/ckx,ky->cxy/dot_general | solution.py:200
  128.7 1.6 %reshape.126 = f32[8,165,128]{2,1,0:T(8,128)} reshape(f32[8,2,40,264]{3,2,1,0:T(8,128)S(1)} %copy.89) | data formatting | bytes 1351680 | tf_op jit(solution)/shard_map/reshape | solution.py:213
  130.3 3.7 %all-to-all-start.4 = ((f32[8,165,128]{2,1,0:T(8,128)}), f32[8,165,128]{2,1,0:T(8,128)S(1)}, u32[]{:S(2)}, u32[]{:S(2)}) async-start(f32[8,165,128]{2,1,0:T(8,128)} %reshape.126), calls=%async_computation.4 | async-start | bytes 1376256 | tf_op jit(solution)/shard_map/all_to_all | solution.py:214
  134.0 10.7 %all-to-all-done.4 = f32[8,165,128]{2,1,0:T(8,128)S(1)} async-done(((f32[8,165,128]{2,1,0:T(8,128)}), f32[8,165,128]{2,1,0:T(8,128)S(1)}, u32[]{:S(2)}, u32[]{:S(2)}) %all-to-all-start.4) | async-done | bytes 675872 | tf_op jit(solution)/shard_map/all_to_all | solution.py:214
  (119 shorter events, 26.9 us)
Async XLA Ops:
  1.4 1.9 %copy-start.2 = (f32[1,32,256]{2,1,0:T(8,128)}, f32[1,32,256]{2,1,0:T(8,128)S(1)}, u32[]{:S(2)}) copy-start(f32[1,32,256]{2,1,0:T(8,128)S(1)} %get-tuple-element.38) | copy-start | bytes 98308
  1.4 1.9 %copy-start.4 = (f32[1,32,256]{2,1,0:T(8,128)}, f32[1,32,256]{2,1,0:T(8,128)S(1)}, u32[]{:S(2)}) copy-start(f32[1,32,256]{2,1,0:T(8,128)S(1)} %get-tuple-element.39) | copy-start | bytes 98308
  3.3 13.6 %copy-start = (f32[4,32,2048]{2,1,0:T(8,128)S(1)}, f32[4,32,2048]{2,1,0:T(8,128)}, u32[]{:S(2)}) copy-start(f32[4,32,2048]{2,1,0:T(8,128)} %param.9) | copy-start | bytes 3145732
  4.0 75.0 %collective-permute-start.1 = (f32[35840]{0:T(1024)}, f32[35840]{0:T(1024)}, u32[]{:S(2)}, u32[]{:S(2)}) collective-permute-start(f32[35840]{0:T(1024)} %pad_maximum_fusion.9), channel_id=1, source_target_pairs={{8,0},{16,8},{24,16},{32,24},{40,32},{48,40},{56,48},{64,56},{72,6... | collective-permute-start | bytes 430088 | tf_op jit(solution)/shard_map/ppermute | solution.py:100
  21.3 31.9 %all-to-all-start = ((f32[64,1,512]{2,1,0:T(1,128)}), f32[64,1,512]{2,1,0:T(1,128)S(1)}, u32[]{:S(2)}, u32[]{:S(2)}) async-start(f32[64,1,512]{2,1,0:T(1,128)} %reshape.137), calls=%async_computation | async-start | bytes 262144 | tf_op jit(solution)/shard_map/all_to_all | solution.py:158
  34.9 44.8 %collective-permute-start = (f32[35840]{0:T(1024)}, f32[35840]{0:T(1024)}, u32[]{:S(2)}, u32[]{:S(2)}) collective-permute-start(f32[35840]{0:T(1024)} %pad_maximum_fusion.8), channel_id=1, source_target_pairs={{0,8},{8,16},{16,24},{24,32},{32,40},{40,48},{48,56},{56,64},{64,7... | collective-permute-start | bytes 430088 | tf_op jit(solution)/shard_map/ppermute | solution.py:99
  61.9 9.3 %all-to-all-start.1 = ((f32[8,1,256]{2,1,0:T(1,128)}), f32[8,1,256]{2,1,0:T(1,128)S(1)}, u32[]{:S(2)}, u32[]{:S(2)}) async-start(f32[8,1,256]{2,1,0:T(1,128)} %reshape.139), calls=%async_computation.1 | async-start | bytes 16384 | tf_op jit(solution)/shard_map/all_to_all | solution.py:170
  72.5 12.5 %copy-start.11 = (pred[65]{0:T(512)(128)(4,1)S(1)}, pred[65]{0:T(512)(128)(4,1)}, u32[]{:S(2)}) copy-start(pred[65]{0:T(512)(128)(4,1)} %constant.37.clone.1) | copy-start | bytes 199
  75.5 8.2 %all-to-all-start.2 = ((f32[8,1,256]{2,1,0:T(1,128)}), f32[8,1,256]{2,1,0:T(1,128)S(1)}, u32[]{:S(2)}, u32[]{:S(2)}) async-start(f32[8,1,256]{2,1,0:T(1,128)} %reshape.141), calls=%async_computation.2 | async-start | bytes 16384 | tf_op jit(solution)/shard_map/all_to_all | solution.py:179
  89.6 10.7 %copy-start.3 = (f32[1,32,256]{2,1,0:T(8,128)S(1)}, f32[1,32,256]{2,1,0:T(8,128)}, u32[]{:S(2)}) copy-start(f32[1,32,256]{2,1,0:T(8,128)} %copy-done.2) | copy-start | bytes 98308
  89.6 10.7 %copy-start.5 = (f32[1,32,256]{2,1,0:T(8,128)S(1)}, f32[1,32,256]{2,1,0:T(8,128)}, u32[]{:S(2)}) copy-start(f32[1,32,256]{2,1,0:T(8,128)} %copy-done.4) | copy-start | bytes 98308
  89.6 10.7 %copy-start.7 = (f32[32,256]{1,0:T(8,128)S(1)}, f32[32,256]{1,0:T(8,128)}, u32[]{:S(2)}) copy-start(f32[32,256]{1,0:T(8,128)} %param.10) | copy-start | bytes 98308
  93.5 26.7 %all-to-all-start.3 = ((f32[64,1,640]{2,1,0:T(1,128)}), f32[64,1,640]{2,1,0:T(1,128)S(1)}, u32[]{:S(2)}, u32[]{:S(2)}) async-start(f32[64,1,640]{2,1,0:T(1,128)} %reshape.143), calls=%async_computation.3 | async-start | bytes 327680 | tf_op jit(solution)/shard_map/all_to_all | solution.py:195
  107.6 5.7 %collective-permute-start.2 = (f32[3,40,4]{2,1,0:T(8,128)S(1)}, f32[3,40,4]{2,1,0:T(8,128)S(1)}, u32[]{:S(2)}, u32[]{:S(2)}) collective-permute-start(f32[3,40,4]{2,1,0:T(8,128)S(1)} %get-tuple-element.21), channel_id=1, source_target_pairs={{0,1},{1,2},{2,3},{3,4},{4,5},{5,6},{6,7},{8,9},{9,10},{10,11},{11... | collective-permute-start | bytes 5768 | tf_op jit(solution)/shard_map/ppermute | solution.py:21
  109.8 5.3 %copy-start.6 = (f32[1,32,256]{2,1,0:T(8,128)S(1)}, f32[1,32,256]{2,1,0:T(8,128)}, u32[]{:S(2)}) copy-start(f32[1,32,256]{2,1,0:T(8,128)} %copy-done.4) | copy-start | bytes 98308
  109.8 5.3 %copy-start.8 = (f32[32,256]{1,0:T(8,128)S(1)}, f32[32,256]{1,0:T(8,128)}, u32[]{:S(2)}) copy-start(f32[32,256]{1,0:T(8,128)} %param.10) | copy-start | bytes 98308
  109.8 5.3 %collective-permute-start.3 = (f32[3,40,4]{2,1,0:T(8,128)S(1)}, f32[3,40,4]{2,1,0:T(8,128)S(1)}, u32[]{:S(2)}, u32[]{:S(2)}) collective-permute-start(f32[3,40,4]{2,1,0:T(8,128)S(1)} %get-tuple-element.22), channel_id=1, source_target_pairs={{1,0},{2,1},{3,2},{4,3},{5,4},{6,5},{7,6},{9,8},{10,9},{11,10},{12... | collective-permute-start | bytes 5768 | tf_op jit(solution)/shard_map/ppermute | solution.py:24
  121.2 1.4 copy-start.12
  121.2 1.4 copy-start.13
  122.2 1.3 copy-start.1
  123.5 3.8 %copy-start.9 = (f32[2,4]{1,0:T(2,128)S(1)}, f32[2,4]{1,0:T(2,128)}, u32[]{:S(2)}) copy-start(f32[2,4]{1,0:T(2,128)} %param.14) | copy-start | bytes 100
  130.3 14.6 %copy-start.10 = (f32[2]{0:T(128)S(1)}, f32[2]{0:T(128)}, u32[]{:S(2)}) copy-start(f32[2]{0:T(128)} %param.15) | copy-start | bytes 28
  130.3 14.4 %all-to-all-start.4 = ((f32[8,165,128]{2,1,0:T(8,128)}), f32[8,165,128]{2,1,0:T(8,128)S(1)}, u32[]{:S(2)}, u32[]{:S(2)}) async-start(f32[8,165,128]{2,1,0:T(8,128)} %reshape.126), calls=%async_computation.4 | async-start | bytes 1376256 | tf_op jit(solution)/shard_map/all_to_all | solution.py:214

commit v5 on v4

--- a/solution.py
+++ b/solution.py
@@ -154,9 +154,10 @@
     x_modes = x_table.shape[0] // 2
 
     spec_y = jnp.einsum("cxy,ky->ckx", hidden, table, precision=high)
-    spec_y = spec_y.reshape(local_chan, 2, all_ymodes, row_count)
-    by_freq = lax.all_to_all(spec_y, "rows", split_axis=2, concat_axis=3, tiled=True)
-    parts = jnp.einsum("caqx,kx->caqk", by_freq, x_table, precision=high)
+    spec_y = spec_y.reshape(local_chan, 2, row_devices, local_ymodes, row_count)
+    by_freq = lax.all_to_all(spec_y, "rows", split_axis=2, concat_axis=0, tiled=False)
+    blocked_table = x_table.reshape(x_table.shape[0], row_devices, row_count)
+    parts = jnp.einsum("scaqx,ksx->caqk", by_freq, blocked_table, precision=high)
     cos_part = parts[..., :x_modes]
     sin_part = parts[..., x_modes:]
     real_in = unfold_modes(

time: 148 us -> 151 us (1.020)
  waiting for transfers between devices: 40.7 us -> 30.6 us
  starting transfers between devices: 46.7 us -> 54 us
  other arithmetic: 18.2 us -> 24 us
    all_to_all x1, waiting for transfers between devices: 14.8 us -> 6.17 us  [on_device(): lax.all_to_all(spec_y, 'rows', split_axis=2, concat_axis=0, tiled=False)]
    ppermute x1, starting transfers between devices: 8.74 us -> 1.91 us  [rows_halo_pair(): lax.ppermute(high, 'rows', backward)]
    all_to_all x1, starting transfers between devices: 6.78 us -> 13.5 us  [on_device(): lax.all_to_all(inverted, 'rows', split_axis=3, concat_axis=2, tiled=True)]
    all_to_all x1, starting transfers between devices: 12.9 us -> 19.6 us  [on_device(): lax.all_to_all(spec_y, 'rows', split_axis=2, concat_axis=0, tiled=False)]
    cos x0 -> x1, other arithmetic: none -> 5.85 us  [base_table(): return jnp.concatenate([jnp.cos(phase), -jnp.sin(phase)])]
    another operation x0 -> x1, local copies, waits for them, and re-layouts: none -> 2.19 us  [on_device(): lax.all_to_all(spec_y, 'rows', split_axis=2, concat_axis=0, tiled=False)]
    all_to_all x4 -> x2, local copies, waits for them, and re-layouts: 3.84 us -> 1.87 us  [on_device(): lax.all_to_all(spec_y, 'rows', split_axis=2, concat_axis=0, tiled=False)]
    ppermute x1, waiting for transfers between devices: 1.78 us -> 0.01 us  [with_halo(): lax.ppermute(lax.slice_in_dim(block, 0, width, axis=dim), axis, backward)]
  transfers between devices with their start and end apart: 9 -> 9, of which waited for: 6 -> 5; matrix products, arithmetic and copies ran while one was open for 22% -> 21% of each run, Pallas kernels for 0% -> 0%
where the time goes in v5:
time: 151 us; the launch traced here: 150 us
  starting transfers between devices  54 us (36%)
  local copies, waits for them, and re-layouts  32.2 us (21%)
  waiting for transfers between devices  30.6 us (20%)
  other arithmetic  24 us (16%)
  matrix products  7.93 us (5%)
    all_to_all x1, starting transfers between devices, on_device(): lax.all_to_all(spec_y, 'rows', split_axis=2, concat_axis=0, tiled=False)  19.6 us
    all_to_all x1, starting transfers between devices, on_device(): lax.all_to_all(inverted, 'rows', split_axis=3, concat_axis=2, tiled=True)  13.5 us
    all_to_all x1, waiting for transfers between devices, on_device(): lax.all_to_all(flat, 'chan', split_axis=0, concat_axis=0, tiled=True)  10.7 us
    unnamed x46, local copies, waits for them, and re-layouts  10.5 us
    all_to_all x1, waiting for transfers between devices, on_device(): lax.all_to_all(spec_y, 'rows', split_axis=2, concat_axis=0, tiled=False)  6.17 us
    cos x1, other arithmetic, base_table(): return jnp.concatenate([jnp.cos(phase), -jnp.sin(phase)])  5.85 us
    all_to_all x1, waiting for transfers between devices, on_device(): lax.all_to_all(inverted, 'rows', split_axis=3, concat_axis=2, tiled=True)  5.33 us
    all_to_all x1, waiting for transfers between devices, on_device(): lax.all_to_all(spectra, 'chan', split_axis=3, concat_axis=0, tiled=True)  5.04 us
  transfers between devices with their start and end apart: 9, of which 5 were waited for; matrix products, arithmetic and copies ran while one was open for 21% of the time, Pallas kernels for 0%

profile of v5, /device:TPU:1, one launch (start us, length us, event | category | flops | bytes accessed | tf_op | source)
XLA Modules:
  0.0 150.0 jit_solution(17843001796350159462)
XLA Ops:
  0.6 4.1 %sine_negate_fusion.1 = (f32[128,2048]{1,0:T(8,128)S(1)}, f32[128,2048]{1,0:T(8,128)S(1)}) fusion(), kind=kLoop, calls=%fused_computation.49 | loop fusion | flops 3932160 | bytes 2097152 | tf_op jit(solution)/shard_map/neg | solution.py:36
  4.8 1.2 fusion.18
  6.9 2.2 %copy.110 = f32[1,4,2,64,2,32]{5,1,4,2,0,3:T(4,128)} copy(f32[1,4,2,64,2,32]{5,4,3,2,1,0:T(2,128)} %bitcast.191) | data formatting | bytes 262144 | tf_op jit(solution)/shard_map/broadcast_in_dim;reshape | solution.py:158
  9.1 2.0 %reshape.157 = f32[64,1,512]{2,1,0:T(1,128)} reshape(f32[64,1,2,2,4,32]{5,4,3,2,1,0:T(4,128)} %bitcast.192) | data formatting | bytes 262144
  11.2 19.6 %all-to-all-start = ((f32[64,1,512]{2,1,0:T(1,128)}), f32[64,1,512]{2,1,0:T(1,128)S(1)}, u32[]{:S(2)}, u32[]{:S(2)}) async-start(f32[64,1,512]{2,1,0:T(1,128)} %reshape.157), calls=%async_computation | async-start | bytes 262144 | tf_op jit(solution)/shard_map/all_to_all | solution.py:158
  31.6 3.5 %collective-permute-start = (f32[35840]{0:T(1024)}, f32[35840]{0:T(1024)}, u32[]{:S(2)}, u32[]{:S(2)}) collective-permute-start(f32[35840]{0:T(1024)} %pad_maximum_fusion.7), channel_id=1, source_target_pairs={{0,8},{8,16},{16,24},{24,32},{32,40},{40,48},{48,56},{56,64},{64,7... | collective-permute-start | bytes 430088 | tf_op jit(solution)/shard_map/ppermute | solution.py:99
  35.8 1.9 %collective-permute-start.1 = (f32[35840]{0:T(1024)}, f32[35840]{0:T(1024)}, u32[]{:S(2)}, u32[]{:S(2)}) collective-permute-start(f32[35840]{0:T(1024)} %pad_maximum_fusion.8), channel_id=1, source_target_pairs={{8,0},{16,8},{24,16},{32,24},{40,32},{48,40},{56,48},{64,56},{72,6... | collective-permute-start | bytes 430088 | tf_op jit(solution)/shard_map/ppermute | solution.py:100
  37.8 5.8 %fusion.41 = (f32[128,64,32]{0,1,2:T(8,128)}, f32[128,64,32]{0,1,2:T(8,128)}) fusion(s32[64,32]{0,1:T(8,128)S(1)} %multiply_add_fusion), kind=kLoop, calls=%fused_computation.67 | loop fusion | flops 3932160 | bytes 2105344 | tf_op jit(solution)/shard_map/cos | solution.py:36
  43.6 6.2 %all-to-all-done = f32[64,1,512]{2,1,0:T(1,128)S(1)} async-done(((f32[64,1,512]{2,1,0:T(1,128)}), f32[64,1,512]{2,1,0:T(1,128)S(1)}, u32[]{:S(2)}, u32[]{:S(2)}) %all-to-all-start) | async-done | bytes 131104 | tf_op jit(solution)/shard_map/all_to_all | solution.py:158
  51.4 1.1 reshape.158
  52.5 1.3 copy.58
  53.7 2.3 %fusion.21 = f32[4,2,2,256]{3,0,2,1:T(4,128)S(1)} fusion(f32[128,64,32]{0,1,2:T(8,128)} %get-tuple-element.32, f32[128,64,32]{0,1,2:T(8,128)} %get-tuple-element.31, f32[1,4,2,64,2,32]{3,1,5,4,2,0:T(4,128)S(1)} %copy.58), kind=kOutput, calls=%fused_computation.39 | convolution fusion | flops 50855936 | bytes 2244608 | tf_op jit(solution)/shard_map/scaqx,ksx->caqk/dot_general | solution.py:160
  57.7 4.2 %all-to-all-start.1 = ((f32[8,1,256]{2,1,0:T(1,128)}), f32[8,1,256]{2,1,0:T(1,128)S(1)}, u32[]{:S(2)}, u32[]{:S(2)}) async-start(f32[8,1,256]{2,1,0:T(1,128)} %reshape.159), calls=%async_computation.1 | async-start | bytes 16384 | tf_op jit(solution)/shard_map/all_to_all | solution.py:171
  62.0 5.0 %all-to-all-done.1 = f32[8,1,256]{2,1,0:T(1,128)S(1)} async-done(((f32[8,1,256]{2,1,0:T(1,128)}), f32[8,1,256]{2,1,0:T(1,128)S(1)}, u32[]{:S(2)}, u32[]{:S(2)}) %all-to-all-start.1) | async-done | bytes 8224 | tf_op jit(solution)/shard_map/all_to_all | solution.py:171
  68.6 1.7 %fusion.36 = (f32[2,16,32]{2,1,0:T(8,128)S(1)}, f32[2,16,32]{2,1,0:T(8,128)S(1)}, f32[2,16,32]{2,1,0:T(8,128)S(1)}, f32[2,16,32]{2,1,0:T(8,128)S(1)}) fusion(f32[2,2,16,32,32]{4,3,2,1,0:T(8,128)} %param.11, f32[2,16,32]{2,1,0:T(8,128)S(1)} %copy.98, f32[2,16,32]{2,1,0:T(8,128)S(1)} %copy.97), kind=kLoop, calls=%fused_computation.60 | loop fusion | flops 258048 | bytes 286720
  71.5 3.5 %all-to-all-start.2 = ((f32[8,1,256]{2,1,0:T(1,128)}), f32[8,1,256]{2,1,0:T(1,128)S(1)}, u32[]{:S(2)}, u32[]{:S(2)}) async-start(f32[8,1,256]{2,1,0:T(1,128)} %reshape.161), calls=%async_computation.2 | async-start | bytes 16384 | tf_op jit(solution)/shard_map/all_to_all | solution.py:180
  76.5 3.3 %all-to-all-done.2 = f32[8,1,256]{2,1,0:T(1,128)S(1)} async-done(((f32[8,1,256]{2,1,0:T(1,128)}), f32[8,1,256]{2,1,0:T(1,128)S(1)}, u32[]{:S(2)}, u32[]{:S(2)}) %all-to-all-start.2) | async-done | bytes 8224 | tf_op jit(solution)/shard_map/all_to_all | solution.py:180
  84.4 1.4 pad_maximum_fusion.5
  85.8 1.2 copy.109
  87.0 2.7 %reshape.163 = f32[64,1,640]{2,1,0:T(1,128)} reshape(f32[64,4,2,2,40]{4,3,2,1,0:T(2,128)} %bitcast.193) | data formatting | bytes 327680
  89.7 13.5 %all-to-all-start.3 = ((f32[64,1,640]{2,1,0:T(1,128)}), f32[64,1,640]{2,1,0:T(1,128)S(1)}, u32[]{:S(2)}, u32[]{:S(2)}) async-start(f32[64,1,640]{2,1,0:T(1,128)} %reshape.163), calls=%async_computation.3 | async-start | bytes 327680 | tf_op jit(solution)/shard_map/all_to_all | solution.py:196
  104.7 2.8 %collective-permute-start.2 = (f32[3,40,4]{2,1,0:T(8,128)}, f32[3,40,4]{2,1,0:T(8,128)}, u32[]{:S(2)}, u32[]{:S(2)}) collective-permute-start(f32[3,40,4]{2,1,0:T(8,128)} %get-tuple-element.21), channel_id=1, source_target_pairs={{0,1},{1,2},{2,3},{3,4},{4,5},{5,6},{6,7},{8,9},{9,10},{10,11},{11... | collective-permute-start | bytes 5768 | tf_op jit(solution)/shard_map/ppermute | solution.py:21
  107.6 1.3 collective-permute-start.3
  108.8 1.6 %slice.337 = f32[32768]{0:T(1024)} slice(f32[35840]{0:T(1024)} %collective-permute-done), slice={[0:32768]} | slice | bytes 262144 | tf_op jit(solution)/shard_map/slice | solution.py:95
  111.4 1.6 %slice.338 = f32[32768]{0:T(1024)} slice(f32[35840]{0:T(1024)} %collective-permute-done.1), slice={[0:32768]} | slice | bytes 262144 | tf_op jit(solution)/shard_map/slice | solution.py:95
  112.9 1.6 %reshape.141 = f32[4,4,2048]{2,1,0:T(4,128)} reshape(f32[32768]{0:T(1024)} %slice.338) | data formatting | bytes 262144 | tf_op jit(solution)/shard_map/reshape | solution.py:95
  114.5 2.2 %pad_maximum_fusion.4 = f32[4,40,2048]{2,1,0:T(8,128)} fusion(f32[4,4,2048]{2,1,0:T(4,128)} %reshape.141, f32[4,32,2048]{2,1,0:T(8,128)S(1)} %copy-done, f32[4,4,2048]{2,1,0:T(4,128)S(1)} %reshape.140), kind=kLoop, calls=%fused_computation.22 | loop fusion | flops 655360 | bytes 2621440 | tf_op jit(solution)/shard_map/concatenate | solution.py:102
  117.7 5.3 %all-to-all-done.3 = f32[64,1,640]{2,1,0:T(1,128)S(1)} async-done(((f32[64,1,640]{2,1,0:T(1,128)}), f32[64,1,640]{2,1,0:T(1,128)S(1)}, u32[]{:S(2)}, u32[]{:S(2)}) %all-to-all-start.3) | async-done | bytes 163872 | tf_op jit(solution)/shard_map/all_to_all | solution.py:196
  126.4 3.8 %fusion.10 = f32[4,40,2048]{2,1,0:T(8,128)S(1)} fusion(f32[4]{0:T(128)S(1)} %copy-done.12, f32[4,40,2048]{2,1,0:T(8,128)S(1)} %copy-done.1, f32[128,2048]{1,0:T(8,128)S(1)} %get-tuple-element.43, f32[128,2048]{1,0:T(8,128)S(1)} %get-tuple-element.44, f32[4]{0:T(128)S(1)} %copy-done.13, f32[4,256,40]{2,1,0:T(8,128)S(1)} %bitcast.197, ...), kind=kOutput, calls=%fused_computation.21 | convolution fusion | flops 525836288 | bytes 4883488 | tf_op jit(solution)/shard_map/ckx,ky->cxy/dot_general | solution.py:201
  131.7 1.6 %reshape.144 = f32[8,165,128]{2,1,0:T(8,128)} reshape(f32[8,2,40,264]{3,2,1,0:T(8,128)S(1)} %copy.68) | data formatting | bytes 1351680 | tf_op jit(solution)/shard_map/reshape | solution.py:214
  133.3 3.7 %all-to-all-start.4 = ((f32[8,165,128]{2,1,0:T(8,128)}), f32[8,165,128]{2,1,0:T(8,128)S(1)}, u32[]{:S(2)}, u32[]{:S(2)}) async-start(f32[8,165,128]{2,1,0:T(8,128)} %reshape.144), calls=%async_computation.4 | async-start | bytes 1376256 | tf_op jit(solution)/shard_map/all_to_all | solution.py:215
  137.0 10.7 %all-to-all-done.4 = f32[8,165,128]{2,1,0:T(8,128)S(1)} async-done(((f32[8,165,128]{2,1,0:T(8,128)}), f32[8,165,128]{2,1,0:T(8,128)S(1)}, u32[]{:S(2)}, u32[]{:S(2)}) %all-to-all-start.4) | async-done | bytes 675872 | tf_op jit(solution)/shard_map/all_to_all | solution.py:215
  (118 shorter events, 24.8 us)
Async XLA Ops:
  0.6 4.1 %copy-start = (f32[4,32,2048]{2,1,0:T(8,128)S(1)}, f32[4,32,2048]{2,1,0:T(8,128)}, u32[]{:S(2)}) copy-start(f32[4,32,2048]{2,1,0:T(8,128)} %param.9) | copy-start | bytes 3145732
  6.9 23.9 %copy-start.7 = (s32[32,256]{1,0:T(8,128)S(1)}, s32[32,256]{1,0:T(8,128)}, u32[]{:S(2)}) copy-start(s32[32,256]{1,0:T(8,128)} %param.16) | copy-start | bytes 98308
  6.9 23.9 %copy-start.8 = (s32[32,256]{1,0:T(8,128)S(1)}, s32[32,256]{1,0:T(8,128)}, u32[]{:S(2)}) copy-start(s32[32,256]{1,0:T(8,128)} %param.17) | copy-start | bytes 98308
  6.9 23.9 %copy-start.5 = (f32[32,256]{1,0:T(8,128)S(1)}, f32[32,256]{1,0:T(8,128)}, u32[]{:S(2)}) copy-start(f32[32,256]{1,0:T(8,128)} %param.10) | copy-start | bytes 98308
  11.2 38.6 %all-to-all-start = ((f32[64,1,512]{2,1,0:T(1,128)}), f32[64,1,512]{2,1,0:T(1,128)S(1)}, u32[]{:S(2)}, u32[]{:S(2)}) async-start(f32[64,1,512]{2,1,0:T(1,128)} %reshape.157), calls=%async_computation | async-start | bytes 262144 | tf_op jit(solution)/shard_map/all_to_all | solution.py:158
  30.9 12.8 %copy-start.2 = (f32[1,32,256]{2,1,0:T(8,128)}, f32[1,32,256]{2,1,0:T(8,128)S(1)}, u32[]{:S(2)}) copy-start(f32[1,32,256]{2,1,0:T(8,128)S(1)} %get-tuple-element.42) | copy-start | bytes 98308
  31.6 43.5 %collective-permute-start = (f32[35840]{0:T(1024)}, f32[35840]{0:T(1024)}, u32[]{:S(2)}, u32[]{:S(2)}) collective-permute-start(f32[35840]{0:T(1024)} %pad_maximum_fusion.7), channel_id=1, source_target_pairs={{0,8},{8,16},{16,24},{24,32},{32,40},{40,48},{48,56},{56,64},{64,7... | collective-permute-start | bytes 430088 | tf_op jit(solution)/shard_map/ppermute | solution.py:99
  35.8 40.0 %collective-permute-start.1 = (f32[35840]{0:T(1024)}, f32[35840]{0:T(1024)}, u32[]{:S(2)}, u32[]{:S(2)}) collective-permute-start(f32[35840]{0:T(1024)} %pad_maximum_fusion.8), channel_id=1, source_target_pairs={{8,0},{16,8},{24,16},{32,24},{40,32},{48,40},{56,48},{64,56},{72,6... | collective-permute-start | bytes 430088 | tf_op jit(solution)/shard_map/ppermute | solution.py:100
  57.7 9.3 %all-to-all-start.1 = ((f32[8,1,256]{2,1,0:T(1,128)}), f32[8,1,256]{2,1,0:T(1,128)S(1)}, u32[]{:S(2)}, u32[]{:S(2)}) async-start(f32[8,1,256]{2,1,0:T(1,128)} %reshape.159), calls=%async_computation.1 | async-start | bytes 16384 | tf_op jit(solution)/shard_map/all_to_all | solution.py:171
  68.5 12.7 %copy-start.11 = (pred[65]{0:T(512)(128)(4,1)S(1)}, pred[65]{0:T(512)(128)(4,1)}, u32[]{:S(2)}) copy-start(pred[65]{0:T(512)(128)(4,1)} %constant.38.clone.1) | copy-start | bytes 199
  71.5 8.3 %all-to-all-start.2 = ((f32[8,1,256]{2,1,0:T(1,128)}), f32[8,1,256]{2,1,0:T(1,128)S(1)}, u32[]{:S(2)}, u32[]{:S(2)}) async-start(f32[8,1,256]{2,1,0:T(1,128)} %reshape.161), calls=%async_computation.2 | async-start | bytes 16384 | tf_op jit(solution)/shard_map/all_to_all | solution.py:180
  85.8 17.4 %copy-start.3 = (f32[1,32,256]{2,1,0:T(8,128)S(1)}, f32[1,32,256]{2,1,0:T(8,128)}, u32[]{:S(2)}) copy-start(f32[1,32,256]{2,1,0:T(8,128)} %copy-done.2) | copy-start | bytes 98308
  89.7 33.4 %all-to-all-start.3 = ((f32[64,1,640]{2,1,0:T(1,128)}), f32[64,1,640]{2,1,0:T(1,128)S(1)}, u32[]{:S(2)}, u32[]{:S(2)}) async-start(f32[64,1,640]{2,1,0:T(1,128)} %reshape.163), calls=%async_computation.3 | async-start | bytes 327680 | tf_op jit(solution)/shard_map/all_to_all | solution.py:196
  104.7 12.0 %collective-permute-start.2 = (f32[3,40,4]{2,1,0:T(8,128)}, f32[3,40,4]{2,1,0:T(8,128)}, u32[]{:S(2)}, u32[]{:S(2)}) collective-permute-start(f32[3,40,4]{2,1,0:T(8,128)} %get-tuple-element.21), channel_id=1, source_target_pairs={{0,1},{1,2},{2,3},{3,4},{4,5},{5,6},{6,7},{8,9},{9,10},{10,11},{11... | collective-permute-start | bytes 5768 | tf_op jit(solution)/shard_map/ppermute | solution.py:21
  107.6 9.2 %collective-permute-start.3 = (f32[3,40,4]{2,1,0:T(8,128)}, f32[3,40,4]{2,1,0:T(8,128)}, u32[]{:S(2)}, u32[]{:S(2)}) collective-permute-start(f32[3,40,4]{2,1,0:T(8,128)} %get-tuple-element.22), channel_id=1, source_target_pairs={{1,0},{2,1},{3,2},{4,3},{5,4},{6,5},{7,6},{9,8},{10,9},{11,10},{12... | collective-permute-start | bytes 5768 | tf_op jit(solution)/shard_map/ppermute | solution.py:24
  114.5 2.2 %copy-start.4 = (f32[1,32,256]{2,1,0:T(8,128)S(1)}, f32[1,32,256]{2,1,0:T(8,128)}, u32[]{:S(2)}) copy-start(f32[1,32,256]{2,1,0:T(8,128)} %copy-done.2) | copy-start | bytes 98308
  114.5 2.2 %copy-start.6 = (f32[32,256]{1,0:T(8,128)S(1)}, f32[32,256]{1,0:T(8,128)}, u32[]{:S(2)}) copy-start(f32[32,256]{1,0:T(8,128)} %param.10) | copy-start | bytes 98308
  124.2 1.4 copy-start.12
  124.2 1.4 copy-start.13
  125.1 1.3 copy-start.1
  126.4 3.8 %copy-start.9 = (f32[2,4]{1,0:T(2,128)S(1)}, f32[2,4]{1,0:T(2,128)}, u32[]{:S(2)}) copy-start(f32[2,4]{1,0:T(2,128)} %param.14) | copy-start | bytes 100
  133.3 14.6 %copy-start.10 = (f32[2]{0:T(128)S(1)}, f32[2]{0:T(128)}, u32[]{:S(2)}) copy-start(f32[2]{0:T(128)} %param.15) | copy-start | bytes 28
  133.3 14.4 %all-to-all-start.4 = ((f32[8,165,128]{2,1,0:T(8,128)}), f32[8,165,128]{2,1,0:T(8,128)S(1)}, u32[]{:S(2)}, u32[]{:S(2)}) async-start(f32[8,165,128]{2,1,0:T(8,128)} %reshape.144), calls=%async_computation.4 | async-start | bytes 1376256 | tf_op jit(solution)/shard_map/all_to_all | solution.py:215

commit v6 on v4

--- a/solution.py
+++ b/solution.py
@@ -141,9 +141,6 @@
     fields = jnp.stack(
         [front, front_flags.astype(jnp.float32), ice_mask.astype(jnp.float32)]
     )
-    hidden_win, fields = rows_halo_pair(hidden, fields, halo)
-    fields = with_halo(fields, (("chan", 2),), halo)
-    fields, hidden_win = lax.optimization_barrier((fields, hidden_win))
 
     table = base_table(all_ymodes, columns)
     half = all_xmodes // 2
@@ -156,6 +153,10 @@
     spec_y = jnp.einsum("cxy,ky->ckx", hidden, table, precision=high)
     spec_y = spec_y.reshape(local_chan, 2, all_ymodes, row_count)
     by_freq = lax.all_to_all(spec_y, "rows", split_axis=2, concat_axis=3, tiled=True)
+    hidden_late, fields, by_freq = lax.optimization_barrier((hidden, fields, by_freq))
+    hidden_win, fields = rows_halo_pair(hidden_late, fields, halo)
+    fields = with_halo(fields, (("chan", 2),), halo)
+    fields, hidden_win = lax.optimization_barrier((fields, hidden_win))
     parts = jnp.einsum("caqx,kx->caqk", by_freq, x_table, precision=high)
     cos_part = parts[..., :x_modes]
     sin_part = parts[..., x_modes:]

time: 148 us -> 148 us (level)
  starting transfers between devices: 46.7 us -> 48.2 us
    all_to_all x1, starting transfers between devices: 12.9 us -> 19.6 us  [on_device(): lax.all_to_all(spec_y, 'rows', split_axis=2, concat_axis=3, tiled=True)]
    ppermute x1, starting transfers between devices: 8.74 us -> 2.57 us  [rows_halo_pair(): lax.ppermute(high, 'rows', backward)]
    all_to_all x1, waiting for transfers between devices: 5.04 us -> 1.07 us  [on_device(): lax.all_to_all(spectra, 'chan', split_axis=3, concat_axis=0, tiled=True)]
    all_to_all x1, waiting for transfers between devices: 14.8 us -> 18.5 us  [on_device(): lax.all_to_all(spec_y, 'rows', split_axis=2, concat_axis=3, tiled=True)]
    all_to_all x1, waiting for transfers between devices: 3.32 us -> 0.98 us  [on_device(): lax.all_to_all(jnp.stack([real_out, imag_out], axis=2), 'chan', split_axi...]
    reshape x2, local copies, waits for them, and re-layouts: 2.54 us -> 0.99 us  [unpacked(): return (flat[:split].reshape(a_shape), flat[split:].reshape(b_shape))]
    unnamed x46 -> x41, local copies, waits for them, and re-layouts: 11.9 us -> 12.4 us
  transfers between devices with their start and end apart: 9 -> 9, of which waited for: 6 -> 6; matrix products, arithmetic and copies ran while one was open for 22% -> 18% of each run, Pallas kernels for 0% -> 0%
where the time goes in v6:
time: 148 us; the launch traced here: 147 us
  starting transfers between devices  48.2 us (33%)
  waiting for transfers between devices  39.6 us (27%)
  local copies, waits for them, and re-layouts  34.2 us (23%)
  other arithmetic  17.2 us (12%)
  matrix products  6.62 us (4%)
    all_to_all x1, starting transfers between devices, on_device(): lax.all_to_all(spec_y, 'rows', split_axis=2, concat_axis=3, tiled=True)  19.6 us
    all_to_all x1, waiting for transfers between devices, on_device(): lax.all_to_all(spec_y, 'rows', split_axis=2, concat_axis=3, tiled=True)  18.5 us
    unnamed x41, local copies, waits for them, and re-layouts  12.4 us
    all_to_all x1, waiting for transfers between devices, on_device(): lax.all_to_all(flat, 'chan', split_axis=0, concat_axis=0, tiled=True)  10.7 us
    all_to_all x1, starting transfers between devices, on_device(): lax.all_to_all(inverted, 'rows', split_axis=3, concat_axis=2, tiled=True)  6.95 us
    all_to_all x1, waiting for transfers between devices, on_device(): lax.all_to_all(inverted, 'rows', split_axis=3, concat_axis=2, tiled=True)  5.5 us
    all_to_all x1, starting transfers between devices, on_device(): lax.all_to_all(jnp.stack([real_out, imag_out], axis=2), 'chan', split_axi...  4.37 us
    all_to_all x1, starting transfers between devices, on_device(): lax.all_to_all(spectra, 'chan', split_axis=3, concat_axis=0, tiled=True)  4.22 us
  transfers between devices with their start and end apart: 9, of which 6 were waited for; matrix products, arithmetic and copies ran while one was open for 18% of the time, Pallas kernels for 0%

profile of v6, /device:TPU:1, one launch (start us, length us, event | category | flops | bytes accessed | tf_op | source)
XLA Modules:
  0.0 147.0 jit_solution(12337561697430436597)
XLA Ops:
  0.6 4.1 %sine_negate_fusion = (f32[128,2048]{1,0:T(8,128)S(1)}, f32[128,2048]{1,0:T(8,128)S(1)}) fusion(), kind=kLoop, calls=%fused_computation.37 | loop fusion | flops 3932160 | bytes 2097152 | tf_op jit(solution)/shard_map/neg | solution.py:36
  4.8 1.2 fusion.17
  6.0 1.0 copy.72
  7.1 2.2 %reshape.137 = f32[64,1,512]{2,1,0:T(1,128)} reshape(f32[128,4,2,32]{3,2,1,0:T(2,128)} %bitcast.200) | data formatting | bytes 262144
  9.3 19.6 %all-to-all-start = ((f32[64,1,512]{2,1,0:T(1,128)}), f32[64,1,512]{2,1,0:T(1,128)S(1)}, u32[]{:S(2)}, u32[]{:S(2)}) async-start(f32[64,1,512]{2,1,0:T(1,128)} %reshape.137), calls=%async_computation | async-start | bytes 262144 | tf_op jit(solution)/shard_map/all_to_all | solution.py:155
  29.0 18.5 %all-to-all-done = f32[64,1,512]{2,1,0:T(1,128)S(1)} async-done(((f32[64,1,512]{2,1,0:T(1,128)}), f32[64,1,512]{2,1,0:T(1,128)S(1)}, u32[]{:S(2)}, u32[]{:S(2)}) %all-to-all-start) | async-done | bytes 131104 | tf_op jit(solution)/shard_map/all_to_all | solution.py:155
  49.1 1.2 reshape.138
  50.3 1.1 copy.73
  52.3 1.3 all_to_all.56
  56.4 4.2 %all-to-all-start.1 = ((f32[8,1,256]{2,1,0:T(1,128)}), f32[8,1,256]{2,1,0:T(1,128)S(1)}, u32[]{:S(2)}, u32[]{:S(2)}) async-start(f32[8,1,256]{2,1,0:T(1,128)} %reshape.139), calls=%async_computation.1 | async-start | bytes 16384 | tf_op jit(solution)/shard_map/all_to_all | solution.py:171
  62.0 2.6 %collective-permute-start.1 = (f32[35840]{0:T(1024)}, f32[35840]{0:T(1024)}, u32[]{:S(2)}, u32[]{:S(2)}) collective-permute-start(f32[35840]{0:T(1024)} %pad_maximum_fusion.9), channel_id=1, source_target_pairs={{8,0},{16,8},{24,16},{32,24},{40,32},{48,40},{56,48},{64,56},{72,6... | collective-permute-start | bytes 430088 | tf_op jit(solution)/shard_map/ppermute | solution.py:100
  64.6 1.1 all-to-all-done.1
  68.7 1.7 %fusion.28 = (f32[2,16,32]{2,1,0:T(8,128)S(1)}, f32[2,16,32]{2,1,0:T(8,128)S(1)}, f32[2,16,32]{2,1,0:T(8,128)S(1)}, f32[2,16,32]{2,1,0:T(8,128)S(1)}) fusion(f32[2,2,16,32,32]{4,3,2,1,0:T(8,128)} %param.11, f32[2,16,32]{2,1,0:T(8,128)S(1)} %copy.120, f32[2,16,32]{2,1,0:T(8,128)S(1)} %copy.119), kind=kLoop, calls=%fused_computation.47 | loop fusion | flops 258048 | bytes 286720
  71.6 4.4 %all-to-all-start.2 = ((f32[8,1,256]{2,1,0:T(1,128)}), f32[8,1,256]{2,1,0:T(1,128)S(1)}, u32[]{:S(2)}, u32[]{:S(2)}) async-start(f32[8,1,256]{2,1,0:T(1,128)} %reshape.141), calls=%async_computation.2 | async-start | bytes 16384 | tf_op jit(solution)/shard_map/all_to_all | solution.py:180
  76.6 3.4 %collective-permute-start = (f32[35840]{0:T(1024)}, f32[35840]{0:T(1024)}, u32[]{:S(2)}, u32[]{:S(2)}) collective-permute-start(f32[35840]{0:T(1024)} %pad_maximum_fusion.8), channel_id=1, source_target_pairs={{0,8},{8,16},{16,24},{24,32},{32,40},{40,48},{48,56},{56,64},{64,7... | collective-permute-start | bytes 430088 | tf_op jit(solution)/shard_map/ppermute | solution.py:99
  84.1 2.0 %reshape.116 = f32[4,2,2,64,32]{4,3,2,1,0:T(8,128)} reshape(f32[4,2,2,2048]{3,2,1,0:T(2,128)} %copy.85) | data formatting | bytes 262144 | tf_op jit(solution)/shard_map/reshape | solution.py:53
  86.1 1.0 reshape.115
  87.1 1.4 pad_maximum_fusion.6
  88.5 1.2 copy.130
  89.7 2.7 %reshape.143 = f32[64,1,640]{2,1,0:T(1,128)} reshape(f32[64,4,2,2,40]{4,3,2,1,0:T(2,128)} %bitcast.203) | data formatting | bytes 327680
  92.4 7.0 %all-to-all-start.3 = ((f32[64,1,640]{2,1,0:T(1,128)}), f32[64,1,640]{2,1,0:T(1,128)}, u32[]{:S(2)}, u32[]{:S(2)}) async-start(f32[64,1,640]{2,1,0:T(1,128)} %reshape.143), calls=%async_computation.3 | async-start | bytes 327680 | tf_op jit(solution)/shard_map/all_to_all | solution.py:196
  102.5 1.6 %slice.337 = f32[32768]{0:T(1024)} slice(f32[35840]{0:T(1024)} %collective-permute-done), slice={[0:32768]} | slice | bytes 262144 | tf_op jit(solution)/shard_map/slice | solution.py:95
  105.9 2.2 %collective-permute-start.2 = (f32[3,40,4]{2,1,0:T(8,128)S(1)}, f32[3,40,4]{2,1,0:T(8,128)S(1)}, u32[]{:S(2)}, u32[]{:S(2)}) collective-permute-start(f32[3,40,4]{2,1,0:T(8,128)S(1)} %get-tuple-element.27), channel_id=1, source_target_pairs={{0,1},{1,2},{2,3},{3,4},{4,5},{5,6},{6,7},{8,9},{9,10},{10,11},{11... | collective-permute-start | bytes 5768 | tf_op jit(solution)/shard_map/ppermute | solution.py:21
  108.1 1.3 collective-permute-start.3
  109.4 1.2 pad_maximum_fusion.1
  110.7 2.8 %collective-permute-done.3 = f32[3,40,4]{2,1,0:T(8,128)S(1)} collective-permute-done((f32[3,40,4]{2,1,0:T(8,128)S(1)}, f32[3,40,4]{2,1,0:T(8,128)S(1)}, u32[]{:S(2)}, u32[]{:S(2)}) %collective-permute-start.3) | collective-permute-done | bytes 1952 | tf_op jit(solution)/shard_map/ppermute | solution.py:24
  113.6 5.5 %all-to-all-done.3 = f32[64,1,640]{2,1,0:T(1,128)} async-done(((f32[64,1,640]{2,1,0:T(1,128)}), f32[64,1,640]{2,1,0:T(1,128)}, u32[]{:S(2)}, u32[]{:S(2)}) %all-to-all-start.3) | async-done | bytes 163872 | tf_op jit(solution)/shard_map/all_to_all | solution.py:196
  119.1 2.0 %reduce.11 = f32[64,640]{1,0:T(8,128)S(1)} reduce(f32[64,1,640]{2,1,0:T(1,128)} %all-to-all-done.3, f32[]{:T(128)} %broadcast.132), dimensions={1}, to_apply=%all_to_all.65.reduce_sub_computation | reduce | bytes 327684 | tf_op jit(solution)/shard_map/all_to_all | solution.py:196
  123.4 3.8 %fusion.9 = f32[4,40,2048]{2,1,0:T(8,128)S(1)} fusion(f32[4]{0:T(128)S(1)} %copy-done.9, f32[4,40,2048]{2,1,0:T(8,128)S(1)} %copy-done.1, f32[128,2048]{1,0:T(8,128)S(1)} %get-tuple-element.46, f32[128,2048]{1,0:T(8,128)S(1)} %get-tuple-element.47, f32[4]{0:T(128)S(1)} %copy-done.10, f32[4,256,40]{2,1,0:T(8,128)S(1)} %bitcast.207, ...), kind=kOutput, calls=%fused_computation.16 | convolution fusion | flops 525836288 | bytes 4883488 | tf_op jit(solution)/shard_map/ckx,ky->cxy/dot_general | solution.py:201
  128.7 1.6 %reshape.126 = f32[8,165,128]{2,1,0:T(8,128)} reshape(f32[8,2,40,264]{3,2,1,0:T(8,128)S(1)} %copy.89) | data formatting | bytes 1351680 | tf_op jit(solution)/shard_map/reshape | solution.py:214
  130.2 3.7 %all-to-all-start.4 = ((f32[8,165,128]{2,1,0:T(8,128)}), f32[8,165,128]{2,1,0:T(8,128)S(1)}, u32[]{:S(2)}, u32[]{:S(2)}) async-start(f32[8,165,128]{2,1,0:T(8,128)} %reshape.126), calls=%async_computation.4 | async-start | bytes 1376256 | tf_op jit(solution)/shard_map/all_to_all | solution.py:215
  133.9 10.7 %all-to-all-done.4 = f32[8,165,128]{2,1,0:T(8,128)S(1)} async-done(((f32[8,165,128]{2,1,0:T(8,128)}), f32[8,165,128]{2,1,0:T(8,128)S(1)}, u32[]{:S(2)}, u32[]{:S(2)}) %all-to-all-start.4) | async-done | bytes 675872 | tf_op jit(solution)/shard_map/all_to_all | solution.py:215
  (114 shorter events, 26.5 us)
Async XLA Ops:
  0.6 4.1 %copy-start = (f32[4,32,2048]{2,1,0:T(8,128)S(1)}, f32[4,32,2048]{2,1,0:T(8,128)}, u32[]{:S(2)}) copy-start(f32[4,32,2048]{2,1,0:T(8,128)} %param.9) | copy-start | bytes 3145732
  5.9 23.0 %copy-start.3 = (s32[32,256]{1,0:T(8,128)S(1)}, s32[32,256]{1,0:T(8,128)}, u32[]{:S(2)}) copy-start(s32[32,256]{1,0:T(8,128)} %param.16) | copy-start | bytes 98308
  5.9 23.0 %copy-start.4 = (s32[32,256]{1,0:T(8,128)S(1)}, s32[32,256]{1,0:T(8,128)}, u32[]{:S(2)}) copy-start(s32[32,256]{1,0:T(8,128)} %param.17) | copy-start | bytes 98308
  6.0 23.0 %copy-start.5 = (f32[32,256]{1,0:T(8,128)S(1)}, f32[32,256]{1,0:T(8,128)}, u32[]{:S(2)}) copy-start(f32[32,256]{1,0:T(8,128)} %param.10) | copy-start | bytes 98308
  9.3 38.2 %all-to-all-start = ((f32[64,1,512]{2,1,0:T(1,128)}), f32[64,1,512]{2,1,0:T(1,128)S(1)}, u32[]{:S(2)}, u32[]{:S(2)}) async-start(f32[64,1,512]{2,1,0:T(1,128)} %reshape.137), calls=%async_computation | async-start | bytes 262144 | tf_op jit(solution)/shard_map/all_to_all | solution.py:155
  56.4 9.3 %all-to-all-start.1 = ((f32[8,1,256]{2,1,0:T(1,128)}), f32[8,1,256]{2,1,0:T(1,128)S(1)}, u32[]{:S(2)}, u32[]{:S(2)}) async-start(f32[8,1,256]{2,1,0:T(1,128)} %reshape.139), calls=%async_computation.1 | async-start | bytes 16384 | tf_op jit(solution)/shard_map/all_to_all | solution.py:171
  62.0 37.4 %collective-permute-start.1 = (f32[35840]{0:T(1024)}, f32[35840]{0:T(1024)}, u32[]{:S(2)}, u32[]{:S(2)}) collective-permute-start(f32[35840]{0:T(1024)} %pad_maximum_fusion.9), channel_id=1, source_target_pairs={{8,0},{16,8},{24,16},{32,24},{40,32},{48,40},{56,48},{64,56},{72,6... | collective-permute-start | bytes 430088 | tf_op jit(solution)/shard_map/ppermute | solution.py:100
  67.7 8.3 %copy-start.2 = (f32[4,16,4,128]{3,1,2,0:T(8,128)S(1)}, f32[4,16,4,128]{3,1,2,0:T(8,128)}, u32[]{:S(2)}) copy-start(f32[4,16,4,128]{3,1,2,0:T(8,128)} %copy.123) | copy-start | bytes 393220
  68.5 13.8 %copy-start.8 = (pred[65]{0:T(512)(128)(4,1)S(1)}, pred[65]{0:T(512)(128)(4,1)}, u32[]{:S(2)}) copy-start(pred[65]{0:T(512)(128)(4,1)} %constant.37.clone.1) | copy-start | bytes 199
  71.6 9.4 %all-to-all-start.2 = ((f32[8,1,256]{2,1,0:T(1,128)}), f32[8,1,256]{2,1,0:T(1,128)S(1)}, u32[]{:S(2)}, u32[]{:S(2)}) async-start(f32[8,1,256]{2,1,0:T(1,128)} %reshape.141), calls=%async_computation.2 | async-start | bytes 16384 | tf_op jit(solution)/shard_map/all_to_all | solution.py:180
  76.6 23.5 %collective-permute-start = (f32[35840]{0:T(1024)}, f32[35840]{0:T(1024)}, u32[]{:S(2)}, u32[]{:S(2)}) collective-permute-start(f32[35840]{0:T(1024)} %pad_maximum_fusion.8), channel_id=1, source_target_pairs={{0,8},{8,16},{16,24},{24,32},{32,40},{40,48},{48,56},{56,64},{64,7... | collective-permute-start | bytes 430088 | tf_op jit(solution)/shard_map/ppermute | solution.py:99
  92.4 26.7 %all-to-all-start.3 = ((f32[64,1,640]{2,1,0:T(1,128)}), f32[64,1,640]{2,1,0:T(1,128)}, u32[]{:S(2)}, u32[]{:S(2)}) async-start(f32[64,1,640]{2,1,0:T(1,128)} %reshape.143), calls=%async_computation.3 | async-start | bytes 327680 | tf_op jit(solution)/shard_map/all_to_all | solution.py:196
  105.9 4.7 %collective-permute-start.2 = (f32[3,40,4]{2,1,0:T(8,128)S(1)}, f32[3,40,4]{2,1,0:T(8,128)S(1)}, u32[]{:S(2)}, u32[]{:S(2)}) collective-permute-start(f32[3,40,4]{2,1,0:T(8,128)S(1)} %get-tuple-element.27), channel_id=1, source_target_pairs={{0,1},{1,2},{2,3},{3,4},{4,5},{5,6},{6,7},{8,9},{9,10},{10,11},{11... | collective-permute-start | bytes 5768 | tf_op jit(solution)/shard_map/ppermute | solution.py:21
  108.1 5.4 %collective-permute-start.3 = (f32[3,40,4]{2,1,0:T(8,128)S(1)}, f32[3,40,4]{2,1,0:T(8,128)S(1)}, u32[]{:S(2)}, u32[]{:S(2)}) collective-permute-start(f32[3,40,4]{2,1,0:T(8,128)S(1)} %get-tuple-element.28), channel_id=1, source_target_pairs={{1,0},{2,1},{3,2},{4,3},{5,4},{6,5},{7,6},{9,8},{10,9},{11,10},{12... | collective-permute-start | bytes 5768 | tf_op jit(solution)/shard_map/ppermute | solution.py:24
  121.1 1.4 copy-start.9
  121.1 1.4 copy-start.10
  122.1 1.3 copy-start.1
  123.4 3.8 %copy-start.6 = (f32[2,4]{1,0:T(2,128)S(1)}, f32[2,4]{1,0:T(2,128)}, u32[]{:S(2)}) copy-start(f32[2,4]{1,0:T(2,128)} %param.14) | copy-start | bytes 100
  130.2 14.6 %copy-start.7 = (f32[2]{0:T(128)S(1)}, f32[2]{0:T(128)}, u32[]{:S(2)}) copy-start(f32[2]{0:T(128)} %param.15) | copy-start | bytes 28
  130.2 14.4 %all-to-all-start.4 = ((f32[8,165,128]{2,1,0:T(8,128)}), f32[8,165,128]{2,1,0:T(8,128)S(1)}, u32[]{:S(2)}, u32[]{:S(2)}) async-start(f32[8,165,128]{2,1,0:T(8,128)} %reshape.126), calls=%async_computation.4 | async-start | bytes 1376256 | tf_op jit(solution)/shard_map/all_to_all | solution.py:215

commit v7 on v6

--- a/solution.py
+++ b/solution.py
@@ -81,21 +81,21 @@
     return jnp.concatenate(bands, axis=-2)
 
 
-def rows_halo_pair(first, second, width):
+def rows_halo_pair(first, second, width, second_width):
     count = lax.axis_size("rows")
     forward = [(i, i + 1) for i in range(count - 1)]
     backward = [(target, source) for source, target in forward]
 
-    def packed(rows):
-        a, b = first[..., rows, :], second[..., rows, :]
+    def packed(rows, second_rows):
+        a, b = first[..., rows, :], second[..., second_rows, :]
         return jnp.concatenate([a.reshape(-1), b.reshape(-1)]), a.shape, b.shape
 
     def unpacked(flat, a_shape, b_shape):
         split = math.prod(a_shape)
         return flat[:split].reshape(a_shape), flat[split:].reshape(b_shape)
 
-    low, a_shape, b_shape = packed(slice(-width, None))
-    high, _, _ = packed(slice(0, width))
+    low, a_shape, b_shape = packed(slice(-width, None), slice(-second_width, None))
+    high, _, _ = packed(slice(0, width), slice(0, second_width))
     low_a, low_b = unpacked(lax.ppermute(low, "rows", forward), a_shape, b_shape)
     high_a, high_b = unpacked(lax.ppermute(high, "rows", backward), a_shape, b_shape)
     return (
@@ -127,6 +127,7 @@
     front_flags,
 ):
     halo = LS_STEPS
+    speed_halo = LS_STEPS - 1
     local_chan, row_count, columns = hidden.shape
     row_devices = lax.axis_size("rows")
     chan_devices = lax.axis_size("chan")
@@ -135,7 +136,7 @@
     all_xmodes = spectral_weight.shape[2] * chan_devices
     all_ymodes = local_ymodes * row_devices
     tile_cols = columns // chan_devices
-    win_rows = row_count + 2 * halo
+    win_rows = row_count + 2 * speed_halo
     norm_scale = 1.0 / math.sqrt(all_rows * columns * all_xmodes * all_ymodes)
 
     fields = jnp.stack(
@@ -154,7 +155,7 @@
     spec_y = spec_y.reshape(local_chan, 2, all_ymodes, row_count)
     by_freq = lax.all_to_all(spec_y, "rows", split_axis=2, concat_axis=3, tiled=True)
     hidden_late, fields, by_freq = lax.optimization_barrier((hidden, fields, by_freq))
-    hidden_win, fields = rows_halo_pair(hidden_late, fields, halo)
+    hidden_win, fields = rows_halo_pair(hidden_late, fields, speed_halo, halo)
     fields = with_halo(fields, (("chan", 2),), halo)
     fields, hidden_win = lax.optimization_barrier((fields, hidden_win))
     parts = jnp.einsum("caqx,kx->caqk", by_freq, x_table, precision=high)
@@ -192,7 +193,7 @@
     )
     coef = jnp.stack([coef_real, coef_imag], axis=1)
     inverted = jnp.einsum("otqk,kx->otqx", coef, x_table, precision=high)
-    inverted = windows(inverted, row_devices, row_count, halo)
+    inverted = windows(inverted, row_devices, row_count, speed_halo)
     inverted = lax.all_to_all(inverted, "rows", split_axis=3, concat_axis=2, tiled=True)
     y_weights = jnp.where(jnp.arange(all_ymodes) == 0, 1.0, 2.0).astype(jnp.float32) * norm_scale
     inverted = inverted.reshape(local_chan, 2, all_ymodes, win_rows) * y_weights[:, None]
@@ -204,7 +205,7 @@
         approximate=False,
     )
     partial_speed = jnp.sum(project_weight[:, :, None, None] * activated[None], axis=1)
-    sent = windows(partial_speed, chan_devices, tile_cols, halo)
+    sent = windows(partial_speed, chan_devices, tile_cols, speed_halo)
     sent = jnp.moveaxis(sent, 2, 0)
     chunk_shape = sent.shape[1:]
     chunk = math.prod(chunk_shape)
@@ -215,20 +216,20 @@
     received = lax.all_to_all(flat, "chan", split_axis=0, concat_axis=0, tiled=True)
     speed = jnp.sum(received, axis=0).reshape(-1)[:chunk].reshape(chunk_shape)
     speed = speed + project_bias[:, None, None]
-    speed = speed * fields[2][None]
-    velocity = speed[:, halo : halo + row_count, halo : halo + tile_cols]
+    speed = speed * fields[2][None, 1:-1, 1:-1]
+    velocity = speed[:, speed_halo : speed_halo + row_count, speed_halo : speed_halo + tile_cols]
 
     level = fields[0]
-    band = fields[1]
+    band = fields[1][1:-1, 1:-1]
+    speed_rows, speed_cols = band.shape
     for level_step in range(LS_STEPS):
-        inner = level_step + 1
-        rows_end = win_rows - inner
-        cols_end = tile_cols + 2 * halo - inner
+        rows_end = speed_rows - level_step
+        cols_end = speed_cols - level_step
         level = advance(
             level,
-            speed[0, inner:rows_end, inner:cols_end],
-            speed[1, inner:rows_end, inner:cols_end],
-            band[inner:rows_end, inner:cols_end],
+            speed[0, level_step:rows_end, level_step:cols_end],
+            speed[1, level_step:rows_end, level_step:cols_end],
+            band[level_step:rows_end, level_step:cols_end],
         )
     return (velocity, level)
 

time: 148 us -> 151 us (1.020)
  other arithmetic: 17.2 us -> 19.1 us
    reshape x0 -> x4, local copies, waits for them, and re-layouts: none -> 1.99 us  [the longest x2 1.4 us: packed(): return (jnp.concatenate([a.reshape(-1), b.reshape(-1)]), a.shape, b.shape)]
    unnamed x41 -> x36, local copies, waits for them, and re-layouts: 12.4 us -> 11.2 us
  transfers between devices with their start and end apart: 9 -> 9, of which waited for: 6 -> 5; matrix products, arithmetic and copies ran while one was open for 18% -> 19% of each run, Pallas kernels for 0% -> 0%
where the time goes in v7:
time: 151 us; the launch traced here: 150 us
  starting transfers between devices  49 us (32%)
  waiting for transfers between devices  38.3 us (25%)
  local copies, waits for them, and re-layouts  35.4 us (23%)
  other arithmetic  19.1 us (13%)
  matrix products  6.62 us (4%)
    all_to_all x1, starting transfers between devices, on_device(): lax.all_to_all(spec_y, 'rows', split_axis=2, concat_axis=3, tiled=True)  19.6 us
    all_to_all x1, waiting for transfers between devices, on_device(): lax.all_to_all(spec_y, 'rows', split_axis=2, concat_axis=3, tiled=True)  18.5 us
    unnamed x36, local copies, waits for them, and re-layouts  11.2 us
    all_to_all x1, waiting for transfers between devices, on_device(): lax.all_to_all(flat, 'chan', split_axis=0, concat_axis=0, tiled=True)  10.2 us
    all_to_all x1, starting transfers between devices, on_device(): lax.all_to_all(inverted, 'rows', split_axis=3, concat_axis=2, tiled=True)  6.94 us
    all_to_all x1, waiting for transfers between devices, on_device(): lax.all_to_all(inverted, 'rows', split_axis=3, concat_axis=2, tiled=True)  5.57 us
    all_to_all x1, starting transfers between devices, on_device(): lax.all_to_all(jnp.stack([real_out, imag_out], axis=2), 'chan', split_axi...  5.42 us
    all_to_all x1, starting transfers between devices, on_device(): lax.all_to_all(spectra, 'chan', split_axis=3, concat_axis=0, tiled=True)  4.22 us
  transfers between devices with their start and end apart: 9, of which 5 were waited for; matrix products, arithmetic and copies ran while one was open for 19% of the time, Pallas kernels for 0%

profile of v7, /device:TPU:1, one launch (start us, length us, event | category | flops | bytes accessed | tf_op | source)
XLA Modules:
  0.0 149.7 jit_solution(1046751023349098410)
XLA Ops:
  0.6 4.1 %sine_negate_fusion = (f32[128,2048]{1,0:T(8,128)S(1)}, f32[128,2048]{1,0:T(8,128)S(1)}) fusion(), kind=kLoop, calls=%fused_computation.37 | loop fusion | flops 3932160 | bytes 2097152 | tf_op jit(solution)/shard_map/neg | solution.py:36
  4.8 1.2 fusion.17
  7.1 2.2 %reshape.148 = f32[64,1,512]{2,1,0:T(1,128)} reshape(f32[128,4,2,32]{3,2,1,0:T(2,128)} %bitcast.185) | data formatting | bytes 262144
  9.3 19.6 %all-to-all-start = ((f32[64,1,512]{2,1,0:T(1,128)}), f32[64,1,512]{2,1,0:T(1,128)S(1)}, u32[]{:S(2)}, u32[]{:S(2)}) async-start(f32[64,1,512]{2,1,0:T(1,128)} %reshape.148), calls=%async_computation | async-start | bytes 262144 | tf_op jit(solution)/shard_map/all_to_all | solution.py:156
  29.0 18.5 %all-to-all-done = f32[64,1,512]{2,1,0:T(1,128)S(1)} async-done(((f32[64,1,512]{2,1,0:T(1,128)}), f32[64,1,512]{2,1,0:T(1,128)S(1)}, u32[]{:S(2)}, u32[]{:S(2)}) %all-to-all-start) | async-done | bytes 131104 | tf_op jit(solution)/shard_map/all_to_all | solution.py:156
  49.0 1.2 reshape.149
  50.3 1.1 copy.43
  52.3 1.3 all_to_all.56
  56.3 4.2 %all-to-all-start.1 = ((f32[8,1,256]{2,1,0:T(1,128)}), f32[8,1,256]{2,1,0:T(1,128)S(1)}, u32[]{:S(2)}, u32[]{:S(2)}) async-start(f32[8,1,256]{2,1,0:T(1,128)} %reshape.150), calls=%async_computation.1 | async-start | bytes 16384 | tf_op jit(solution)/shard_map/all_to_all | solution.py:172
  61.3 1.5 %pad_maximum_fusion.10 = f32[27648]{0:T(1024)} fusion(f32[3072]{0:T(1024)S(1)} %bitcast.198, f32[24576]{0:T(1024)} %reshape.128), kind=kLoop, calls=%fused_computation.63 | loop fusion | flops 27648 | bytes 221184 | tf_op jit(solution)/shard_map/concatenate | solution.py:91
  63.6 2.6 %collective-permute-start.1 = (f32[27648]{0:T(1024)}, f32[27648]{0:T(1024)}, u32[]{:S(2)}, u32[]{:S(2)}) collective-permute-start(f32[27648]{0:T(1024)} %pad_maximum_fusion.10), channel_id=1, source_target_pairs={{8,0},{16,8},{24,16},{32,24},{40,32},{48,40},{56,48},{64,56},{72,6... | collective-permute-start | bytes 331784 | tf_op jit(solution)/shard_map/ppermute | solution.py:100
  69.1 1.7 %fusion.28 = (f32[2,16,32]{2,1,0:T(8,128)S(1)}, f32[2,16,32]{2,1,0:T(8,128)S(1)}, f32[2,16,32]{2,1,0:T(8,128)S(1)}, f32[2,16,32]{2,1,0:T(8,128)S(1)}) fusion(f32[2,2,16,32,32]{4,3,2,1,0:T(8,128)} %param.11, f32[2,16,32]{2,1,0:T(8,128)S(1)} %copy.92, f32[2,16,32]{2,1,0:T(8,128)S(1)} %copy.91), kind=kLoop, calls=%fused_computation.48 | loop fusion | flops 258048 | bytes 286720
  72.0 5.4 %all-to-all-start.2 = ((f32[8,1,256]{2,1,0:T(1,128)}), f32[8,1,256]{2,1,0:T(1,128)S(1)}, u32[]{:S(2)}, u32[]{:S(2)}) async-start(f32[8,1,256]{2,1,0:T(1,128)} %reshape.152), calls=%async_computation.2 | async-start | bytes 16384 | tf_op jit(solution)/shard_map/all_to_all | solution.py:181
  78.1 3.1 %collective-permute-start = (f32[27648]{0:T(1024)}, f32[27648]{0:T(1024)}, u32[]{:S(2)}, u32[]{:S(2)}) collective-permute-start(f32[27648]{0:T(1024)} %pad_maximum_fusion.9), channel_id=1, source_target_pairs={{0,8},{8,16},{16,24},{24,32},{32,40},{40,48},{48,56},{56,64},{64,7... | collective-permute-start | bytes 331784 | tf_op jit(solution)/shard_map/ppermute | solution.py:99
  81.3 1.2 all-to-all-done.2
  85.6 2.0 %reshape.124 = f32[4,2,2,64,32]{4,3,2,1,0:T(8,128)} reshape(f32[4,2,2,2048]{3,2,1,0:T(2,128)} %copy.55) | data formatting | bytes 262144 | tf_op jit(solution)/shard_map/reshape | solution.py:53
  87.5 1.0 reshape.123
  88.6 1.4 pad_maximum_fusion.6
  90.0 1.2 copy.98
  91.2 2.7 %reshape.154 = f32[64,1,608]{2,1,0:T(1,128)} reshape(f32[64,4,2,2,38]{4,3,2,1,0:T(2,128)} %bitcast.188) | data formatting | bytes 311296
  93.9 6.9 %all-to-all-start.3 = ((f32[64,1,608]{2,1,0:T(1,128)}), f32[64,1,608]{2,1,0:T(1,128)}, u32[]{:S(2)}, u32[]{:S(2)}) async-start(f32[64,1,608]{2,1,0:T(1,128)} %reshape.154), calls=%async_computation.3 | async-start | bytes 327680 | tf_op jit(solution)/shard_map/all_to_all | solution.py:197
  103.9 1.5 %slice.348 = f32[24576]{0:T(1024)} slice(f32[27648]{0:T(1024)} %collective-permute-done), slice={[0:24576]} | slice | bytes 196608 | tf_op jit(solution)/shard_map/slice | solution.py:95
  107.3 2.2 %collective-permute-start.2 = (f32[3,40,4]{2,1,0:T(8,128)S(1)}, f32[3,40,4]{2,1,0:T(8,128)S(1)}, u32[]{:S(2)}, u32[]{:S(2)}) collective-permute-start(f32[3,40,4]{2,1,0:T(8,128)S(1)} %get-tuple-element.27), channel_id=1, source_target_pairs={{0,1},{1,2},{2,3},{3,4},{4,5},{5,6},{6,7},{8,9},{9,10},{10,11},{11... | collective-permute-start | bytes 5768 | tf_op jit(solution)/shard_map/ppermute | solution.py:21
  109.5 1.3 collective-permute-start.3
  110.8 1.2 pad_maximum_fusion.1
  112.1 2.8 %collective-permute-done.3 = f32[3,40,4]{2,1,0:T(8,128)S(1)} collective-permute-done((f32[3,40,4]{2,1,0:T(8,128)S(1)}, f32[3,40,4]{2,1,0:T(8,128)S(1)}, u32[]{:S(2)}, u32[]{:S(2)}) %collective-permute-start.3) | collective-permute-done | bytes 1952 | tf_op jit(solution)/shard_map/ppermute | solution.py:24
  115.0 5.6 %all-to-all-done.3 = f32[64,1,608]{2,1,0:T(1,128)} async-done(((f32[64,1,608]{2,1,0:T(1,128)}), f32[64,1,608]{2,1,0:T(1,128)}, u32[]{:S(2)}, u32[]{:S(2)}) %all-to-all-start.3) | async-done | bytes 155680 | tf_op jit(solution)/shard_map/all_to_all | solution.py:197
  120.6 1.9 %reduce.11 = f32[64,608]{1,0:T(8,128)S(1)} reduce(f32[64,1,608]{2,1,0:T(1,128)} %all-to-all-done.3, f32[]{:T(128)} %broadcast.135), dimensions={1}, to_apply=%all_to_all.65.reduce_sub_computation | reduce | bytes 311300 | tf_op jit(solution)/shard_map/all_to_all | solution.py:197
  124.8 3.8 %fusion.9 = f32[4,38,2048]{2,1,0:T(8,128)S(1)} fusion(f32[4]{0:T(128)S(1)} %copy-done.9, f32[4,38,2048]{2,1,0:T(8,128)S(1)} %copy-done.1, f32[128,2048]{1,0:T(8,128)S(1)} %get-tuple-element.46, f32[128,2048]{1,0:T(8,128)S(1)} %get-tuple-element.47, f32[4]{0:T(128)S(1)} %copy-done.10, f32[4,256,38]{2,1,0:T(8,128)S(1)} %bitcast.191, ...), kind=kOutput, calls=%fused_computation.16 | convolution fusion | flops 499570688 | bytes 4744224 | tf_op jit(solution)/shard_map/ckx,ky->cxy/dot_general | solution.py:202
  129.5 1.6 %multiply_reduce_fusion = f32[2,38,2048]{2,1,0:T(8,128)S(1)} fusion(f32[4,38,2048]{2,0,1:T(4,128)S(1)} %copy.59, f32[2,4]{1,0:T(2,128)S(1)} %copy-done.6), kind=kLoop, calls=%fused_computation.2 | loop fusion | flops 1089536 | bytes 1867808 | tf_op jit(solution)/shard_map/reduce_sum | solution.py:207
  133.4 3.7 %all-to-all-start.4 = ((f32[8,156,128]{2,1,0:T(8,128)}), f32[8,156,128]{2,1,0:T(8,128)S(1)}, u32[]{:S(2)}, u32[]{:S(2)}) async-start(f32[8,156,128]{2,1,0:T(8,128)} %copy.61), calls=%async_computation.4 | async-start | bytes 1310720 | tf_op jit(solution)/shard_map/all_to_all | solution.py:216
  137.2 10.2 %all-to-all-done.4 = f32[8,156,128]{2,1,0:T(8,128)S(1)} async-done(((f32[8,156,128]{2,1,0:T(8,128)}), f32[8,156,128]{2,1,0:T(8,128)S(1)}, u32[]{:S(2)}, u32[]{:S(2)}) %all-to-all-start.4) | async-done | bytes 639008 | tf_op jit(solution)/shard_map/all_to_all | solution.py:216
  (118 shorter events, 28.2 us)
Async XLA Ops:
  0.6 4.1 %copy-start = (f32[4,32,2048]{2,1,0:T(8,128)S(1)}, f32[4,32,2048]{2,1,0:T(8,128)}, u32[]{:S(2)}) copy-start(f32[4,32,2048]{2,1,0:T(8,128)} %param.9) | copy-start | bytes 3145732
  5.9 23.0 %copy-start.3 = (s32[32,256]{1,0:T(8,128)S(1)}, s32[32,256]{1,0:T(8,128)}, u32[]{:S(2)}) copy-start(s32[32,256]{1,0:T(8,128)} %param.16) | copy-start | bytes 98308
  5.9 23.0 %copy-start.4 = (s32[32,256]{1,0:T(8,128)S(1)}, s32[32,256]{1,0:T(8,128)}, u32[]{:S(2)}) copy-start(s32[32,256]{1,0:T(8,128)} %param.17) | copy-start | bytes 98308
  6.0 23.0 %copy-start.5 = (f32[32,256]{1,0:T(8,128)S(1)}, f32[32,256]{1,0:T(8,128)}, u32[]{:S(2)}) copy-start(f32[32,256]{1,0:T(8,128)} %param.10) | copy-start | bytes 98308
  9.3 38.2 %all-to-all-start = ((f32[64,1,512]{2,1,0:T(1,128)}), f32[64,1,512]{2,1,0:T(1,128)S(1)}, u32[]{:S(2)}, u32[]{:S(2)}) async-start(f32[64,1,512]{2,1,0:T(1,128)} %reshape.148), calls=%async_computation | async-start | bytes 262144 | tf_op jit(solution)/shard_map/all_to_all | solution.py:156
  56.3 9.8 %all-to-all-start.1 = ((f32[8,1,256]{2,1,0:T(1,128)}), f32[8,1,256]{2,1,0:T(1,128)S(1)}, u32[]{:S(2)}, u32[]{:S(2)}) async-start(f32[8,1,256]{2,1,0:T(1,128)} %reshape.150), calls=%async_computation.1 | async-start | bytes 16384 | tf_op jit(solution)/shard_map/all_to_all | solution.py:172
  63.6 37.3 %collective-permute-start.1 = (f32[27648]{0:T(1024)}, f32[27648]{0:T(1024)}, u32[]{:S(2)}, u32[]{:S(2)}) collective-permute-start(f32[27648]{0:T(1024)} %pad_maximum_fusion.10), channel_id=1, source_target_pairs={{8,0},{16,8},{24,16},{32,24},{40,32},{48,40},{56,48},{64,56},{72,6... | collective-permute-start | bytes 331784 | tf_op jit(solution)/shard_map/ppermute | solution.py:100
  68.2 9.3 %copy-start.2 = (f32[24576]{0:T(1024)S(1)}, f32[24576]{0:T(1024)}, u32[]{:S(2)}) copy-start(f32[24576]{0:T(1024)} %reshape.126) | copy-start | bytes 294916
  69.0 14.8 %copy-start.8 = (pred[65]{0:T(512)(128)(4,1)S(1)}, pred[65]{0:T(512)(128)(4,1)}, u32[]{:S(2)}) copy-start(pred[65]{0:T(512)(128)(4,1)} %constant.37.clone.1) | copy-start | bytes 199
  72.0 10.5 %all-to-all-start.2 = ((f32[8,1,256]{2,1,0:T(1,128)}), f32[8,1,256]{2,1,0:T(1,128)S(1)}, u32[]{:S(2)}, u32[]{:S(2)}) async-start(f32[8,1,256]{2,1,0:T(1,128)} %reshape.152), calls=%async_computation.2 | async-start | bytes 16384 | tf_op jit(solution)/shard_map/all_to_all | solution.py:181
  78.1 23.4 %collective-permute-start = (f32[27648]{0:T(1024)}, f32[27648]{0:T(1024)}, u32[]{:S(2)}, u32[]{:S(2)}) collective-permute-start(f32[27648]{0:T(1024)} %pad_maximum_fusion.9), channel_id=1, source_target_pairs={{0,8},{8,16},{16,24},{24,32},{32,40},{40,48},{48,56},{56,64},{64,7... | collective-permute-start | bytes 331784 | tf_op jit(solution)/shard_map/ppermute | solution.py:99
  93.9 26.7 %all-to-all-start.3 = ((f32[64,1,608]{2,1,0:T(1,128)}), f32[64,1,608]{2,1,0:T(1,128)}, u32[]{:S(2)}, u32[]{:S(2)}) async-start(f32[64,1,608]{2,1,0:T(1,128)} %reshape.154), calls=%async_computation.3 | async-start | bytes 327680 | tf_op jit(solution)/shard_map/all_to_all | solution.py:197
  107.3 4.7 %collective-permute-start.2 = (f32[3,40,4]{2,1,0:T(8,128)S(1)}, f32[3,40,4]{2,1,0:T(8,128)S(1)}, u32[]{:S(2)}, u32[]{:S(2)}) collective-permute-start(f32[3,40,4]{2,1,0:T(8,128)S(1)} %get-tuple-element.27), channel_id=1, source_target_pairs={{0,1},{1,2},{2,3},{3,4},{4,5},{5,6},{6,7},{8,9},{9,10},{10,11},{11... | collective-permute-start | bytes 5768 | tf_op jit(solution)/shard_map/ppermute | solution.py:21
  109.5 5.4 %collective-permute-start.3 = (f32[3,40,4]{2,1,0:T(8,128)S(1)}, f32[3,40,4]{2,1,0:T(8,128)S(1)}, u32[]{:S(2)}, u32[]{:S(2)}) collective-permute-start(f32[3,40,4]{2,1,0:T(8,128)S(1)} %get-tuple-element.28), channel_id=1, source_target_pairs={{1,0},{2,1},{3,2},{4,3},{5,4},{6,5},{7,6},{9,8},{10,9},{11,10},{12... | collective-permute-start | bytes 5768 | tf_op jit(solution)/shard_map/ppermute | solution.py:24
  122.6 1.4 copy-start.9
  122.6 1.4 copy-start.10
  123.5 1.3 copy-start.1
  128.7 0.8 copy-start.6
  133.4 14.2 %copy-start.7 = (f32[2]{0:T(128)S(1)}, f32[2]{0:T(128)}, u32[]{:S(2)}) copy-start(f32[2]{0:T(128)} %param.15) | copy-start | bytes 28
  133.4 14.0 %all-to-all-start.4 = ((f32[8,156,128]{2,1,0:T(8,128)}), f32[8,156,128]{2,1,0:T(8,128)S(1)}, u32[]{:S(2)}, u32[]{:S(2)}) async-start(f32[8,156,128]{2,1,0:T(8,128)} %copy.61), calls=%async_computation.4 | async-start | bytes 1310720 | tf_op jit(solution)/shard_map/all_to_all | solution.py:216

commit v8 on v6

--- a/solution.py
+++ b/solution.py
@@ -32,8 +32,15 @@
 
 
 def base_table(modes, length):
-    phase = angles(jnp.arange(modes, dtype=jnp.int32), jnp.arange(length, dtype=jnp.int32), length)
-    return jnp.concatenate([jnp.cos(phase), -jnp.sin(phase)])
+    lanes = 128 if length % 128 == 0 else length
+    ids = jnp.arange(modes, dtype=jnp.int32)
+    coarse = angles(ids, jnp.arange(length // lanes, dtype=jnp.int32) * lanes, length)
+    fine = angles(ids, jnp.arange(lanes, dtype=jnp.int32), length)
+    cos_hi, sin_hi = jnp.cos(coarse)[:, :, None], jnp.sin(coarse)[:, :, None]
+    cos_lo, sin_lo = jnp.cos(fine)[:, None, :], jnp.sin(fine)[:, None, :]
+    cos_all = (cos_hi * cos_lo - sin_hi * sin_lo).reshape(modes, length)
+    sin_all = (sin_hi * cos_lo + cos_hi * sin_lo).reshape(modes, length)
+    return jnp.concatenate([cos_all, -sin_all])
 
 
 def fold_modes(vec, half):

time: 148 us -> 146 us (0.986)
  other arithmetic: 17.2 us -> 13.8 us
  local copies, waits for them, and re-layouts: 34.2 us -> 35.8 us
    neg x1, other arithmetic: 4.1 us -> 0.61 us  [base_table(): return jnp.concatenate([cos_all, -sin_all])]
    unnamed x41 -> x42, local copies, waits for them, and re-layouts: 12.4 us -> 13.6 us
  transfers between devices with their start and end apart: 9 -> 9, of which waited for: 6 -> 6; matrix products, arithmetic and copies ran while one was open for 18% -> 19% of each run, Pallas kernels for 0% -> 0%
where the time goes in v8:
time: 146 us; the launch traced here: 145 us
  starting transfers between devices  48.2 us (33%)
  waiting for transfers between devices  39.6 us (27%)
  local copies, waits for them, and re-layouts  35.8 us (25%)
  other arithmetic  13.8 us (9%)
  matrix products  6.62 us (5%)
    all_to_all x1, starting transfers between devices, on_device(): lax.all_to_all(spec_y, 'rows', split_axis=2, concat_axis=3, tiled=True)  19.6 us
    all_to_all x1, waiting for transfers between devices, on_device(): lax.all_to_all(spec_y, 'rows', split_axis=2, concat_axis=3, tiled=True)  18.5 us
    unnamed x42, local copies, waits for them, and re-layouts  13.6 us
    all_to_all x1, waiting for transfers between devices, on_device(): lax.all_to_all(flat, 'chan', split_axis=0, concat_axis=0, tiled=True)  10.7 us
    all_to_all x1, starting transfers between devices, on_device(): lax.all_to_all(inverted, 'rows', split_axis=3, concat_axis=2, tiled=True)  6.95 us
    all_to_all x1, waiting for transfers between devices, on_device(): lax.all_to_all(inverted, 'rows', split_axis=3, concat_axis=2, tiled=True)  5.51 us
    all_to_all x1, starting transfers between devices, on_device(): lax.all_to_all(jnp.stack([real_out, imag_out], axis=2), 'chan', split_axi...  4.37 us
    all_to_all x1, starting transfers between devices, on_device(): lax.all_to_all(spectra, 'chan', split_axis=3, concat_axis=0, tiled=True)  4.22 us
  transfers between devices with their start and end apart: 9, of which 6 were waited for; matrix products, arithmetic and copies ran while one was open for 19% of the time, Pallas kernels for 0%

profile of v8, /device:TPU:1, one launch (start us, length us, event | category | flops | bytes accessed | tf_op | source)
XLA Modules:
  0.0 145.3 jit_solution(16249334630822035622)
XLA Ops:
  3.4 1.2 fusion.17
  4.7 1.0 copy.92
  5.7 2.2 %reshape.243 = f32[64,1,512]{2,1,0:T(1,128)} reshape(f32[128,4,2,32]{3,2,1,0:T(2,128)} %bitcast.208) | data formatting | bytes 262144
  8.0 19.6 %all-to-all-start = ((f32[64,1,512]{2,1,0:T(1,128)}), f32[64,1,512]{2,1,0:T(1,128)S(1)}, u32[]{:S(2)}, u32[]{:S(2)}) async-start(f32[64,1,512]{2,1,0:T(1,128)} %reshape.243), calls=%async_computation | async-start | bytes 262144 | tf_op jit(solution)/shard_map/all_to_all | solution.py:162
  27.6 18.5 %all-to-all-done = f32[64,1,512]{2,1,0:T(1,128)S(1)} async-done(((f32[64,1,512]{2,1,0:T(1,128)}), f32[64,1,512]{2,1,0:T(1,128)S(1)}, u32[]{:S(2)}, u32[]{:S(2)}) %all-to-all-start) | async-done | bytes 131104 | tf_op jit(solution)/shard_map/all_to_all | solution.py:162
  47.6 1.2 reshape.244
  48.9 1.1 copy.93
  50.9 1.3 all_to_all.56
  52.2 1.0 fusion.3
  55.0 4.2 %all-to-all-start.1 = ((f32[8,1,256]{2,1,0:T(1,128)}), f32[8,1,256]{2,1,0:T(1,128)S(1)}, u32[]{:S(2)}, u32[]{:S(2)}) async-start(f32[8,1,256]{2,1,0:T(1,128)} %reshape.245), calls=%async_computation.1 | async-start | bytes 16384 | tf_op jit(solution)/shard_map/all_to_all | solution.py:178
  60.6 2.6 %collective-permute-start.1 = (f32[35840]{0:T(1024)}, f32[35840]{0:T(1024)}, u32[]{:S(2)}, u32[]{:S(2)}) collective-permute-start(f32[35840]{0:T(1024)} %pad_maximum_fusion.4), channel_id=1, source_target_pairs={{8,0},{16,8},{24,16},{32,24},{40,32},{48,40},{56,48},{64,56},{72,6... | collective-permute-start | bytes 430088 | tf_op jit(solution)/shard_map/ppermute | solution.py:107
  63.1 1.1 all-to-all-done.1
  67.2 1.7 %fusion.22 = (f32[2,16,32]{2,1,0:T(8,128)S(1)}, f32[2,16,32]{2,1,0:T(8,128)S(1)}, f32[2,16,32]{2,1,0:T(8,128)S(1)}, f32[2,16,32]{2,1,0:T(8,128)S(1)}) fusion(f32[2,2,16,32,32]{4,3,2,1,0:T(8,128)} %param.11, f32[2,16,32]{2,1,0:T(8,128)S(1)} %copy.140, f32[2,16,32]{2,1,0:T(8,128)S(1)} %copy.139), kind=kLoop, calls=%fused_computation.40 | loop fusion | flops 258048 | bytes 286720
  70.1 4.4 %all-to-all-start.2 = ((f32[8,1,256]{2,1,0:T(1,128)}), f32[8,1,256]{2,1,0:T(1,128)S(1)}, u32[]{:S(2)}, u32[]{:S(2)}) async-start(f32[8,1,256]{2,1,0:T(1,128)} %reshape.247), calls=%async_computation.2 | async-start | bytes 16384 | tf_op jit(solution)/shard_map/all_to_all | solution.py:187
  75.2 3.4 %collective-permute-start = (f32[35840]{0:T(1024)}, f32[35840]{0:T(1024)}, u32[]{:S(2)}, u32[]{:S(2)}) collective-permute-start(f32[35840]{0:T(1024)} %pad_maximum_fusion.3), channel_id=1, source_target_pairs={{0,8},{8,16},{16,24},{24,32},{32,40},{40,48},{48,56},{56,64},{64,7... | collective-permute-start | bytes 430088 | tf_op jit(solution)/shard_map/ppermute | solution.py:106
  82.6 1.9 %reshape.222 = f32[4,2,2,64,32]{4,3,2,1,0:T(8,128)} reshape(f32[4,2,2,2048]{3,2,1,0:T(2,128)} %copy.105) | data formatting | bytes 262144 | tf_op jit(solution)/shard_map/reshape | solution.py:60
  84.5 1.0 reshape.221
  85.5 1.4 pad_maximum_fusion.1
  86.9 1.2 copy.154
  88.1 2.7 %reshape.249 = f32[64,1,640]{2,1,0:T(1,128)} reshape(f32[64,4,2,2,40]{4,3,2,1,0:T(2,128)} %bitcast.211) | data formatting | bytes 327680
  90.8 7.0 %all-to-all-start.3 = ((f32[64,1,640]{2,1,0:T(1,128)}), f32[64,1,640]{2,1,0:T(1,128)}, u32[]{:S(2)}, u32[]{:S(2)}) async-start(f32[64,1,640]{2,1,0:T(1,128)} %reshape.249), calls=%async_computation.3 | async-start | bytes 327680 | tf_op jit(solution)/shard_map/all_to_all | solution.py:203
  100.9 1.6 %slice.337 = f32[32768]{0:T(1024)} slice(f32[35840]{0:T(1024)} %collective-permute-done), slice={[0:32768]} | slice | bytes 262144 | tf_op jit(solution)/shard_map/slice | solution.py:102
  104.3 2.2 %collective-permute-start.2 = (f32[3,40,4]{2,1,0:T(8,128)S(1)}, f32[3,40,4]{2,1,0:T(8,128)S(1)}, u32[]{:S(2)}, u32[]{:S(2)}) collective-permute-start(f32[3,40,4]{2,1,0:T(8,128)S(1)} %get-tuple-element.29), channel_id=1, source_target_pairs={{0,1},{1,2},{2,3},{3,4},{4,5},{5,6},{6,7},{8,9},{9,10},{10,11},{11... | collective-permute-start | bytes 5768 | tf_op jit(solution)/shard_map/ppermute | solution.py:21
  106.5 1.3 collective-permute-start.3
  107.8 1.3 pad_maximum_fusion
  109.1 2.8 %collective-permute-done.3 = f32[3,40,4]{2,1,0:T(8,128)S(1)} collective-permute-done((f32[3,40,4]{2,1,0:T(8,128)S(1)}, f32[3,40,4]{2,1,0:T(8,128)S(1)}, u32[]{:S(2)}, u32[]{:S(2)}) %collective-permute-start.3) | collective-permute-done | bytes 1952 | tf_op jit(solution)/shard_map/ppermute | solution.py:24
  112.0 5.5 %all-to-all-done.3 = f32[64,1,640]{2,1,0:T(1,128)} async-done(((f32[64,1,640]{2,1,0:T(1,128)}), f32[64,1,640]{2,1,0:T(1,128)}, u32[]{:S(2)}, u32[]{:S(2)}) %all-to-all-start.3) | async-done | bytes 163872 | tf_op jit(solution)/shard_map/all_to_all | solution.py:203
  117.6 1.9 %reduce.11 = f32[64,640]{1,0:T(8,128)S(1)} reduce(f32[64,1,640]{2,1,0:T(1,128)} %all-to-all-done.3, f32[]{:T(128)} %broadcast.268), dimensions={1}, to_apply=%all_to_all.65.reduce_sub_computation | reduce | bytes 327684 | tf_op jit(solution)/shard_map/all_to_all | solution.py:203
  121.8 3.8 %fusion.9 = f32[4,40,2048]{2,1,0:T(8,128)S(1)} fusion(f32[4,40,2048]{2,1,0:T(8,128)S(1)} %copy-done.1, f32[256,2048]{1,0:T(8,128)S(1)} %bitcast_dynamic-update-slice_fusion, f32[4]{0:T(128)S(1)} %copy-done.9, f32[4]{0:T(128)S(1)} %copy-done.10, f32[4,256,40]{2,1,0:T(8,128)S(1)} %bitcast.215, f32[256]{0:T(256)S(1)} %broadcast_bitcast_fusion), kind=kOutput, calls=%fused_computation.12 | convolution fusion | flops 525312000 | bytes 4883488 | tf_op jit(solution)/shard_map/ckx,ky->cxy/dot_general | solution.py:208
  127.0 1.6 %reshape.232 = f32[8,165,128]{2,1,0:T(8,128)} reshape(f32[8,2,40,264]{3,2,1,0:T(8,128)S(1)} %copy.109) | data formatting | bytes 1351680 | tf_op jit(solution)/shard_map/reshape | solution.py:221
  128.6 3.7 %all-to-all-start.4 = ((f32[8,165,128]{2,1,0:T(8,128)}), f32[8,165,128]{2,1,0:T(8,128)S(1)}, u32[]{:S(2)}, u32[]{:S(2)}) async-start(f32[8,165,128]{2,1,0:T(8,128)} %reshape.232), calls=%async_computation.4 | async-start | bytes 1376256 | tf_op jit(solution)/shard_map/all_to_all | solution.py:222
  132.3 10.7 %all-to-all-done.4 = f32[8,165,128]{2,1,0:T(8,128)S(1)} async-done(((f32[8,165,128]{2,1,0:T(8,128)}), f32[8,165,128]{2,1,0:T(8,128)S(1)}, u32[]{:S(2)}, u32[]{:S(2)}) %all-to-all-start.4) | async-done | bytes 675872 | tf_op jit(solution)/shard_map/all_to_all | solution.py:222
  (121 shorter events, 28.1 us)
Async XLA Ops:
  2.2 1.2 copy-start
  4.6 23.0 %copy-start.3 = (s32[32,256]{1,0:T(8,128)S(1)}, s32[32,256]{1,0:T(8,128)}, u32[]{:S(2)}) copy-start(s32[32,256]{1,0:T(8,128)} %param.16) | copy-start | bytes 98308
  4.6 23.0 %copy-start.4 = (s32[32,256]{1,0:T(8,128)S(1)}, s32[32,256]{1,0:T(8,128)}, u32[]{:S(2)}) copy-start(s32[32,256]{1,0:T(8,128)} %param.17) | copy-start | bytes 98308
  4.6 23.0 %copy-start.5 = (f32[32,256]{1,0:T(8,128)S(1)}, f32[32,256]{1,0:T(8,128)}, u32[]{:S(2)}) copy-start(f32[32,256]{1,0:T(8,128)} %param.10) | copy-start | bytes 98308
  8.0 38.2 %all-to-all-start = ((f32[64,1,512]{2,1,0:T(1,128)}), f32[64,1,512]{2,1,0:T(1,128)S(1)}, u32[]{:S(2)}, u32[]{:S(2)}) async-start(f32[64,1,512]{2,1,0:T(1,128)} %reshape.243), calls=%async_computation | async-start | bytes 262144 | tf_op jit(solution)/shard_map/all_to_all | solution.py:162
  55.0 9.3 %all-to-all-start.1 = ((f32[8,1,256]{2,1,0:T(1,128)}), f32[8,1,256]{2,1,0:T(1,128)S(1)}, u32[]{:S(2)}, u32[]{:S(2)}) async-start(f32[8,1,256]{2,1,0:T(1,128)} %reshape.245), calls=%async_computation.1 | async-start | bytes 16384 | tf_op jit(solution)/shard_map/all_to_all | solution.py:178
  60.6 37.2 %collective-permute-start.1 = (f32[35840]{0:T(1024)}, f32[35840]{0:T(1024)}, u32[]{:S(2)}, u32[]{:S(2)}) collective-permute-start(f32[35840]{0:T(1024)} %pad_maximum_fusion.4), channel_id=1, source_target_pairs={{8,0},{16,8},{24,16},{32,24},{40,32},{48,40},{56,48},{64,56},{72,6... | collective-permute-start | bytes 430088 | tf_op jit(solution)/shard_map/ppermute | solution.py:107
  66.2 8.3 %copy-start.2 = (f32[4,16,4,128]{3,1,2,0:T(8,128)S(1)}, f32[4,16,4,128]{3,1,2,0:T(8,128)}, u32[]{:S(2)}) copy-start(f32[4,16,4,128]{3,1,2,0:T(8,128)} %copy.145) | copy-start | bytes 393220
  67.0 13.7 %copy-start.8 = (pred[65]{0:T(512)(128)(4,1)S(1)}, pred[65]{0:T(512)(128)(4,1)}, u32[]{:S(2)}) copy-start(pred[65]{0:T(512)(128)(4,1)} %constant.38.clone.1) | copy-start | bytes 199
  70.1 9.4 %all-to-all-start.2 = ((f32[8,1,256]{2,1,0:T(1,128)}), f32[8,1,256]{2,1,0:T(1,128)S(1)}, u32[]{:S(2)}, u32[]{:S(2)}) async-start(f32[8,1,256]{2,1,0:T(1,128)} %reshape.247), calls=%async_computation.2 | async-start | bytes 16384 | tf_op jit(solution)/shard_map/all_to_all | solution.py:187
  75.2 23.4 %collective-permute-start = (f32[35840]{0:T(1024)}, f32[35840]{0:T(1024)}, u32[]{:S(2)}, u32[]{:S(2)}) collective-permute-start(f32[35840]{0:T(1024)} %pad_maximum_fusion.3), channel_id=1, source_target_pairs={{0,8},{8,16},{16,24},{24,32},{32,40},{40,48},{48,56},{56,64},{64,7... | collective-permute-start | bytes 430088 | tf_op jit(solution)/shard_map/ppermute | solution.py:106
  90.8 26.7 %all-to-all-start.3 = ((f32[64,1,640]{2,1,0:T(1,128)}), f32[64,1,640]{2,1,0:T(1,128)}, u32[]{:S(2)}, u32[]{:S(2)}) async-start(f32[64,1,640]{2,1,0:T(1,128)} %reshape.249), calls=%async_computation.3 | async-start | bytes 327680 | tf_op jit(solution)/shard_map/all_to_all | solution.py:203
  104.3 4.8 %collective-permute-start.2 = (f32[3,40,4]{2,1,0:T(8,128)S(1)}, f32[3,40,4]{2,1,0:T(8,128)S(1)}, u32[]{:S(2)}, u32[]{:S(2)}) collective-permute-start(f32[3,40,4]{2,1,0:T(8,128)S(1)} %get-tuple-element.29), channel_id=1, source_target_pairs={{0,1},{1,2},{2,3},{3,4},{4,5},{5,6},{6,7},{8,9},{9,10},{10,11},{11... | collective-permute-start | bytes 5768 | tf_op jit(solution)/shard_map/ppermute | solution.py:21
  106.5 5.4 %collective-permute-start.3 = (f32[3,40,4]{2,1,0:T(8,128)S(1)}, f32[3,40,4]{2,1,0:T(8,128)S(1)}, u32[]{:S(2)}, u32[]{:S(2)}) collective-permute-start(f32[3,40,4]{2,1,0:T(8,128)S(1)} %get-tuple-element.30), channel_id=1, source_target_pairs={{1,0},{2,1},{3,2},{4,3},{5,4},{6,5},{7,6},{9,8},{10,9},{11,10},{12... | collective-permute-start | bytes 5768 | tf_op jit(solution)/shard_map/ppermute | solution.py:24
  119.5 1.4 copy-start.9
  119.5 1.4 copy-start.10
  120.4 1.3 copy-start.1
  121.8 3.8 %copy-start.6 = (f32[2,4]{1,0:T(2,128)S(1)}, f32[2,4]{1,0:T(2,128)}, u32[]{:S(2)}) copy-start(f32[2,4]{1,0:T(2,128)} %param.14) | copy-start | bytes 100
  128.6 14.6 %copy-start.7 = (f32[2]{0:T(128)S(1)}, f32[2]{0:T(128)}, u32[]{:S(2)}) copy-start(f32[2]{0:T(128)} %param.15) | copy-start | bytes 28
  128.6 14.4 %all-to-all-start.4 = ((f32[8,165,128]{2,1,0:T(8,128)}), f32[8,165,128]{2,1,0:T(8,128)S(1)}, u32[]{:S(2)}, u32[]{:S(2)}) async-start(f32[8,165,128]{2,1,0:T(8,128)} %reshape.232), calls=%async_computation.4 | async-start | bytes 1376256 | tf_op jit(solution)/shard_map/all_to_all | solution.py:222

commit v9 on v8

--- a/solution.py
+++ b/solution.py
@@ -158,13 +158,14 @@
     x_modes = x_table.shape[0] // 2
 
     spec_y = jnp.einsum("cxy,ky->ckx", hidden, table, precision=high)
-    spec_y = spec_y.reshape(local_chan, 2, all_ymodes, row_count)
-    by_freq = lax.all_to_all(spec_y, "rows", split_axis=2, concat_axis=3, tiled=True)
+    spec_y = spec_y.reshape(local_chan, 2, row_devices, local_ymodes, row_count)
+    by_freq = lax.all_to_all(spec_y, "rows", split_axis=2, concat_axis=0, tiled=False)
     hidden_late, fields, by_freq = lax.optimization_barrier((hidden, fields, by_freq))
     hidden_win, fields = rows_halo_pair(hidden_late, fields, halo)
     fields = with_halo(fields, (("chan", 2),), halo)
     fields, hidden_win = lax.optimization_barrier((fields, hidden_win))
-    parts = jnp.einsum("caqx,kx->caqk", by_freq, x_table, precision=high)
+    blocked_table = x_table.reshape(x_table.shape[0], row_devices, row_count)
+    parts = jnp.einsum("scaqx,ksx->caqk", by_freq, blocked_table, precision=high)
     cos_part = parts[..., :x_modes]
     sin_part = parts[..., x_modes:]
     real_in = unfold_modes(

time: 146 us -> 149 us (1.021)
  waiting for transfers between devices: 39.6 us -> 32.2 us
  local copies, waits for them, and re-layouts: 35.8 us -> 41.5 us
  other arithmetic: 13.8 us -> 16.8 us
    sub x1 -> x2, other arithmetic: 0.01 us -> 3.82 us  [base_table(): cos_all = (cos_hi * cos_lo - sin_hi * sin_lo).reshape(modes, length)]
    all_to_all x4 -> x1, local copies, waits for them, and re-layouts: 3.9 us -> 0.48 us  [on_device(): lax.all_to_all(spec_y, 'rows', split_axis=2, concat_axis=0, tiled=False)]
    all_to_all x1, waiting for transfers between devices: 18.5 us -> 15.2 us  [on_device(): lax.all_to_all(spec_y, 'rows', split_axis=2, concat_axis=0, tiled=False)]
    all_to_all x1, waiting for transfers between devices: 5.51 us -> 2.84 us  [on_device(): lax.all_to_all(inverted, 'rows', split_axis=3, concat_axis=2, tiled=True)]
    reshape x2, local copies, waits for them, and re-layouts: 0.99 us -> 3.19 us  [unpacked(): return (flat[:split].reshape(a_shape), flat[split:].reshape(b_shape))]
    squeeze x0 -> x1, local copies, waits for them, and re-layouts: none -> 2.03 us  [on_device(): lax.all_to_all(spec_y, 'rows', split_axis=2, concat_axis=0, tiled=False)]
    another operation x0 -> x1, local copies, waits for them, and re-layouts: none -> 2.02 us  [on_device(): lax.all_to_all(spec_y, 'rows', split_axis=2, concat_axis=0, tiled=False)]
    neg x0 -> x1, local copies, waits for them, and re-layouts: none -> 1.64 us  [base_table(): return jnp.concatenate([cos_all, -sin_all])]
  transfers between devices with their start and end apart: 9 -> 9, of which waited for: 6 -> 6; matrix products, arithmetic and copies ran while one was open for 19% -> 23% of each run, Pallas kernels for 0% -> 0%
where the time goes in v9:
time: 149 us; the launch traced here: 148 us
  starting transfers between devices  48.1 us (32%)
  local copies, waits for them, and re-layouts  41.5 us (28%)
  waiting for transfers between devices  32.2 us (22%)
  other arithmetic  16.8 us (11%)
  matrix products  7.93 us (5%)
    all_to_all x1, starting transfers between devices, on_device(): lax.all_to_all(spec_y, 'rows', split_axis=2, concat_axis=0, tiled=False)  19.6 us
    all_to_all x1, waiting for transfers between devices, on_device(): lax.all_to_all(spec_y, 'rows', split_axis=2, concat_axis=0, tiled=False)  15.2 us
    unnamed x43, local copies, waits for them, and re-layouts  12.4 us
    all_to_all x1, waiting for transfers between devices, on_device(): lax.all_to_all(flat, 'chan', split_axis=0, concat_axis=0, tiled=True)  10.3 us
    all_to_all x1, starting transfers between devices, on_device(): lax.all_to_all(inverted, 'rows', split_axis=3, concat_axis=2, tiled=True)  6.79 us
    slice x6, local copies, waits for them, and re-layouts, unpacked(): return (flat[:split].reshape(a_shape), flat[split:].reshape(b_shape))  4.57 us
    all_to_all x1, starting transfers between devices, on_device(): lax.all_to_all(jnp.stack([real_out, imag_out], axis=2), 'chan', split_axi...  4.37 us
    all_to_all x1, starting transfers between devices, on_device(): lax.all_to_all(spectra, 'chan', split_axis=3, concat_axis=0, tiled=True)  4.22 us
  transfers between devices with their start and end apart: 9, of which 6 were waited for; matrix products, arithmetic and copies ran while one was open for 23% of the time, Pallas kernels for 0%

profile of v9, /device:TPU:1, one launch (start us, length us, event | category | flops | bytes accessed | tf_op | source)
XLA Modules:
  0.0 147.7 jit_solution(17531148536603653577)
XLA Ops:
  1.0 1.3 multiply_subtract_fusion.1
  2.7 1.6 %copy.111 = f32[128,2048]{1,0:T(8,128)S(1)} copy(f32[128,2048]{0,1:T(8,128)} %bitcast.193) | data formatting | bytes 2097152 | tf_op jit(solution)/shard_map/neg | solution.py:43
  6.5 2.0 %copy.129 = f32[1,4,2,64,2,32]{5,4,2,1,0,3:T(2,128)} copy(f32[1,4,2,64,2,32]{5,4,3,2,1,0:T(2,128)} %bitcast.201) | data formatting | bytes 262144 | tf_op jit(solution)/shard_map/broadcast_in_dim;reshape | solution.py:162
  8.6 2.2 %reshape.257 = f32[64,1,512]{2,1,0:T(1,128)} reshape(f32[64,1,4,2,2,32]{5,4,3,2,1,0:T(2,128)} %bitcast.202) | data formatting | bytes 262144
  10.8 19.6 %all-to-all-start = ((f32[64,1,512]{2,1,0:T(1,128)}), f32[64,1,512]{2,1,0:T(1,128)S(1)}, u32[]{:S(2)}, u32[]{:S(2)}) async-start(f32[64,1,512]{2,1,0:T(1,128)} %reshape.257), calls=%async_computation | async-start | bytes 262144 | tf_op jit(solution)/shard_map/all_to_all | solution.py:162
  31.2 2.6 %multiply_subtract_fusion = (f32[128,64,32]{0,1,2:T(8,128)}, f32[128,64,32]{0,1,2:T(8,128)}) fusion(f32[128,64,32]{0,2,1:T(8,128)S(1)} %bitcast.195, f32[128,64,32]{0,2,1:T(8,128)S(1)} %bitcast.196, f32[128,64]{0,1:T(8,128)S(1)} %bitcast.213, f32[128,64]{0,1:T(8,128)S(1)} %bitcast.212), kind=kLoop, calls=%fused_computation.35 | loop fusion | flops 1835008 | bytes 4259840 | tf_op jit(solution)/shard_map/sub | solution.py:41
  33.8 15.2 %all-to-all-done = f32[64,1,512]{2,1,0:T(1,128)S(1)} async-done(((f32[64,1,512]{2,1,0:T(1,128)}), f32[64,1,512]{2,1,0:T(1,128)S(1)}, u32[]{:S(2)}, u32[]{:S(2)}) %all-to-all-start) | async-done | bytes 131104 | tf_op jit(solution)/shard_map/all_to_all | solution.py:162
  51.6 2.0 %bitcast_bitcast_fusion.1 = f32[64,4,2,2,32]{4,3,2,1,0:T(2,128)} fusion(f32[64,1,4,2,2,32]{5,4,3,2,1,0:T(2,128)} %reshape.258), kind=kLoop, calls=%fused_computation.184 | loop fusion | bytes 262144 | tf_op jit(solution)/shard_map/squeeze | solution.py:162
  53.6 1.3 copy.71
  54.9 2.3 %fusion.21 = f32[4,2,2,256]{3,0,2,1:T(4,128)S(1)} fusion(f32[64,4,2,2,32]{0,1,4,3,2:T(4,128)S(1)} %copy.71, f32[128,64,32]{0,1,2:T(8,128)} %get-tuple-element.19, f32[128,64,32]{0,1,2:T(8,128)} %get-tuple-element.18), kind=kOutput, calls=%fused_computation.33 | convolution fusion | flops 50855936 | bytes 2244608 | tf_op jit(solution)/shard_map/scaqx,ksx->caqk/dot_general | solution.py:168
  58.9 4.2 %all-to-all-start.1 = ((f32[8,1,256]{2,1,0:T(1,128)}), f32[8,1,256]{2,1,0:T(1,128)S(1)}, u32[]{:S(2)}, u32[]{:S(2)}) async-start(f32[8,1,256]{2,1,0:T(1,128)} %reshape.259), calls=%async_computation.1 | async-start | bytes 16384 | tf_op jit(solution)/shard_map/all_to_all | solution.py:179
  64.5 2.6 %collective-permute-start.1 = (f32[35840]{0:T(1024)}, f32[35840]{0:T(1024)}, u32[]{:S(2)}, u32[]{:S(2)}) collective-permute-start(f32[35840]{0:T(1024)} %pad_maximum_fusion.8), channel_id=1, source_target_pairs={{8,0},{16,8},{24,16},{32,24},{40,32},{48,40},{56,48},{64,56},{72,6... | collective-permute-start | bytes 430088 | tf_op jit(solution)/shard_map/ppermute | solution.py:107
  71.0 1.7 %fusion.24 = (f32[2,16,32]{2,1,0:T(8,128)S(1)}, f32[2,16,32]{2,1,0:T(8,128)S(1)}, f32[2,16,32]{2,1,0:T(8,128)S(1)}, f32[2,16,32]{2,1,0:T(8,128)S(1)}) fusion(f32[2,2,16,32,32]{4,3,2,1,0:T(8,128)} %param.11, f32[2,16,32]{2,1,0:T(8,128)S(1)} %copy.113, f32[2,16,32]{2,1,0:T(8,128)S(1)} %copy.112), kind=kLoop, calls=%fused_computation.44 | loop fusion | flops 258048 | bytes 286720
  74.0 4.4 %all-to-all-start.2 = ((f32[8,1,256]{2,1,0:T(1,128)}), f32[8,1,256]{2,1,0:T(1,128)S(1)}, u32[]{:S(2)}, u32[]{:S(2)}) async-start(f32[8,1,256]{2,1,0:T(1,128)} %reshape.261), calls=%async_computation.2 | async-start | bytes 16384 | tf_op jit(solution)/shard_map/all_to_all | solution.py:188
  79.0 3.4 %collective-permute-start = (f32[35840]{0:T(1024)}, f32[35840]{0:T(1024)}, u32[]{:S(2)}, u32[]{:S(2)}) collective-permute-start(f32[35840]{0:T(1024)} %pad_maximum_fusion.7), channel_id=1, source_target_pairs={{0,8},{8,16},{16,24},{24,32},{32,40},{40,48},{48,56},{56,64},{64,7... | collective-permute-start | bytes 430088 | tf_op jit(solution)/shard_map/ppermute | solution.py:106
  86.4 2.0 %reshape.234 = f32[4,2,2,64,32]{4,3,2,1,0:T(8,128)} reshape(f32[4,2,2,2048]{3,2,1,0:T(2,128)} %copy.77) | data formatting | bytes 262144 | tf_op jit(solution)/shard_map/reshape | solution.py:60
  89.4 1.4 pad_maximum_fusion.5
  92.0 2.7 %reshape.263 = f32[64,1,640]{2,1,0:T(1,128)} reshape(f32[64,4,2,2,40]{4,3,2,1,0:T(2,128)} %bitcast.203) | data formatting | bytes 327680
  94.7 6.8 %all-to-all-start.3 = ((f32[64,1,640]{2,1,0:T(1,128)}), f32[64,1,640]{2,1,0:T(1,128)S(1)}, u32[]{:S(2)}, u32[]{:S(2)}) async-start(f32[64,1,640]{2,1,0:T(1,128)} %reshape.263), calls=%async_computation.3 | async-start | bytes 327680 | tf_op jit(solution)/shard_map/all_to_all | solution.py:204
  103.6 1.6 %slice.338 = f32[32768]{0:T(1024)} slice(f32[35840]{0:T(1024)} %collective-permute-done.1), slice={[0:32768]} | slice | bytes 262144 | tf_op jit(solution)/shard_map/slice | solution.py:102
  105.1 1.6 %reshape.241 = f32[4,4,2048]{2,1,0:T(4,128)} reshape(f32[32768]{0:T(1024)} %slice.338) | data formatting | bytes 262144 | tf_op jit(solution)/shard_map/reshape | solution.py:102
  106.7 1.6 %slice.337 = f32[32768]{0:T(1024)} slice(f32[35840]{0:T(1024)} %collective-permute-done), slice={[0:32768]} | slice | bytes 262144 | tf_op jit(solution)/shard_map/slice | solution.py:102
  108.3 1.6 %reshape.240 = f32[4,4,2048]{2,1,0:T(4,128)} reshape(f32[32768]{0:T(1024)} %slice.337) | data formatting | bytes 262144 | tf_op jit(solution)/shard_map/reshape | solution.py:102
  110.8 2.2 %collective-permute-start.2 = (f32[3,40,4]{2,1,0:T(8,128)S(1)}, f32[3,40,4]{2,1,0:T(8,128)S(1)}, u32[]{:S(2)}, u32[]{:S(2)}) collective-permute-start(f32[3,40,4]{2,1,0:T(8,128)S(1)} %get-tuple-element.31), channel_id=1, source_target_pairs={{0,1},{1,2},{2,3},{3,4},{4,5},{5,6},{6,7},{8,9},{9,10},{10,11},{11... | collective-permute-start | bytes 5768 | tf_op jit(solution)/shard_map/ppermute | solution.py:21
  113.0 1.3 collective-permute-start.3
  114.3 2.2 %pad_maximum_fusion.4 = f32[4,40,2048]{2,1,0:T(8,128)} fusion(f32[4,4,2048]{2,1,0:T(4,128)} %reshape.241, f32[4,32,2048]{2,1,0:T(8,128)S(1)} %copy-done, f32[4,4,2048]{2,1,0:T(4,128)} %reshape.240), kind=kLoop, calls=%fused_computation.16 | loop fusion | flops 655360 | bytes 2621440 | tf_op jit(solution)/shard_map/concatenate | solution.py:109
  116.6 1.7 %collective-permute-done.3 = f32[3,40,4]{2,1,0:T(8,128)S(1)} collective-permute-done((f32[3,40,4]{2,1,0:T(8,128)S(1)}, f32[3,40,4]{2,1,0:T(8,128)S(1)}, u32[]{:S(2)}, u32[]{:S(2)}) %collective-permute-start.3) | collective-permute-done | bytes 1952 | tf_op jit(solution)/shard_map/ppermute | solution.py:24
  118.5 2.8 %all-to-all-done.3 = f32[64,1,640]{2,1,0:T(1,128)S(1)} async-done(((f32[64,1,640]{2,1,0:T(1,128)}), f32[64,1,640]{2,1,0:T(1,128)S(1)}, u32[]{:S(2)}, u32[]{:S(2)}) %all-to-all-start.3) | async-done | bytes 163872 | tf_op jit(solution)/shard_map/all_to_all | solution.py:204
  124.5 3.8 %fusion.10 = f32[4,40,2048]{2,1,0:T(8,128)S(1)} fusion(f32[4]{0:T(128)S(1)} %copy-done.9, f32[4,40,2048]{2,1,0:T(8,128)S(1)} %copy-done.1, f32[128,2048]{1,0:T(8,128)S(1)} %copy.111, f32[128,2048]{1,0:T(8,128)S(1)} %copy.110, f32[4]{0:T(128)S(1)} %copy-done.10, f32[4,256,40]{2,1,0:T(8,128)S(1)} %bitcast.207, f32[256]{0:T(256)S(1)} %copy-done.11), kind=kOutput, calls=%fused_computation.15 | convolution fusion | flops 525836288 | bytes 4883488 | tf_op jit(solution)/shard_map/ckx,ky->cxy/dot_general | solution.py:209
  129.8 1.6 %reshape.244 = f32[8,165,128]{2,1,0:T(8,128)} reshape(f32[8,2,40,264]{3,2,1,0:T(8,128)S(1)} %copy.81) | data formatting | bytes 1351680 | tf_op jit(solution)/shard_map/reshape | solution.py:222
  131.3 3.7 %all-to-all-start.4 = ((f32[8,165,128]{2,1,0:T(8,128)}), f32[8,165,128]{2,1,0:T(8,128)S(1)}, u32[]{:S(2)}, u32[]{:S(2)}) async-start(f32[8,165,128]{2,1,0:T(8,128)} %reshape.244), calls=%async_computation.4 | async-start | bytes 1376256 | tf_op jit(solution)/shard_map/all_to_all | solution.py:223
  135.0 10.3 %all-to-all-done.4 = f32[8,165,128]{2,1,0:T(8,128)S(1)} async-done(((f32[8,165,128]{2,1,0:T(8,128)}), f32[8,165,128]{2,1,0:T(8,128)S(1)}, u32[]{:S(2)}, u32[]{:S(2)}) %all-to-all-start.4) | async-done | bytes 675872 | tf_op jit(solution)/shard_map/all_to_all | solution.py:223
  (124 shorter events, 31.3 us)
Async XLA Ops:
  2.6 1.7 %copy-start = (f32[4,32,2048]{2,1,0:T(8,128)S(1)}, f32[4,32,2048]{2,1,0:T(8,128)}, u32[]{:S(2)}) copy-start(f32[4,32,2048]{2,1,0:T(8,128)} %param.9) | copy-start | bytes 3145732
  5.5 24.9 %copy-start.3 = (s32[32,256]{1,0:T(8,128)S(1)}, s32[32,256]{1,0:T(8,128)}, u32[]{:S(2)}) copy-start(s32[32,256]{1,0:T(8,128)} %param.16) | copy-start | bytes 98308
  5.5 24.9 %copy-start.4 = (s32[32,256]{1,0:T(8,128)S(1)}, s32[32,256]{1,0:T(8,128)}, u32[]{:S(2)}) copy-start(s32[32,256]{1,0:T(8,128)} %param.17) | copy-start | bytes 98308
  5.5 24.9 %copy-start.5 = (f32[32,256]{1,0:T(8,128)S(1)}, f32[32,256]{1,0:T(8,128)}, u32[]{:S(2)}) copy-start(f32[32,256]{1,0:T(8,128)} %param.10) | copy-start | bytes 98308
  10.8 38.2 %all-to-all-start = ((f32[64,1,512]{2,1,0:T(1,128)}), f32[64,1,512]{2,1,0:T(1,128)S(1)}, u32[]{:S(2)}, u32[]{:S(2)}) async-start(f32[64,1,512]{2,1,0:T(1,128)} %reshape.257), calls=%async_computation | async-start | bytes 262144 | tf_op jit(solution)/shard_map/all_to_all | solution.py:162
  58.9 9.3 %all-to-all-start.1 = ((f32[8,1,256]{2,1,0:T(1,128)}), f32[8,1,256]{2,1,0:T(1,128)S(1)}, u32[]{:S(2)}, u32[]{:S(2)}) async-start(f32[8,1,256]{2,1,0:T(1,128)} %reshape.259), calls=%async_computation.1 | async-start | bytes 16384 | tf_op jit(solution)/shard_map/all_to_all | solution.py:179
  64.5 36.9 %collective-permute-start.1 = (f32[35840]{0:T(1024)}, f32[35840]{0:T(1024)}, u32[]{:S(2)}, u32[]{:S(2)}) collective-permute-start(f32[35840]{0:T(1024)} %pad_maximum_fusion.8), channel_id=1, source_target_pairs={{8,0},{16,8},{24,16},{32,24},{40,32},{48,40},{56,48},{64,56},{72,6... | collective-permute-start | bytes 430088 | tf_op jit(solution)/shard_map/ppermute | solution.py:107
  70.1 8.3 %copy-start.2 = (f32[4,16,4,128]{3,1,2,0:T(8,128)S(1)}, f32[4,16,4,128]{3,1,2,0:T(8,128)}, u32[]{:S(2)}) copy-start(f32[4,16,4,128]{3,1,2,0:T(8,128)} %copy.116) | copy-start | bytes 393220
  70.9 13.7 %copy-start.8 = (pred[65]{0:T(512)(128)(4,1)S(1)}, pred[65]{0:T(512)(128)(4,1)}, u32[]{:S(2)}) copy-start(pred[65]{0:T(512)(128)(4,1)} %constant.38.clone.1) | copy-start | bytes 199
  74.0 9.4 %all-to-all-start.2 = ((f32[8,1,256]{2,1,0:T(1,128)}), f32[8,1,256]{2,1,0:T(1,128)S(1)}, u32[]{:S(2)}, u32[]{:S(2)}) async-start(f32[8,1,256]{2,1,0:T(1,128)} %reshape.261), calls=%async_computation.2 | async-start | bytes 16384 | tf_op jit(solution)/shard_map/all_to_all | solution.py:188
  79.0 23.2 %collective-permute-start = (f32[35840]{0:T(1024)}, f32[35840]{0:T(1024)}, u32[]{:S(2)}, u32[]{:S(2)}) collective-permute-start(f32[35840]{0:T(1024)} %pad_maximum_fusion.7), channel_id=1, source_target_pairs={{0,8},{8,16},{16,24},{24,32},{32,40},{40,48},{48,56},{56,64},{64,7... | collective-permute-start | bytes 430088 | tf_op jit(solution)/shard_map/ppermute | solution.py:106
  94.7 26.6 %all-to-all-start.3 = ((f32[64,1,640]{2,1,0:T(1,128)}), f32[64,1,640]{2,1,0:T(1,128)S(1)}, u32[]{:S(2)}, u32[]{:S(2)}) async-start(f32[64,1,640]{2,1,0:T(1,128)} %reshape.263), calls=%async_computation.3 | async-start | bytes 327680 | tf_op jit(solution)/shard_map/all_to_all | solution.py:204
  110.8 5.7 %collective-permute-start.2 = (f32[3,40,4]{2,1,0:T(8,128)S(1)}, f32[3,40,4]{2,1,0:T(8,128)S(1)}, u32[]{:S(2)}, u32[]{:S(2)}) collective-permute-start(f32[3,40,4]{2,1,0:T(8,128)S(1)} %get-tuple-element.31), channel_id=1, source_target_pairs={{0,1},{1,2},{2,3},{3,4},{4,5},{5,6},{6,7},{8,9},{9,10},{10,11},{11... | collective-permute-start | bytes 5768 | tf_op jit(solution)/shard_map/ppermute | solution.py:21
  113.0 5.3 %collective-permute-start.3 = (f32[3,40,4]{2,1,0:T(8,128)S(1)}, f32[3,40,4]{2,1,0:T(8,128)S(1)}, u32[]{:S(2)}, u32[]{:S(2)}) collective-permute-start(f32[3,40,4]{2,1,0:T(8,128)S(1)} %get-tuple-element.32), channel_id=1, source_target_pairs={{1,0},{2,1},{3,2},{4,3},{5,4},{6,5},{7,6},{9,8},{10,9},{11,10},{12... | collective-permute-start | bytes 5768 | tf_op jit(solution)/shard_map/ppermute | solution.py:24
  122.2 1.4 copy-start.9
  122.2 1.4 copy-start.10
  122.2 1.4 copy-start.11
  123.2 1.3 copy-start.1
  124.5 3.8 %copy-start.6 = (f32[2,4]{1,0:T(2,128)S(1)}, f32[2,4]{1,0:T(2,128)}, u32[]{:S(2)}) copy-start(f32[2,4]{1,0:T(2,128)} %param.14) | copy-start | bytes 100
  131.3 14.2 %copy-start.7 = (f32[2]{0:T(128)S(1)}, f32[2]{0:T(128)}, u32[]{:S(2)}) copy-start(f32[2]{0:T(128)} %param.15) | copy-start | bytes 28
  131.3 14.0 %all-to-all-start.4 = ((f32[8,165,128]{2,1,0:T(8,128)}), f32[8,165,128]{2,1,0:T(8,128)S(1)}, u32[]{:S(2)}, u32[]{:S(2)}) async-start(f32[8,165,128]{2,1,0:T(8,128)} %reshape.244), calls=%async_computation.4 | async-start | bytes 1376256 | tf_op jit(solution)/shard_map/all_to_all | solution.py:223

commit v10 on v8

--- a/solution.py
+++ b/solution.py
@@ -179,11 +179,11 @@
     real_in = gathered[:, :, 0]
     imag_in = gathered[:, :, 1]
     real_out = jnp.einsum(
-        "qpio,iqp->oqp", spectral_weight[0], real_in, precision=highest
-    ) - jnp.einsum("qpio,iqp->oqp", spectral_weight[1], imag_in, precision=highest)
+        "qpio,iqp->oqp", spectral_weight[0], real_in, precision=high
+    ) - jnp.einsum("qpio,iqp->oqp", spectral_weight[1], imag_in, precision=high)
     imag_out = jnp.einsum(
-        "qpio,iqp->oqp", spectral_weight[0], imag_in, precision=highest
-    ) + jnp.einsum("qpio,iqp->oqp", spectral_weight[1], real_in, precision=highest)
+        "qpio,iqp->oqp", spectral_weight[0], imag_in, precision=high
+    ) + jnp.einsum("qpio,iqp->oqp", spectral_weight[1], real_in, precision=high)
     mixed = lax.all_to_all(
         jnp.stack([real_out, imag_out], axis=2), "chan", split_axis=0, concat_axis=3, tiled=True
     )

time: 146 us -> 146 us (level)
  no operation moved by 1% of the time
where the time goes in v10:
time: 146 us; the launch traced here: 145 us
  starting transfers between devices  48.2 us (33%)
  waiting for transfers between devices  39.6 us (27%)
  local copies, waits for them, and re-layouts  35.8 us (25%)
  other arithmetic  13.8 us (9%)
  matrix products  6.62 us (5%)
    all_to_all x1, starting transfers between devices, on_device(): lax.all_to_all(spec_y, 'rows', split_axis=2, concat_axis=3, tiled=True)  19.6 us
    all_to_all x1, waiting for transfers between devices, on_device(): lax.all_to_all(spec_y, 'rows', split_axis=2, concat_axis=3, tiled=True)  18.5 us
    unnamed x42, local copies, waits for them, and re-layouts  13.6 us
    all_to_all x1, waiting for transfers between devices, on_device(): lax.all_to_all(flat, 'chan', split_axis=0, concat_axis=0, tiled=True)  10.7 us
    all_to_all x1, starting transfers between devices, on_device(): lax.all_to_all(inverted, 'rows', split_axis=3, concat_axis=2, tiled=True)  6.95 us
    all_to_all x1, waiting for transfers between devices, on_device(): lax.all_to_all(inverted, 'rows', split_axis=3, concat_axis=2, tiled=True)  5.51 us
    all_to_all x1, starting transfers between devices, on_device(): lax.all_to_all(jnp.stack([real_out, imag_out], axis=2), 'chan', split_axi...  4.37 us
    all_to_all x1, starting transfers between devices, on_device(): lax.all_to_all(spectra, 'chan', split_axis=3, concat_axis=0, tiled=True)  4.22 us
  transfers between devices with their start and end apart: 9, of which 6 were waited for; matrix products, arithmetic and copies ran while one was open for 19% of the time, Pallas kernels for 0%

profile of v10, /device:TPU:1, one launch (start us, length us, event | category | flops | bytes accessed | tf_op | source)
XLA Modules:
  0.0 145.3 jit_solution(16249334630822035622)
XLA Ops:
  3.4 1.2 fusion.17
  4.7 1.0 copy.92
  5.7 2.2 %reshape.243 = f32[64,1,512]{2,1,0:T(1,128)} reshape(f32[128,4,2,32]{3,2,1,0:T(2,128)} %bitcast.208) | data formatting | bytes 262144
  8.0 19.6 %all-to-all-start = ((f32[64,1,512]{2,1,0:T(1,128)}), f32[64,1,512]{2,1,0:T(1,128)S(1)}, u32[]{:S(2)}, u32[]{:S(2)}) async-start(f32[64,1,512]{2,1,0:T(1,128)} %reshape.243), calls=%async_computation | async-start | bytes 262144 | tf_op jit(solution)/shard_map/all_to_all | solution.py:162
  27.6 18.5 %all-to-all-done = f32[64,1,512]{2,1,0:T(1,128)S(1)} async-done(((f32[64,1,512]{2,1,0:T(1,128)}), f32[64,1,512]{2,1,0:T(1,128)S(1)}, u32[]{:S(2)}, u32[]{:S(2)}) %all-to-all-start) | async-done | bytes 131104 | tf_op jit(solution)/shard_map/all_to_all | solution.py:162
  47.6 1.2 reshape.244
  48.9 1.1 copy.93
  50.9 1.3 all_to_all.56
  52.2 1.0 fusion.3
  55.0 4.2 %all-to-all-start.1 = ((f32[8,1,256]{2,1,0:T(1,128)}), f32[8,1,256]{2,1,0:T(1,128)S(1)}, u32[]{:S(2)}, u32[]{:S(2)}) async-start(f32[8,1,256]{2,1,0:T(1,128)} %reshape.245), calls=%async_computation.1 | async-start | bytes 16384 | tf_op jit(solution)/shard_map/all_to_all | solution.py:178
  60.6 2.6 %collective-permute-start.1 = (f32[35840]{0:T(1024)}, f32[35840]{0:T(1024)}, u32[]{:S(2)}, u32[]{:S(2)}) collective-permute-start(f32[35840]{0:T(1024)} %pad_maximum_fusion.4), channel_id=1, source_target_pairs={{8,0},{16,8},{24,16},{32,24},{40,32},{48,40},{56,48},{64,56},{72,6... | collective-permute-start | bytes 430088 | tf_op jit(solution)/shard_map/ppermute | solution.py:107
  63.1 1.1 all-to-all-done.1
  67.2 1.7 %fusion.22 = (f32[2,16,32]{2,1,0:T(8,128)S(1)}, f32[2,16,32]{2,1,0:T(8,128)S(1)}, f32[2,16,32]{2,1,0:T(8,128)S(1)}, f32[2,16,32]{2,1,0:T(8,128)S(1)}) fusion(f32[2,2,16,32,32]{4,3,2,1,0:T(8,128)} %param.11, f32[2,16,32]{2,1,0:T(8,128)S(1)} %copy.140, f32[2,16,32]{2,1,0:T(8,128)S(1)} %copy.139), kind=kLoop, calls=%fused_computation.40 | loop fusion | flops 258048 | bytes 286720
  70.1 4.4 %all-to-all-start.2 = ((f32[8,1,256]{2,1,0:T(1,128)}), f32[8,1,256]{2,1,0:T(1,128)S(1)}, u32[]{:S(2)}, u32[]{:S(2)}) async-start(f32[8,1,256]{2,1,0:T(1,128)} %reshape.247), calls=%async_computation.2 | async-start | bytes 16384 | tf_op jit(solution)/shard_map/all_to_all | solution.py:187
  75.2 3.4 %collective-permute-start = (f32[35840]{0:T(1024)}, f32[35840]{0:T(1024)}, u32[]{:S(2)}, u32[]{:S(2)}) collective-permute-start(f32[35840]{0:T(1024)} %pad_maximum_fusion.3), channel_id=1, source_target_pairs={{0,8},{8,16},{16,24},{24,32},{32,40},{40,48},{48,56},{56,64},{64,7... | collective-permute-start | bytes 430088 | tf_op jit(solution)/shard_map/ppermute | solution.py:106
  82.6 1.9 %reshape.222 = f32[4,2,2,64,32]{4,3,2,1,0:T(8,128)} reshape(f32[4,2,2,2048]{3,2,1,0:T(2,128)} %copy.105) | data formatting | bytes 262144 | tf_op jit(solution)/shard_map/reshape | solution.py:60
  84.5 1.0 reshape.221
  85.5 1.4 pad_maximum_fusion.1
  86.9 1.2 copy.154
  88.1 2.7 %reshape.249 = f32[64,1,640]{2,1,0:T(1,128)} reshape(f32[64,4,2,2,40]{4,3,2,1,0:T(2,128)} %bitcast.211) | data formatting | bytes 327680
  90.8 7.0 %all-to-all-start.3 = ((f32[64,1,640]{2,1,0:T(1,128)}), f32[64,1,640]{2,1,0:T(1,128)}, u32[]{:S(2)}, u32[]{:S(2)}) async-start(f32[64,1,640]{2,1,0:T(1,128)} %reshape.249), calls=%async_computation.3 | async-start | bytes 327680 | tf_op jit(solution)/shard_map/all_to_all | solution.py:203
  100.9 1.6 %slice.337 = f32[32768]{0:T(1024)} slice(f32[35840]{0:T(1024)} %collective-permute-done), slice={[0:32768]} | slice | bytes 262144 | tf_op jit(solution)/shard_map/slice | solution.py:102
  104.3 2.2 %collective-permute-start.2 = (f32[3,40,4]{2,1,0:T(8,128)S(1)}, f32[3,40,4]{2,1,0:T(8,128)S(1)}, u32[]{:S(2)}, u32[]{:S(2)}) collective-permute-start(f32[3,40,4]{2,1,0:T(8,128)S(1)} %get-tuple-element.29), channel_id=1, source_target_pairs={{0,1},{1,2},{2,3},{3,4},{4,5},{5,6},{6,7},{8,9},{9,10},{10,11},{11... | collective-permute-start | bytes 5768 | tf_op jit(solution)/shard_map/ppermute | solution.py:21
  106.5 1.3 collective-permute-start.3
  107.8 1.3 pad_maximum_fusion
  109.1 2.8 %collective-permute-done.3 = f32[3,40,4]{2,1,0:T(8,128)S(1)} collective-permute-done((f32[3,40,4]{2,1,0:T(8,128)S(1)}, f32[3,40,4]{2,1,0:T(8,128)S(1)}, u32[]{:S(2)}, u32[]{:S(2)}) %collective-permute-start.3) | collective-permute-done | bytes 1952 | tf_op jit(solution)/shard_map/ppermute | solution.py:24
  112.0 5.5 %all-to-all-done.3 = f32[64,1,640]{2,1,0:T(1,128)} async-done(((f32[64,1,640]{2,1,0:T(1,128)}), f32[64,1,640]{2,1,0:T(1,128)}, u32[]{:S(2)}, u32[]{:S(2)}) %all-to-all-start.3) | async-done | bytes 163872 | tf_op jit(solution)/shard_map/all_to_all | solution.py:203
  117.6 1.9 %reduce.11 = f32[64,640]{1,0:T(8,128)S(1)} reduce(f32[64,1,640]{2,1,0:T(1,128)} %all-to-all-done.3, f32[]{:T(128)} %broadcast.268), dimensions={1}, to_apply=%all_to_all.65.reduce_sub_computation | reduce | bytes 327684 | tf_op jit(solution)/shard_map/all_to_all | solution.py:203
  121.8 3.8 %fusion.9 = f32[4,40,2048]{2,1,0:T(8,128)S(1)} fusion(f32[4,40,2048]{2,1,0:T(8,128)S(1)} %copy-done.1, f32[256,2048]{1,0:T(8,128)S(1)} %bitcast_dynamic-update-slice_fusion, f32[4]{0:T(128)S(1)} %copy-done.9, f32[4]{0:T(128)S(1)} %copy-done.10, f32[4,256,40]{2,1,0:T(8,128)S(1)} %bitcast.215, f32[256]{0:T(256)S(1)} %broadcast_bitcast_fusion), kind=kOutput, calls=%fused_computation.12 | convolution fusion | flops 525312000 | bytes 4883488 | tf_op jit(solution)/shard_map/ckx,ky->cxy/dot_general | solution.py:208
  127.0 1.6 %reshape.232 = f32[8,165,128]{2,1,0:T(8,128)} reshape(f32[8,2,40,264]{3,2,1,0:T(8,128)S(1)} %copy.109) | data formatting | bytes 1351680 | tf_op jit(solution)/shard_map/reshape | solution.py:221
  128.6 3.7 %all-to-all-start.4 = ((f32[8,165,128]{2,1,0:T(8,128)}), f32[8,165,128]{2,1,0:T(8,128)S(1)}, u32[]{:S(2)}, u32[]{:S(2)}) async-start(f32[8,165,128]{2,1,0:T(8,128)} %reshape.232), calls=%async_computation.4 | async-start | bytes 1376256 | tf_op jit(solution)/shard_map/all_to_all | solution.py:222
  132.3 10.7 %all-to-all-done.4 = f32[8,165,128]{2,1,0:T(8,128)S(1)} async-done(((f32[8,165,128]{2,1,0:T(8,128)}), f32[8,165,128]{2,1,0:T(8,128)S(1)}, u32[]{:S(2)}, u32[]{:S(2)}) %all-to-all-start.4) | async-done | bytes 675872 | tf_op jit(solution)/shard_map/all_to_all | solution.py:222
  (121 shorter events, 28.1 us)
Async XLA Ops:
  2.2 1.2 copy-start
  4.6 23.0 %copy-start.3 = (s32[32,256]{1,0:T(8,128)S(1)}, s32[32,256]{1,0:T(8,128)}, u32[]{:S(2)}) copy-start(s32[32,256]{1,0:T(8,128)} %param.16) | copy-start | bytes 98308
  4.6 23.0 %copy-start.4 = (s32[32,256]{1,0:T(8,128)S(1)}, s32[32,256]{1,0:T(8,128)}, u32[]{:S(2)}) copy-start(s32[32,256]{1,0:T(8,128)} %param.17) | copy-start | bytes 98308
  4.6 23.0 %copy-start.5 = (f32[32,256]{1,0:T(8,128)S(1)}, f32[32,256]{1,0:T(8,128)}, u32[]{:S(2)}) copy-start(f32[32,256]{1,0:T(8,128)} %param.10) | copy-start | bytes 98308
  8.0 38.2 %all-to-all-start = ((f32[64,1,512]{2,1,0:T(1,128)}), f32[64,1,512]{2,1,0:T(1,128)S(1)}, u32[]{:S(2)}, u32[]{:S(2)}) async-start(f32[64,1,512]{2,1,0:T(1,128)} %reshape.243), calls=%async_computation | async-start | bytes 262144 | tf_op jit(solution)/shard_map/all_to_all | solution.py:162
  55.0 9.3 %all-to-all-start.1 = ((f32[8,1,256]{2,1,0:T(1,128)}), f32[8,1,256]{2,1,0:T(1,128)S(1)}, u32[]{:S(2)}, u32[]{:S(2)}) async-start(f32[8,1,256]{2,1,0:T(1,128)} %reshape.245), calls=%async_computation.1 | async-start | bytes 16384 | tf_op jit(solution)/shard_map/all_to_all | solution.py:178
  60.6 37.2 %collective-permute-start.1 = (f32[35840]{0:T(1024)}, f32[35840]{0:T(1024)}, u32[]{:S(2)}, u32[]{:S(2)}) collective-permute-start(f32[35840]{0:T(1024)} %pad_maximum_fusion.4), channel_id=1, source_target_pairs={{8,0},{16,8},{24,16},{32,24},{40,32},{48,40},{56,48},{64,56},{72,6... | collective-permute-start | bytes 430088 | tf_op jit(solution)/shard_map/ppermute | solution.py:107
  66.2 8.3 %copy-start.2 = (f32[4,16,4,128]{3,1,2,0:T(8,128)S(1)}, f32[4,16,4,128]{3,1,2,0:T(8,128)}, u32[]{:S(2)}) copy-start(f32[4,16,4,128]{3,1,2,0:T(8,128)} %copy.145) | copy-start | bytes 393220
  67.0 13.7 %copy-start.8 = (pred[65]{0:T(512)(128)(4,1)S(1)}, pred[65]{0:T(512)(128)(4,1)}, u32[]{:S(2)}) copy-start(pred[65]{0:T(512)(128)(4,1)} %constant.38.clone.1) | copy-start | bytes 199
  70.1 9.4 %all-to-all-start.2 = ((f32[8,1,256]{2,1,0:T(1,128)}), f32[8,1,256]{2,1,0:T(1,128)S(1)}, u32[]{:S(2)}, u32[]{:S(2)}) async-start(f32[8,1,256]{2,1,0:T(1,128)} %reshape.247), calls=%async_computation.2 | async-start | bytes 16384 | tf_op jit(solution)/shard_map/all_to_all | solution.py:187
  75.2 23.4 %collective-permute-start = (f32[35840]{0:T(1024)}, f32[35840]{0:T(1024)}, u32[]{:S(2)}, u32[]{:S(2)}) collective-permute-start(f32[35840]{0:T(1024)} %pad_maximum_fusion.3), channel_id=1, source_target_pairs={{0,8},{8,16},{16,24},{24,32},{32,40},{40,48},{48,56},{56,64},{64,7... | collective-permute-start | bytes 430088 | tf_op jit(solution)/shard_map/ppermute | solution.py:106
  90.8 26.7 %all-to-all-start.3 = ((f32[64,1,640]{2,1,0:T(1,128)}), f32[64,1,640]{2,1,0:T(1,128)}, u32[]{:S(2)}, u32[]{:S(2)}) async-start(f32[64,1,640]{2,1,0:T(1,128)} %reshape.249), calls=%async_computation.3 | async-start | bytes 327680 | tf_op jit(solution)/shard_map/all_to_all | solution.py:203
  104.3 4.8 %collective-permute-start.2 = (f32[3,40,4]{2,1,0:T(8,128)S(1)}, f32[3,40,4]{2,1,0:T(8,128)S(1)}, u32[]{:S(2)}, u32[]{:S(2)}) collective-permute-start(f32[3,40,4]{2,1,0:T(8,128)S(1)} %get-tuple-element.29), channel_id=1, source_target_pairs={{0,1},{1,2},{2,3},{3,4},{4,5},{5,6},{6,7},{8,9},{9,10},{10,11},{11... | collective-permute-start | bytes 5768 | tf_op jit(solution)/shard_map/ppermute | solution.py:21
  106.5 5.4 %collective-permute-start.3 = (f32[3,40,4]{2,1,0:T(8,128)S(1)}, f32[3,40,4]{2,1,0:T(8,128)S(1)}, u32[]{:S(2)}, u32[]{:S(2)}) collective-permute-start(f32[3,40,4]{2,1,0:T(8,128)S(1)} %get-tuple-element.30), channel_id=1, source_target_pairs={{1,0},{2,1},{3,2},{4,3},{5,4},{6,5},{7,6},{9,8},{10,9},{11,10},{12... | collective-permute-start | bytes 5768 | tf_op jit(solution)/shard_map/ppermute | solution.py:24
  119.5 1.4 copy-start.9
  119.5 1.4 copy-start.10
  120.4 1.3 copy-start.1
  121.8 3.8 %copy-start.6 = (f32[2,4]{1,0:T(2,128)S(1)}, f32[2,4]{1,0:T(2,128)}, u32[]{:S(2)}) copy-start(f32[2,4]{1,0:T(2,128)} %param.14) | copy-start | bytes 100
  128.6 14.6 %copy-start.7 = (f32[2]{0:T(128)S(1)}, f32[2]{0:T(128)}, u32[]{:S(2)}) copy-start(f32[2]{0:T(128)} %param.15) | copy-start | bytes 28
  128.6 14.4 %all-to-all-start.4 = ((f32[8,165,128]{2,1,0:T(8,128)}), f32[8,165,128]{2,1,0:T(8,128)S(1)}, u32[]{:S(2)}, u32[]{:S(2)}) async-start(f32[8,165,128]{2,1,0:T(8,128)} %reshape.232), calls=%async_computation.4 | async-start | bytes 1376256 | tf_op jit(solution)/shard_map/all_to_all | solution.py:222

commit v11 on v8

--- a/solution.py
+++ b/solution.py
@@ -40,6 +40,17 @@
     cos_lo, sin_lo = jnp.cos(fine)[:, None, :], jnp.sin(fine)[:, None, :]
     cos_all = (cos_hi * cos_lo - sin_hi * sin_lo).reshape(modes, length)
     sin_all = (sin_hi * cos_lo + cos_hi * sin_lo).reshape(modes, length)
+    return jnp.concatenate([cos_all, -sin_all])
+
+
+def window_table(modes, length, count, size, halo):
+    ids = jnp.arange(modes, dtype=jnp.int32)
+    coarse = angles(ids, jnp.arange(count, dtype=jnp.int32) * size, length)
+    fine = angles(ids, (jnp.arange(size + 2 * halo, dtype=jnp.int32) - halo) % length, length)
+    cos_hi, sin_hi = jnp.cos(coarse)[:, :, None], jnp.sin(coarse)[:, :, None]
+    cos_lo, sin_lo = jnp.cos(fine)[:, None, :], jnp.sin(fine)[:, None, :]
+    cos_all = cos_hi * cos_lo - sin_hi * sin_lo
+    sin_all = sin_hi * cos_lo + cos_hi * sin_lo
     return jnp.concatenate([cos_all, -sin_all])
 
 
@@ -198,8 +209,8 @@
         [jnp.pad(imag_pos + imag_neg, pad), jnp.pad(real_neg - real_pos, pad)], axis=-1
     )
     coef = jnp.stack([coef_real, coef_imag], axis=1)
-    inverted = jnp.einsum("otqk,kx->otqx", coef, x_table, precision=high)
-    inverted = windows(inverted, row_devices, row_count, halo)
+    row_windows = window_table(x_modes, all_rows, row_devices, row_count, halo)
+    inverted = jnp.einsum("otqk,krj->otqrj", coef, row_windows, precision=high)
     inverted = lax.all_to_all(inverted, "rows", split_axis=3, concat_axis=2, tiled=True)
     y_weights = jnp.where(jnp.arange(all_ymodes) == 0, 1.0, 2.0).astype(jnp.float32) * norm_scale
     inverted = inverted.reshape(local_chan, 2, all_ymodes, win_rows) * y_weights[:, None]

time: 146 us -> 144 us (0.986)
  local copies, waits for them, and re-layouts: 35.8 us -> 30.4 us
  matrix products: 6.62 us -> 11.7 us
  waiting for transfers between devices: 39.6 us -> 36.6 us
    dot_general x1, matrix products: 0.62 us -> 5.72 us  [on_device(): inverted = jnp.einsum('otqk,krj->otqrj', coef, row_windows, precision=high)]
    reshape x2 -> x0, local copies, waits for them, and re-layouts: 2.97 us -> none  [the longest x1 1.94 us: windows(): tail = padded[..., size:size + count * size].reshape(lead + (count, size))]
    all_to_all x1, waiting for transfers between devices: 18.5 us -> 15.6 us  [on_device(): lax.all_to_all(spec_y, 'rows', split_axis=2, concat_axis=3, tiled=True)]
    ppermute x1, waiting for transfers between devices: 2.79 us -> 0.01 us  [with_halo(): lax.ppermute(lax.slice_in_dim(block, 0, width, axis=dim), axis, backward)]
    all_to_all x1, waiting for transfers between devices: 5.51 us -> 7.82 us  [on_device(): lax.all_to_all(inverted, 'rows', split_axis=3, concat_axis=2, tiled=True)]
  transfers between devices with their start and end apart: 9 -> 9, of which waited for: 6 -> 5; matrix products, arithmetic and copies ran while one was open for 19% -> 19% of each run, Pallas kernels for 0% -> 0%
where the time goes in v11:
time: 144 us; the launch traced here: 143 us
  starting transfers between devices  48.3 us (34%)
  waiting for transfers between devices  36.6 us (25%)
  local copies, waits for them, and re-layouts  30.4 us (21%)
  other arithmetic  15.1 us (10%)
  matrix products  11.7 us (8%)
    all_to_all x1, starting transfers between devices, on_device(): lax.all_to_all(spec_y, 'rows', split_axis=2, concat_axis=3, tiled=True)  19.6 us
    all_to_all x1, waiting for transfers between devices, on_device(): lax.all_to_all(spec_y, 'rows', split_axis=2, concat_axis=3, tiled=True)  15.6 us
    unnamed x42, local copies, waits for them, and re-layouts  13.6 us
    all_to_all x1, waiting for transfers between devices, on_device(): lax.all_to_all(flat, 'chan', split_axis=0, concat_axis=0, tiled=True)  10.6 us
    all_to_all x1, waiting for transfers between devices, on_device(): lax.all_to_all(inverted, 'rows', split_axis=3, concat_axis=2, tiled=True)  7.82 us
    all_to_all x1, starting transfers between devices, on_device(): lax.all_to_all(inverted, 'rows', split_axis=3, concat_axis=2, tiled=True)  6.15 us
    dot_general x1, matrix products, on_device(): inverted = jnp.einsum('otqk,krj->otqrj', coef, row_windows, precision=high)  5.72 us
    all_to_all x1, starting transfers between devices, on_device(): lax.all_to_all(jnp.stack([real_out, imag_out], axis=2), 'chan', split_axi...  4.88 us
  transfers between devices with their start and end apart: 9, of which 5 were waited for; matrix products, arithmetic and copies ran while one was open for 19% of the time, Pallas kernels for 0%

profile of v11, /device:TPU:1, one launch (start us, length us, event | category | flops | bytes accessed | tf_op | source)
XLA Modules:
  0.0 143.3 jit_solution(8885140549587663457)
XLA Ops:
  3.4 1.2 fusion.17
  4.7 1.0 copy.81
  5.7 2.2 %reshape.354 = f32[64,1,512]{2,1,0:T(1,128)} reshape(f32[128,4,2,32]{3,2,1,0:T(2,128)} %bitcast.210) | data formatting | bytes 262144
  8.0 19.6 %all-to-all-start = ((f32[64,1,512]{2,1,0:T(1,128)}), f32[64,1,512]{2,1,0:T(1,128)S(1)}, u32[]{:S(2)}, u32[]{:S(2)}) async-start(f32[64,1,512]{2,1,0:T(1,128)} %reshape.354), calls=%async_computation | async-start | bytes 262144 | tf_op jit(solution)/shard_map/all_to_all | solution.py:173
  28.8 1.7 %maximum_bitcast_fusion = f32[256,64,40,1,1]{0,1,2,3,4:T(8,128)} fusion(f32[128,64,40]{0,1,2:T(8,128)S(1)} %get-tuple-element.30, f32[128,64,40]{0,1,2:T(8,128)S(1)} %get-tuple-element.29), kind=kLoop, calls=%fused_computation | loop fusion | flops 655360 | bytes 5242880 | tf_op jit(solution)/shard_map/concatenate | solution.py:54
  30.5 15.6 %all-to-all-done = f32[64,1,512]{2,1,0:T(1,128)S(1)} async-done(((f32[64,1,512]{2,1,0:T(1,128)}), f32[64,1,512]{2,1,0:T(1,128)S(1)}, u32[]{:S(2)}, u32[]{:S(2)}) %all-to-all-start) | async-done | bytes 131104 | tf_op jit(solution)/shard_map/all_to_all | solution.py:173
  47.6 1.3 reshape.355
  48.9 1.1 copy.82
  50.9 1.3 all_to_all.56
  52.2 1.0 fusion.3
  54.9 4.2 %all-to-all-start.1 = ((f32[8,1,256]{2,1,0:T(1,128)}), f32[8,1,256]{2,1,0:T(1,128)S(1)}, u32[]{:S(2)}, u32[]{:S(2)}) async-start(f32[8,1,256]{2,1,0:T(1,128)} %reshape.356), calls=%async_computation.1 | async-start | bytes 16384 | tf_op jit(solution)/shard_map/all_to_all | solution.py:189
  59.9 3.1 %collective-permute-start = (f32[35840]{0:T(1024)}, f32[35840]{0:T(1024)}, u32[]{:S(2)}, u32[]{:S(2)}) collective-permute-start(f32[35840]{0:T(1024)} %pad_maximum_fusion.2), channel_id=1, source_target_pairs={{0,8},{8,16},{16,24},{24,32},{32,40},{40,48},{48,56},{56,64},{64,7... | collective-permute-start | bytes 430088 | tf_op jit(solution)/shard_map/ppermute | solution.py:117
  67.1 1.7 %fusion.22 = (f32[2,16,32]{2,1,0:T(8,128)S(1)}, f32[2,16,32]{2,1,0:T(8,128)S(1)}, f32[2,16,32]{2,1,0:T(8,128)S(1)}, f32[2,16,32]{2,1,0:T(8,128)S(1)}) fusion(f32[2,2,16,32,32]{4,3,2,1,0:T(8,128)} %param.11, f32[2,16,32]{2,1,0:T(8,128)S(1)} %copy.129, f32[2,16,32]{2,1,0:T(8,128)S(1)} %copy.128), kind=kLoop, calls=%fused_computation.42 | loop fusion | flops 258048 | bytes 286720
  70.1 4.9 %all-to-all-start.2 = ((f32[8,1,256]{2,1,0:T(1,128)}), f32[8,1,256]{2,1,0:T(1,128)S(1)}, u32[]{:S(2)}, u32[]{:S(2)}) async-start(f32[8,1,256]{2,1,0:T(1,128)} %reshape.358), calls=%async_computation.2 | async-start | bytes 16384 | tf_op jit(solution)/shard_map/all_to_all | solution.py:198
  75.6 2.4 %collective-permute-start.1 = (f32[35840]{0:T(1024)}, f32[35840]{0:T(1024)}, u32[]{:S(2)}, u32[]{:S(2)}) collective-permute-start(f32[35840]{0:T(1024)} %pad_maximum_fusion.3), channel_id=1, source_target_pairs={{8,0},{16,8},{24,16},{32,24},{40,32},{48,40},{56,48},{64,56},{72,6... | collective-permute-start | bytes 430088 | tf_op jit(solution)/shard_map/ppermute | solution.py:118
  78.0 2.0 %all-to-all-done.2 = f32[8,1,256]{2,1,0:T(1,128)S(1)} async-done(((f32[8,1,256]{2,1,0:T(1,128)}), f32[8,1,256]{2,1,0:T(1,128)S(1)}, u32[]{:S(2)}, u32[]{:S(2)}) %all-to-all-start.2) | async-done | bytes 8224 | tf_op jit(solution)/shard_map/all_to_all | solution.py:198
  81.3 5.7 %fusion.105 = f32[64,2,2,4,40]{4,3,2,1,0:T(4,128)} fusion(f32[256,64,40,1,1]{0,1,2,3,4:T(8,128)} %maximum_bitcast_fusion, f32[4,1,2,256]{3,0,2,1:T(4,128)S(1)} %fusion.93, f32[4,1,2,256]{3,0,2,1:T(4,128)S(1)} %fusion.94), kind=kOutput, calls=%fused_computation.206 | convolution fusion | flops 62918656 | bytes 2801664 | tf_op jit(solution)/shard_map/otqk,krj->otqrj/dot_general | solution.py:213
  87.1 2.4 %reshape.360 = f32[64,1,640]{2,1,0:T(1,128)} reshape(f32[64,2,2,4,40]{4,3,2,1,0:T(4,128)} %fusion.105) | data formatting | bytes 327680
  89.5 6.1 %all-to-all-start.3 = ((f32[64,1,640]{2,1,0:T(1,128)}), f32[64,1,640]{2,1,0:T(1,128)}, u32[]{:S(2)}, u32[]{:S(2)}) async-start(f32[64,1,640]{2,1,0:T(1,128)} %reshape.360), calls=%async_computation.3 | async-start | bytes 327680 | tf_op jit(solution)/shard_map/all_to_all | solution.py:214
  97.9 2.8 %collective-permute-start.2 = (f32[3,40,4]{2,1,0:T(8,128)}, f32[3,40,4]{2,1,0:T(8,128)}, u32[]{:S(2)}, u32[]{:S(2)}) collective-permute-start(f32[3,40,4]{2,1,0:T(8,128)} %get-tuple-element.27), channel_id=1, source_target_pairs={{0,1},{1,2},{2,3},{3,4},{4,5},{5,6},{6,7},{8,9},{9,10},{10,11},{11... | collective-permute-start | bytes 5768 | tf_op jit(solution)/shard_map/ppermute | solution.py:21
  100.7 1.3 collective-permute-start.3
  102.9 1.6 %slice.325 = f32[32768]{0:T(1024)} slice(f32[35840]{0:T(1024)} %collective-permute-done.1), slice={[0:32768]} | slice | bytes 262144 | tf_op jit(solution)/shard_map/slice | solution.py:113
  104.5 0.9 reshape.338
  105.5 1.3 pad_maximum_fusion
  106.7 1.0 pad_maximum_fusion.1
  107.7 7.8 %all-to-all-done.3 = f32[64,1,640]{2,1,0:T(1,128)} async-done(((f32[64,1,640]{2,1,0:T(1,128)}), f32[64,1,640]{2,1,0:T(1,128)}, u32[]{:S(2)}, u32[]{:S(2)}) %all-to-all-start.3) | async-done | bytes 163872 | tf_op jit(solution)/shard_map/all_to_all | solution.py:214
  115.6 1.9 %reduce.11 = f32[64,640]{1,0:T(8,128)S(1)} reduce(f32[64,1,640]{2,1,0:T(1,128)} %all-to-all-done.3, f32[]{:T(128)} %broadcast.448), dimensions={1}, to_apply=%all_to_all.65.reduce_sub_computation | reduce | bytes 327684 | tf_op jit(solution)/shard_map/all_to_all | solution.py:214
  118.6 1.0 copy-done.1
  119.6 3.8 %fusion.9 = f32[4,40,2048]{2,1,0:T(8,128)S(1)} fusion(f32[4,40,2048]{2,1,0:T(8,128)S(1)} %copy-done.1, f32[256,2048]{1,0:T(8,128)S(1)} %bitcast_dynamic-update-slice_fusion, f32[4]{0:T(128)S(1)} %copy-done.9, f32[4]{0:T(128)S(1)} %copy-done.10, f32[4,256,40]{2,1,0:T(8,128)S(1)} %bitcast.216, f32[256]{0:T(256)S(1)} %broadcast_bitcast_fusion), kind=kOutput, calls=%fused_computation.13 | convolution fusion | flops 525312000 | bytes 4883488 | tf_op jit(solution)/shard_map/ckx,ky->cxy/dot_general | solution.py:219
  124.9 1.6 %reshape.341 = f32[8,165,128]{2,1,0:T(8,128)} reshape(f32[8,2,40,264]{3,2,1,0:T(8,128)S(1)} %copy.96) | data formatting | bytes 1351680 | tf_op jit(solution)/shard_map/reshape | solution.py:232
  126.4 4.0 %all-to-all-start.4 = ((f32[8,165,128]{2,1,0:T(8,128)}), f32[8,165,128]{2,1,0:T(8,128)S(1)}, u32[]{:S(2)}, u32[]{:S(2)}) async-start(f32[8,165,128]{2,1,0:T(8,128)} %reshape.341), calls=%async_computation.4 | async-start | bytes 1376256 | tf_op jit(solution)/shard_map/all_to_all | solution.py:233
  130.4 10.6 %all-to-all-done.4 = f32[8,165,128]{2,1,0:T(8,128)S(1)} async-done(((f32[8,165,128]{2,1,0:T(8,128)}), f32[8,165,128]{2,1,0:T(8,128)S(1)}, u32[]{:S(2)}, u32[]{:S(2)}) %all-to-all-start.4) | async-done | bytes 675872 | tf_op jit(solution)/shard_map/all_to_all | solution.py:233
  (120 shorter events, 23.9 us)
Async XLA Ops:
  2.2 1.2 copy-start
  4.6 23.4 %copy-start.3 = (s32[32,256]{1,0:T(8,128)S(1)}, s32[32,256]{1,0:T(8,128)}, u32[]{:S(2)}) copy-start(s32[32,256]{1,0:T(8,128)} %param.16) | copy-start | bytes 98308
  4.6 23.4 %copy-start.4 = (s32[32,256]{1,0:T(8,128)S(1)}, s32[32,256]{1,0:T(8,128)}, u32[]{:S(2)}) copy-start(s32[32,256]{1,0:T(8,128)} %param.17) | copy-start | bytes 98308
  8.0 38.2 %all-to-all-start = ((f32[64,1,512]{2,1,0:T(1,128)}), f32[64,1,512]{2,1,0:T(1,128)S(1)}, u32[]{:S(2)}, u32[]{:S(2)}) async-start(f32[64,1,512]{2,1,0:T(1,128)} %reshape.354), calls=%async_computation | async-start | bytes 262144 | tf_op jit(solution)/shard_map/all_to_all | solution.py:173
  28.0 0.8 copy-start.5
  54.9 9.3 %all-to-all-start.1 = ((f32[8,1,256]{2,1,0:T(1,128)}), f32[8,1,256]{2,1,0:T(1,128)S(1)}, u32[]{:S(2)}, u32[]{:S(2)}) async-start(f32[8,1,256]{2,1,0:T(1,128)} %reshape.356), calls=%async_computation.1 | async-start | bytes 16384 | tf_op jit(solution)/shard_map/all_to_all | solution.py:189
  59.9 35.8 %collective-permute-start = (f32[35840]{0:T(1024)}, f32[35840]{0:T(1024)}, u32[]{:S(2)}, u32[]{:S(2)}) collective-permute-start(f32[35840]{0:T(1024)} %pad_maximum_fusion.2), channel_id=1, source_target_pairs={{0,8},{8,16},{16,24},{24,32},{32,40},{40,48},{48,56},{56,64},{64,7... | collective-permute-start | bytes 430088 | tf_op jit(solution)/shard_map/ppermute | solution.py:117
  66.2 8.8 %copy-start.2 = (f32[4,16,4,128]{3,1,2,0:T(8,128)S(1)}, f32[4,16,4,128]{3,1,2,0:T(8,128)}, u32[]{:S(2)}) copy-start(f32[4,16,4,128]{3,1,2,0:T(8,128)} %copy.136) | copy-start | bytes 393220
  67.0 14.2 %copy-start.8 = (pred[65]{0:T(512)(128)(4,1)S(1)}, pred[65]{0:T(512)(128)(4,1)}, u32[]{:S(2)}) copy-start(pred[65]{0:T(512)(128)(4,1)} %constant.40.clone.1) | copy-start | bytes 199
  70.1 9.9 %all-to-all-start.2 = ((f32[8,1,256]{2,1,0:T(1,128)}), f32[8,1,256]{2,1,0:T(1,128)S(1)}, u32[]{:S(2)}, u32[]{:S(2)}) async-start(f32[8,1,256]{2,1,0:T(1,128)} %reshape.358), calls=%async_computation.2 | async-start | bytes 16384 | tf_op jit(solution)/shard_map/all_to_all | solution.py:198
  75.6 20.8 %collective-permute-start.1 = (f32[35840]{0:T(1024)}, f32[35840]{0:T(1024)}, u32[]{:S(2)}, u32[]{:S(2)}) collective-permute-start(f32[35840]{0:T(1024)} %pad_maximum_fusion.3), channel_id=1, source_target_pairs={{8,0},{16,8},{24,16},{32,24},{40,32},{48,40},{56,48},{64,56},{72,6... | collective-permute-start | bytes 430088 | tf_op jit(solution)/shard_map/ppermute | solution.py:118
  89.5 26.0 %all-to-all-start.3 = ((f32[64,1,640]{2,1,0:T(1,128)}), f32[64,1,640]{2,1,0:T(1,128)}, u32[]{:S(2)}, u32[]{:S(2)}) async-start(f32[64,1,640]{2,1,0:T(1,128)} %reshape.360), calls=%async_computation.3 | async-start | bytes 327680 | tf_op jit(solution)/shard_map/all_to_all | solution.py:214
  97.9 8.9 %collective-permute-start.2 = (f32[3,40,4]{2,1,0:T(8,128)}, f32[3,40,4]{2,1,0:T(8,128)}, u32[]{:S(2)}, u32[]{:S(2)}) collective-permute-start(f32[3,40,4]{2,1,0:T(8,128)} %get-tuple-element.27), channel_id=1, source_target_pairs={{0,1},{1,2},{2,3},{3,4},{4,5},{5,6},{6,7},{8,9},{9,10},{10,11},{11... | collective-permute-start | bytes 5768 | tf_op jit(solution)/shard_map/ppermute | solution.py:21
  100.7 6.0 %collective-permute-start.3 = (f32[3,40,4]{2,1,0:T(8,128)}, f32[3,40,4]{2,1,0:T(8,128)}, u32[]{:S(2)}, u32[]{:S(2)}) collective-permute-start(f32[3,40,4]{2,1,0:T(8,128)} %get-tuple-element.28), channel_id=1, source_target_pairs={{1,0},{2,1},{3,2},{4,3},{5,4},{6,5},{7,6},{9,8},{10,9},{11,10},{12... | collective-permute-start | bytes 5768 | tf_op jit(solution)/shard_map/ppermute | solution.py:24
  117.5 1.1 copy-start.9
  117.5 1.1 copy-start.10
  118.3 1.3 copy-start.1
  119.6 3.8 %copy-start.6 = (f32[2,4]{1,0:T(2,128)S(1)}, f32[2,4]{1,0:T(2,128)}, u32[]{:S(2)}) copy-start(f32[2,4]{1,0:T(2,128)} %param.14) | copy-start | bytes 100
  126.4 14.8 %copy-start.7 = (f32[2]{0:T(128)S(1)}, f32[2]{0:T(128)}, u32[]{:S(2)}) copy-start(f32[2]{0:T(128)} %param.15) | copy-start | bytes 28
  126.4 14.6 %all-to-all-start.4 = ((f32[8,165,128]{2,1,0:T(8,128)}), f32[8,165,128]{2,1,0:T(8,128)S(1)}, u32[]{:S(2)}, u32[]{:S(2)}) async-start(f32[8,165,128]{2,1,0:T(8,128)} %reshape.341), calls=%async_computation.4 | async-start | bytes 1376256 | tf_op jit(solution)/shard_map/all_to_all | solution.py:233

commit v12 on v11

--- a/solution.py
+++ b/solution.py
@@ -168,14 +168,14 @@
         x_table = base_table(half + 1, all_rows)
     x_modes = x_table.shape[0] // 2
 
-    spec_y = jnp.einsum("cxy,ky->ckx", hidden, table, precision=high)
-    spec_y = spec_y.reshape(local_chan, 2, all_ymodes, row_count)
-    by_freq = lax.all_to_all(spec_y, "rows", split_axis=2, concat_axis=3, tiled=True)
+    spec_y = jnp.einsum("cxy,ky->kcx", hidden, table, precision=high)
+    spec_y = spec_y.reshape(2, all_ymodes, local_chan, row_count)
+    by_freq = lax.all_to_all(spec_y, "rows", split_axis=1, concat_axis=3, tiled=True)
     hidden_late, fields, by_freq = lax.optimization_barrier((hidden, fields, by_freq))
     hidden_win, fields = rows_halo_pair(hidden_late, fields, halo)
     fields = with_halo(fields, (("chan", 2),), halo)
     fields, hidden_win = lax.optimization_barrier((fields, hidden_win))
-    parts = jnp.einsum("caqx,kx->caqk", by_freq, x_table, precision=high)
+    parts = jnp.einsum("aqcx,kx->caqk", by_freq, x_table, precision=high)
     cos_part = parts[..., :x_modes]
     sin_part = parts[..., x_modes:]
     real_in = unfold_modes(

time: 144 us -> 144 us (level)
  no operation moved by 1% of the time
where the time goes in v12:
time: 144 us; the launch traced here: 143 us
  starting transfers between devices  48.3 us (34%)
  waiting for transfers between devices  36.6 us (25%)
  local copies, waits for them, and re-layouts  30 us (21%)
  other arithmetic  15.1 us (10%)
  matrix products  11.7 us (8%)
    all_to_all x1, starting transfers between devices, on_device(): lax.all_to_all(spec_y, 'rows', split_axis=1, concat_axis=3, tiled=True)  19.6 us
    all_to_all x1, waiting for transfers between devices, on_device(): lax.all_to_all(spec_y, 'rows', split_axis=1, concat_axis=3, tiled=True)  15.6 us
    unnamed x42, local copies, waits for them, and re-layouts  13.2 us
    all_to_all x1, waiting for transfers between devices, on_device(): lax.all_to_all(flat, 'chan', split_axis=0, concat_axis=0, tiled=True)  10.6 us
    all_to_all x1, waiting for transfers between devices, on_device(): lax.all_to_all(inverted, 'rows', split_axis=3, concat_axis=2, tiled=True)  7.82 us
    all_to_all x1, starting transfers between devices, on_device(): lax.all_to_all(inverted, 'rows', split_axis=3, concat_axis=2, tiled=True)  6.15 us
    dot_general x1, matrix products, on_device(): inverted = jnp.einsum('otqk,krj->otqrj', coef, row_windows, precision=high)  5.72 us
    all_to_all x1, starting transfers between devices, on_device(): lax.all_to_all(jnp.stack([real_out, imag_out], axis=2), 'chan', split_axi...  4.87 us
  transfers between devices with their start and end apart: 9, of which 5 were waited for; matrix products, arithmetic and copies ran while one was open for 19% of the time, Pallas kernels for 0%

profile of v12, /device:TPU:1, one launch (start us, length us, event | category | flops | bytes accessed | tf_op | source)
XLA Modules:
  0.0 142.9 jit_solution(1966961348577347858)
XLA Ops:
  3.4 1.2 fusion.6
  4.7 1.0 copy.60
  5.7 2.0 %reshape.354 = f32[64,1,512]{2,1,0:T(1,128)} reshape(f32[128,2,4,32]{3,2,1,0:T(4,128)} %bitcast.190) | data formatting | bytes 262144
  7.8 19.6 %all-to-all-start = ((f32[64,1,512]{2,1,0:T(1,128)}), f32[64,1,512]{2,1,0:T(1,128)S(1)}, u32[]{:S(2)}, u32[]{:S(2)}) async-start(f32[64,1,512]{2,1,0:T(1,128)} %reshape.354), calls=%async_computation | async-start | bytes 262144 | tf_op jit(solution)/shard_map/all_to_all | solution.py:173
  28.6 1.7 %maximum_bitcast_fusion = f32[256,64,40,1,1]{0,1,2,3,4:T(8,128)} fusion(f32[128,64,40]{0,1,2:T(8,128)S(1)} %get-tuple-element.30, f32[128,64,40]{0,1,2:T(8,128)S(1)} %get-tuple-element.29), kind=kLoop, calls=%fused_computation | loop fusion | flops 655360 | bytes 5242880 | tf_op jit(solution)/shard_map/concatenate | solution.py:54
  30.3 15.6 %all-to-all-done = f32[64,1,512]{2,1,0:T(1,128)S(1)} async-done(((f32[64,1,512]{2,1,0:T(1,128)}), f32[64,1,512]{2,1,0:T(1,128)S(1)}, u32[]{:S(2)}, u32[]{:S(2)}) %all-to-all-start) | async-done | bytes 131104 | tf_op jit(solution)/shard_map/all_to_all | solution.py:173
  47.4 1.1 reshape.355
  48.5 1.1 copy.61
  50.5 1.3 all_to_all.56
  51.8 1.0 fusion.17
  54.6 4.2 %all-to-all-start.1 = ((f32[8,1,256]{2,1,0:T(1,128)}), f32[8,1,256]{2,1,0:T(1,128)S(1)}, u32[]{:S(2)}, u32[]{:S(2)}) async-start(f32[8,1,256]{2,1,0:T(1,128)} %reshape.356), calls=%async_computation.1 | async-start | bytes 16384 | tf_op jit(solution)/shard_map/all_to_all | solution.py:189
  59.5 3.1 %collective-permute-start = (f32[35840]{0:T(1024)}, f32[35840]{0:T(1024)}, u32[]{:S(2)}, u32[]{:S(2)}) collective-permute-start(f32[35840]{0:T(1024)} %pad_maximum_fusion.2), channel_id=1, source_target_pairs={{0,8},{8,16},{16,24},{24,32},{32,40},{40,48},{48,56},{56,64},{64,7... | collective-permute-start | bytes 430088 | tf_op jit(solution)/shard_map/ppermute | solution.py:117
  66.8 1.7 %fusion.22 = (f32[2,16,32]{2,1,0:T(8,128)S(1)}, f32[2,16,32]{2,1,0:T(8,128)S(1)}, f32[2,16,32]{2,1,0:T(8,128)S(1)}, f32[2,16,32]{2,1,0:T(8,128)S(1)}) fusion(f32[2,2,16,32,32]{4,3,2,1,0:T(8,128)} %param.11, f32[2,16,32]{2,1,0:T(8,128)S(1)} %copy.100, f32[2,16,32]{2,1,0:T(8,128)S(1)} %copy.99), kind=kLoop, calls=%fused_computation.42 | loop fusion | flops 258048 | bytes 286720
  69.7 4.9 %all-to-all-start.2 = ((f32[8,1,256]{2,1,0:T(1,128)}), f32[8,1,256]{2,1,0:T(1,128)S(1)}, u32[]{:S(2)}, u32[]{:S(2)}) async-start(f32[8,1,256]{2,1,0:T(1,128)} %reshape.358), calls=%async_computation.2 | async-start | bytes 16384 | tf_op jit(solution)/shard_map/all_to_all | solution.py:198
  75.2 2.4 %collective-permute-start.1 = (f32[35840]{0:T(1024)}, f32[35840]{0:T(1024)}, u32[]{:S(2)}, u32[]{:S(2)}) collective-permute-start(f32[35840]{0:T(1024)} %pad_maximum_fusion.3), channel_id=1, source_target_pairs={{8,0},{16,8},{24,16},{32,24},{40,32},{48,40},{56,48},{64,56},{72,6... | collective-permute-start | bytes 430088 | tf_op jit(solution)/shard_map/ppermute | solution.py:118
  77.6 2.0 %all-to-all-done.2 = f32[8,1,256]{2,1,0:T(1,128)S(1)} async-done(((f32[8,1,256]{2,1,0:T(1,128)}), f32[8,1,256]{2,1,0:T(1,128)S(1)}, u32[]{:S(2)}, u32[]{:S(2)}) %all-to-all-start.2) | async-done | bytes 8224 | tf_op jit(solution)/shard_map/all_to_all | solution.py:198
  81.0 5.7 %fusion.104 = f32[64,2,2,4,40]{4,3,2,1,0:T(4,128)} fusion(f32[256,64,40,1,1]{0,1,2,3,4:T(8,128)} %maximum_bitcast_fusion, f32[4,1,2,256]{3,0,2,1:T(4,128)S(1)} %fusion.93, f32[4,1,2,256]{3,0,2,1:T(4,128)S(1)} %fusion.94), kind=kOutput, calls=%fused_computation.203 | convolution fusion | flops 62918656 | bytes 2801664 | tf_op jit(solution)/shard_map/otqk,krj->otqrj/dot_general | solution.py:213
  86.7 2.4 %reshape.360 = f32[64,1,640]{2,1,0:T(1,128)} reshape(f32[64,2,2,4,40]{4,3,2,1,0:T(4,128)} %fusion.104) | data formatting | bytes 327680
  89.1 6.1 %all-to-all-start.3 = ((f32[64,1,640]{2,1,0:T(1,128)}), f32[64,1,640]{2,1,0:T(1,128)}, u32[]{:S(2)}, u32[]{:S(2)}) async-start(f32[64,1,640]{2,1,0:T(1,128)} %reshape.360), calls=%async_computation.3 | async-start | bytes 327680 | tf_op jit(solution)/shard_map/all_to_all | solution.py:214
  97.5 2.8 %collective-permute-start.2 = (f32[3,40,4]{2,1,0:T(8,128)}, f32[3,40,4]{2,1,0:T(8,128)}, u32[]{:S(2)}, u32[]{:S(2)}) collective-permute-start(f32[3,40,4]{2,1,0:T(8,128)} %get-tuple-element.27), channel_id=1, source_target_pairs={{0,1},{1,2},{2,3},{3,4},{4,5},{5,6},{6,7},{8,9},{9,10},{10,11},{11... | collective-permute-start | bytes 5768 | tf_op jit(solution)/shard_map/ppermute | solution.py:21
  100.3 1.3 collective-permute-start.3
  102.6 1.6 %slice.325 = f32[32768]{0:T(1024)} slice(f32[35840]{0:T(1024)} %collective-permute-done.1), slice={[0:32768]} | slice | bytes 262144 | tf_op jit(solution)/shard_map/slice | solution.py:113
  104.1 0.9 reshape.338
  105.1 1.3 pad_maximum_fusion
  106.3 1.0 pad_maximum_fusion.1
  107.4 7.8 %all-to-all-done.3 = f32[64,1,640]{2,1,0:T(1,128)} async-done(((f32[64,1,640]{2,1,0:T(1,128)}), f32[64,1,640]{2,1,0:T(1,128)}, u32[]{:S(2)}, u32[]{:S(2)}) %all-to-all-start.3) | async-done | bytes 163872 | tf_op jit(solution)/shard_map/all_to_all | solution.py:214
  115.2 1.9 %reduce.11 = f32[64,640]{1,0:T(8,128)S(1)} reduce(f32[64,1,640]{2,1,0:T(1,128)} %all-to-all-done.3, f32[]{:T(128)} %broadcast.448), dimensions={1}, to_apply=%all_to_all.65.reduce_sub_computation | reduce | bytes 327684 | tf_op jit(solution)/shard_map/all_to_all | solution.py:214
  118.2 1.0 copy-done.1
  119.2 3.8 %fusion.9 = f32[4,40,2048]{2,1,0:T(8,128)S(1)} fusion(f32[4,40,2048]{2,1,0:T(8,128)S(1)} %copy-done.1, f32[256,2048]{1,0:T(8,128)S(1)} %bitcast_dynamic-update-slice_fusion, f32[4]{0:T(128)S(1)} %copy-done.9, f32[4]{0:T(128)S(1)} %copy-done.10, f32[4,256,40]{2,1,0:T(8,128)S(1)} %bitcast.196, f32[256]{0:T(256)S(1)} %broadcast_bitcast_fusion), kind=kOutput, calls=%fused_computation.13 | convolution fusion | flops 525312000 | bytes 4883488 | tf_op jit(solution)/shard_map/ckx,ky->cxy/dot_general | solution.py:219
  124.5 1.6 %reshape.341 = f32[8,165,128]{2,1,0:T(8,128)} reshape(f32[8,2,40,264]{3,2,1,0:T(8,128)S(1)} %copy.70) | data formatting | bytes 1351680 | tf_op jit(solution)/shard_map/reshape | solution.py:232
  126.0 4.0 %all-to-all-start.4 = ((f32[8,165,128]{2,1,0:T(8,128)}), f32[8,165,128]{2,1,0:T(8,128)S(1)}, u32[]{:S(2)}, u32[]{:S(2)}) async-start(f32[8,165,128]{2,1,0:T(8,128)} %reshape.341), calls=%async_computation.4 | async-start | bytes 1376256 | tf_op jit(solution)/shard_map/all_to_all | solution.py:233
  130.0 10.6 %all-to-all-done.4 = f32[8,165,128]{2,1,0:T(8,128)S(1)} async-done(((f32[8,165,128]{2,1,0:T(8,128)}), f32[8,165,128]{2,1,0:T(8,128)S(1)}, u32[]{:S(2)}, u32[]{:S(2)}) %all-to-all-start.4) | async-done | bytes 675872 | tf_op jit(solution)/shard_map/all_to_all | solution.py:233
  (119 shorter events, 23.9 us)
Async XLA Ops:
  2.2 1.2 copy-start
  4.6 23.2 %copy-start.3 = (s32[32,256]{1,0:T(8,128)S(1)}, s32[32,256]{1,0:T(8,128)}, u32[]{:S(2)}) copy-start(s32[32,256]{1,0:T(8,128)} %param.16) | copy-start | bytes 98308
  4.6 23.2 %copy-start.4 = (s32[32,256]{1,0:T(8,128)S(1)}, s32[32,256]{1,0:T(8,128)}, u32[]{:S(2)}) copy-start(s32[32,256]{1,0:T(8,128)} %param.17) | copy-start | bytes 98308
  7.8 38.2 %all-to-all-start = ((f32[64,1,512]{2,1,0:T(1,128)}), f32[64,1,512]{2,1,0:T(1,128)S(1)}, u32[]{:S(2)}, u32[]{:S(2)}) async-start(f32[64,1,512]{2,1,0:T(1,128)} %reshape.354), calls=%async_computation | async-start | bytes 262144 | tf_op jit(solution)/shard_map/all_to_all | solution.py:173
  27.8 0.8 copy-start.5
  54.6 9.3 %all-to-all-start.1 = ((f32[8,1,256]{2,1,0:T(1,128)}), f32[8,1,256]{2,1,0:T(1,128)S(1)}, u32[]{:S(2)}, u32[]{:S(2)}) async-start(f32[8,1,256]{2,1,0:T(1,128)} %reshape.356), calls=%async_computation.1 | async-start | bytes 16384 | tf_op jit(solution)/shard_map/all_to_all | solution.py:189
  59.5 35.8 %collective-permute-start = (f32[35840]{0:T(1024)}, f32[35840]{0:T(1024)}, u32[]{:S(2)}, u32[]{:S(2)}) collective-permute-start(f32[35840]{0:T(1024)} %pad_maximum_fusion.2), channel_id=1, source_target_pairs={{0,8},{8,16},{16,24},{24,32},{32,40},{40,48},{48,56},{56,64},{64,7... | collective-permute-start | bytes 430088 | tf_op jit(solution)/shard_map/ppermute | solution.py:117
  65.8 8.8 %copy-start.2 = (f32[4,16,4,128]{3,1,2,0:T(8,128)S(1)}, f32[4,16,4,128]{3,1,2,0:T(8,128)}, u32[]{:S(2)}) copy-start(f32[4,16,4,128]{3,1,2,0:T(8,128)} %copy.107) | copy-start | bytes 393220
  66.6 14.2 %copy-start.8 = (pred[65]{0:T(512)(128)(4,1)S(1)}, pred[65]{0:T(512)(128)(4,1)}, u32[]{:S(2)}) copy-start(pred[65]{0:T(512)(128)(4,1)} %constant.40.clone.1) | copy-start | bytes 199
  69.7 9.9 %all-to-all-start.2 = ((f32[8,1,256]{2,1,0:T(1,128)}), f32[8,1,256]{2,1,0:T(1,128)S(1)}, u32[]{:S(2)}, u32[]{:S(2)}) async-start(f32[8,1,256]{2,1,0:T(1,128)} %reshape.358), calls=%async_computation.2 | async-start | bytes 16384 | tf_op jit(solution)/shard_map/all_to_all | solution.py:198
  75.2 20.8 %collective-permute-start.1 = (f32[35840]{0:T(1024)}, f32[35840]{0:T(1024)}, u32[]{:S(2)}, u32[]{:S(2)}) collective-permute-start(f32[35840]{0:T(1024)} %pad_maximum_fusion.3), channel_id=1, source_target_pairs={{8,0},{16,8},{24,16},{32,24},{40,32},{48,40},{56,48},{64,56},{72,6... | collective-permute-start | bytes 430088 | tf_op jit(solution)/shard_map/ppermute | solution.py:118
  89.1 26.0 %all-to-all-start.3 = ((f32[64,1,640]{2,1,0:T(1,128)}), f32[64,1,640]{2,1,0:T(1,128)}, u32[]{:S(2)}, u32[]{:S(2)}) async-start(f32[64,1,640]{2,1,0:T(1,128)} %reshape.360), calls=%async_computation.3 | async-start | bytes 327680 | tf_op jit(solution)/shard_map/all_to_all | solution.py:214
  97.5 8.9 %collective-permute-start.2 = (f32[3,40,4]{2,1,0:T(8,128)}, f32[3,40,4]{2,1,0:T(8,128)}, u32[]{:S(2)}, u32[]{:S(2)}) collective-permute-start(f32[3,40,4]{2,1,0:T(8,128)} %get-tuple-element.27), channel_id=1, source_target_pairs={{0,1},{1,2},{2,3},{3,4},{4,5},{5,6},{6,7},{8,9},{9,10},{10,11},{11... | collective-permute-start | bytes 5768 | tf_op jit(solution)/shard_map/ppermute | solution.py:21
  100.3 6.0 %collective-permute-start.3 = (f32[3,40,4]{2,1,0:T(8,128)}, f32[3,40,4]{2,1,0:T(8,128)}, u32[]{:S(2)}, u32[]{:S(2)}) collective-permute-start(f32[3,40,4]{2,1,0:T(8,128)} %get-tuple-element.28), channel_id=1, source_target_pairs={{1,0},{2,1},{3,2},{4,3},{5,4},{6,5},{7,6},{9,8},{10,9},{11,10},{12... | collective-permute-start | bytes 5768 | tf_op jit(solution)/shard_map/ppermute | solution.py:24
  117.1 1.1 copy-start.9
  117.1 1.1 copy-start.10
  117.9 1.3 copy-start.1
  119.2 3.8 %copy-start.6 = (f32[2,4]{1,0:T(2,128)S(1)}, f32[2,4]{1,0:T(2,128)}, u32[]{:S(2)}) copy-start(f32[2,4]{1,0:T(2,128)} %param.14) | copy-start | bytes 100
  126.0 14.8 %copy-start.7 = (f32[2]{0:T(128)S(1)}, f32[2]{0:T(128)}, u32[]{:S(2)}) copy-start(f32[2]{0:T(128)} %param.15) | copy-start | bytes 28
  126.0 14.6 %all-to-all-start.4 = ((f32[8,165,128]{2,1,0:T(8,128)}), f32[8,165,128]{2,1,0:T(8,128)S(1)}, u32[]{:S(2)}, u32[]{:S(2)}) async-start(f32[8,165,128]{2,1,0:T(8,128)} %reshape.341), calls=%async_computation.4 | async-start | bytes 1376256 | tf_op jit(solution)/shard_map/all_to_all | solution.py:233

commit v13 on v12

--- a/solution.py
+++ b/solution.py
@@ -210,8 +210,8 @@
     )
     coef = jnp.stack([coef_real, coef_imag], axis=1)
     row_windows = window_table(x_modes, all_rows, row_devices, row_count, halo)
-    inverted = jnp.einsum("otqk,krj->otqrj", coef, row_windows, precision=high)
-    inverted = lax.all_to_all(inverted, "rows", split_axis=3, concat_axis=2, tiled=True)
+    inverted = jnp.einsum("otqk,krj->rotqj", coef, row_windows, precision=high)
+    inverted = lax.all_to_all(inverted, "rows", split_axis=0, concat_axis=3, tiled=True)
     y_weights = jnp.where(jnp.arange(all_ymodes) == 0, 1.0, 2.0).astype(jnp.float32) * norm_scale
     inverted = inverted.reshape(local_chan, 2, all_ymodes, win_rows) * y_weights[:, None]
     inverted = inverted.reshape(local_chan, 2 * all_ymodes, win_rows)

time: 144 us -> 143 us (level)
    concatenate x1 -> x0, other arithmetic: 1.72 us -> none  [window_table(): return jnp.concatenate([cos_all, -sin_all])]
    sub x1, other arithmetic: 0.38 us -> 1.82 us  [window_table(): cos_all = cos_hi * cos_lo - sin_hi * sin_lo]
where the time goes in v13:
time: 143 us; the launch traced here: 142 us
  starting transfers between devices  48.1 us (34%)
  waiting for transfers between devices  37.4 us (26%)
  local copies, waits for them, and re-layouts  29.6 us (21%)
  other arithmetic  14.8 us (10%)
  matrix products  11.1 us (8%)
    all_to_all x1, starting transfers between devices, on_device(): lax.all_to_all(spec_y, 'rows', split_axis=1, concat_axis=3, tiled=True)  19.6 us
    all_to_all x1, waiting for transfers between devices, on_device(): lax.all_to_all(spec_y, 'rows', split_axis=1, concat_axis=3, tiled=True)  16.3 us
    unnamed x42, local copies, waits for them, and re-layouts  12.9 us
    all_to_all x1, waiting for transfers between devices, on_device(): lax.all_to_all(flat, 'chan', split_axis=0, concat_axis=0, tiled=True)  10.6 us
    all_to_all x1, waiting for transfers between devices, on_device(): lax.all_to_all(inverted, 'rows', split_axis=0, concat_axis=3, tiled=True)  7.82 us
    all_to_all x1, starting transfers between devices, on_device(): lax.all_to_all(inverted, 'rows', split_axis=0, concat_axis=3, tiled=True)  6.33 us
    dot_general x1, matrix products, on_device(): inverted = jnp.einsum('otqk,krj->rotqj', coef, row_windows, precision=high)  5.07 us
    all_to_all x1, starting transfers between devices, on_device(): lax.all_to_all(jnp.stack([real_out, imag_out], axis=2), 'chan', split_axi...  4.88 us
  transfers between devices with their start and end apart: 9, of which 5 were waited for; matrix products, arithmetic and copies ran while one was open for 19% of the time, Pallas kernels for 0%

profile of v13, /device:TPU:1, one launch (start us, length us, event | category | flops | bytes accessed | tf_op | source)
XLA Modules:
  0.0 142.3 jit_solution(11638190444434646438)
XLA Ops:
  3.4 1.2 fusion.7
  4.7 1.0 copy.47
  5.7 2.0 %reshape.354 = f32[64,1,512]{2,1,0:T(1,128)} reshape(f32[128,2,4,32]{3,2,1,0:T(4,128)} %bitcast.201) | data formatting | bytes 262144
  7.8 19.6 %all-to-all-start = ((f32[64,1,512]{2,1,0:T(1,128)}), f32[64,1,512]{2,1,0:T(1,128)S(1)}, u32[]{:S(2)}, u32[]{:S(2)}) async-start(f32[64,1,512]{2,1,0:T(1,128)} %reshape.354), calls=%async_computation | async-start | bytes 262144 | tf_op jit(solution)/shard_map/all_to_all | solution.py:173
  27.9 1.8 %multiply_subtract_fusion = (f32[128,64,40]{0,2,1:T(8,128)}, f32[128,64,40]{0,2,1:T(8,128)}) fusion(f32[128,40]{0,1:T(8,128)S(1)} %get-tuple-element.50, f32[128,64]{0,1:T(8,128)S(1)} %get-tuple-element.48, f32[128,40]{0,1:T(8,128)S(1)} %get-tuple-element.49, f32[128,64]{0,1:T(8,128)S(1)} %get-tuple-element.47), kind=kLoop, calls=%fused_computation.30 | loop fusion | flops 2293760 | bytes 2727936 | tf_op jit(solution)/shard_map/sub | solution.py:52
  29.7 16.3 %all-to-all-done = f32[64,1,512]{2,1,0:T(1,128)S(1)} async-done(((f32[64,1,512]{2,1,0:T(1,128)}), f32[64,1,512]{2,1,0:T(1,128)S(1)}, u32[]{:S(2)}, u32[]{:S(2)}) %all-to-all-start) | async-done | bytes 131104 | tf_op jit(solution)/shard_map/all_to_all | solution.py:173
  47.4 1.1 reshape.355
  48.5 1.1 copy.48
  50.5 1.3 all_to_all.56
  51.8 1.0 fusion.19
  54.6 4.2 %all-to-all-start.1 = ((f32[8,1,256]{2,1,0:T(1,128)}), f32[8,1,256]{2,1,0:T(1,128)S(1)}, u32[]{:S(2)}, u32[]{:S(2)}) async-start(f32[8,1,256]{2,1,0:T(1,128)} %reshape.356), calls=%async_computation.1 | async-start | bytes 16384 | tf_op jit(solution)/shard_map/all_to_all | solution.py:189
  59.5 3.1 %collective-permute-start = (f32[35840]{0:T(1024)}, f32[35840]{0:T(1024)}, u32[]{:S(2)}, u32[]{:S(2)}) collective-permute-start(f32[35840]{0:T(1024)} %pad_maximum_fusion.2), channel_id=1, source_target_pairs={{0,8},{8,16},{16,24},{24,32},{32,40},{40,48},{48,56},{56,64},{64,7... | collective-permute-start | bytes 430088 | tf_op jit(solution)/shard_map/ppermute | solution.py:117
  66.8 1.7 %fusion.24 = (f32[2,16,32]{2,1,0:T(8,128)S(1)}, f32[2,16,32]{2,1,0:T(8,128)S(1)}, f32[2,16,32]{2,1,0:T(8,128)S(1)}, f32[2,16,32]{2,1,0:T(8,128)S(1)}) fusion(f32[2,2,16,32,32]{4,3,2,1,0:T(8,128)} %param.11, f32[2,16,32]{2,1,0:T(8,128)S(1)} %copy.85, f32[2,16,32]{2,1,0:T(8,128)S(1)} %copy.84), kind=kLoop, calls=%fused_computation.44 | loop fusion | flops 258048 | bytes 286720
  69.7 4.9 %all-to-all-start.2 = ((f32[8,1,256]{2,1,0:T(1,128)}), f32[8,1,256]{2,1,0:T(1,128)S(1)}, u32[]{:S(2)}, u32[]{:S(2)}) async-start(f32[8,1,256]{2,1,0:T(1,128)} %reshape.358), calls=%async_computation.2 | async-start | bytes 16384 | tf_op jit(solution)/shard_map/all_to_all | solution.py:198
  75.2 2.2 %collective-permute-start.1 = (f32[35840]{0:T(1024)}, f32[35840]{0:T(1024)}, u32[]{:S(2)}, u32[]{:S(2)}) collective-permute-start(f32[35840]{0:T(1024)} %pad_maximum_fusion.3), channel_id=1, source_target_pairs={{8,0},{16,8},{24,16},{32,24},{40,32},{48,40},{56,48},{64,56},{72,6... | collective-permute-start | bytes 430088 | tf_op jit(solution)/shard_map/ppermute | solution.py:118
  77.4 2.2 %all-to-all-done.2 = f32[8,1,256]{2,1,0:T(1,128)S(1)} async-done(((f32[8,1,256]{2,1,0:T(1,128)}), f32[8,1,256]{2,1,0:T(1,128)S(1)}, u32[]{:S(2)}, u32[]{:S(2)}) %all-to-all-start.2) | async-done | bytes 8224 | tf_op jit(solution)/shard_map/all_to_all | solution.py:198
  81.0 5.1 %fusion.106 = f32[64,2,2,4,40]{4,3,2,1,0:T(4,128)} fusion(f32[4,1,2,256]{3,0,2,1:T(4,128)S(1)} %fusion.95, f32[4,1,2,256]{3,0,2,1:T(4,128)S(1)} %fusion.96, f32[128,64,40]{0,2,1:T(8,128)} %get-tuple-element.30, f32[128,64,40]{0,2,1:T(8,128)} %get-tuple-element.29), kind=kOutput, calls=%fused_computation.205 | convolution fusion | flops 63574016 | bytes 2801664 | tf_op jit(solution)/shard_map/otqk,krj->rotqj/dot_general | solution.py:213
  86.0 2.4 %reshape.360 = f32[64,1,640]{2,1,0:T(1,128)} reshape(f32[64,2,2,4,40]{4,3,2,1,0:T(4,128)} %fusion.106) | data formatting | bytes 327680
  88.5 6.3 %all-to-all-start.3 = ((f32[64,1,640]{2,1,0:T(1,128)}), f32[64,1,640]{2,1,0:T(1,128)}, u32[]{:S(2)}, u32[]{:S(2)}) async-start(f32[64,1,640]{2,1,0:T(1,128)} %reshape.360), calls=%async_computation.3 | async-start | bytes 327680 | tf_op jit(solution)/shard_map/all_to_all | solution.py:214
  97.0 2.8 %collective-permute-start.2 = (f32[3,40,4]{2,1,0:T(8,128)}, f32[3,40,4]{2,1,0:T(8,128)}, u32[]{:S(2)}, u32[]{:S(2)}) collective-permute-start(f32[3,40,4]{2,1,0:T(8,128)} %get-tuple-element.27), channel_id=1, source_target_pairs={{0,1},{1,2},{2,3},{3,4},{4,5},{5,6},{6,7},{8,9},{9,10},{10,11},{11... | collective-permute-start | bytes 5768 | tf_op jit(solution)/shard_map/ppermute | solution.py:21
  99.8 1.3 collective-permute-start.3
  102.1 1.6 %slice.325 = f32[32768]{0:T(1024)} slice(f32[35840]{0:T(1024)} %collective-permute-done.1), slice={[0:32768]} | slice | bytes 262144 | tf_op jit(solution)/shard_map/slice | solution.py:113
  103.7 0.9 reshape.338
  104.6 1.3 pad_maximum_fusion
  105.9 1.0 pad_maximum_fusion.1
  106.9 7.8 %all-to-all-done.3 = f32[64,1,640]{2,1,0:T(1,128)} async-done(((f32[64,1,640]{2,1,0:T(1,128)}), f32[64,1,640]{2,1,0:T(1,128)}, u32[]{:S(2)}, u32[]{:S(2)}) %all-to-all-start.3) | async-done | bytes 163872 | tf_op jit(solution)/shard_map/all_to_all | solution.py:214
  114.7 1.9 %reduce.11 = f32[64,640]{1,0:T(8,128)S(1)} reduce(f32[64,1,640]{2,1,0:T(1,128)} %all-to-all-done.3, f32[]{:T(128)} %broadcast.448), dimensions={1}, to_apply=%all_to_all.65.reduce_sub_computation | reduce | bytes 327684 | tf_op jit(solution)/shard_map/all_to_all | solution.py:214
  117.8 1.0 copy-done.1
  118.8 3.8 %fusion.10 = f32[4,40,2048]{2,1,0:T(8,128)S(1)} fusion(f32[4,40,2048]{2,1,0:T(8,128)S(1)} %copy-done.1, f32[256,2048]{1,0:T(8,128)S(1)} %bitcast_dynamic-update-slice_fusion, f32[4]{0:T(128)S(1)} %copy-done.9, f32[4]{0:T(128)S(1)} %copy-done.10, f32[4,256,40]{2,1,0:T(8,128)S(1)} %bitcast.207, f32[256]{0:T(256)S(1)} %broadcast_bitcast_fusion), kind=kOutput, calls=%fused_computation.14 | convolution fusion | flops 525312000 | bytes 4883488 | tf_op jit(solution)/shard_map/ckx,ky->cxy/dot_general | solution.py:219
  124.0 1.6 %reshape.341 = f32[8,165,128]{2,1,0:T(8,128)} reshape(f32[8,2,40,264]{3,2,1,0:T(8,128)S(1)} %copy.56) | data formatting | bytes 1351680 | tf_op jit(solution)/shard_map/reshape | solution.py:232
  125.6 3.8 %all-to-all-start.4 = ((f32[8,165,128]{2,1,0:T(8,128)}), f32[8,165,128]{2,1,0:T(8,128)S(1)}, u32[]{:S(2)}, u32[]{:S(2)}) async-start(f32[8,165,128]{2,1,0:T(8,128)} %reshape.341), calls=%async_computation.4 | async-start | bytes 1376256 | tf_op jit(solution)/shard_map/all_to_all | solution.py:233
  129.4 10.6 %all-to-all-done.4 = f32[8,165,128]{2,1,0:T(8,128)S(1)} async-done(((f32[8,165,128]{2,1,0:T(8,128)}), f32[8,165,128]{2,1,0:T(8,128)S(1)}, u32[]{:S(2)}, u32[]{:S(2)}) %all-to-all-start.4) | async-done | bytes 675872 | tf_op jit(solution)/shard_map/all_to_all | solution.py:233
  (118 shorter events, 23.2 us)
Async XLA Ops:
  2.2 1.2 copy-start
  4.6 23.2 %copy-start.3 = (s32[32,256]{1,0:T(8,128)S(1)}, s32[32,256]{1,0:T(8,128)}, u32[]{:S(2)}) copy-start(s32[32,256]{1,0:T(8,128)} %param.16) | copy-start | bytes 98308
  4.6 23.2 %copy-start.4 = (s32[32,256]{1,0:T(8,128)S(1)}, s32[32,256]{1,0:T(8,128)}, u32[]{:S(2)}) copy-start(s32[32,256]{1,0:T(8,128)} %param.17) | copy-start | bytes 98308
  4.6 23.2 %copy-start.5 = (f32[32,256]{1,0:T(8,128)S(1)}, f32[32,256]{1,0:T(8,128)}, u32[]{:S(2)}) copy-start(f32[32,256]{1,0:T(8,128)} %param.10) | copy-start | bytes 98308
  7.8 38.2 %all-to-all-start = ((f32[64,1,512]{2,1,0:T(1,128)}), f32[64,1,512]{2,1,0:T(1,128)S(1)}, u32[]{:S(2)}, u32[]{:S(2)}) async-start(f32[64,1,512]{2,1,0:T(1,128)} %reshape.354), calls=%async_computation | async-start | bytes 262144 | tf_op jit(solution)/shard_map/all_to_all | solution.py:173
  54.6 9.3 %all-to-all-start.1 = ((f32[8,1,256]{2,1,0:T(1,128)}), f32[8,1,256]{2,1,0:T(1,128)S(1)}, u32[]{:S(2)}, u32[]{:S(2)}) async-start(f32[8,1,256]{2,1,0:T(1,128)} %reshape.356), calls=%async_computation.1 | async-start | bytes 16384 | tf_op jit(solution)/shard_map/all_to_all | solution.py:189
  59.5 35.3 %collective-permute-start = (f32[35840]{0:T(1024)}, f32[35840]{0:T(1024)}, u32[]{:S(2)}, u32[]{:S(2)}) collective-permute-start(f32[35840]{0:T(1024)} %pad_maximum_fusion.2), channel_id=1, source_target_pairs={{0,8},{8,16},{16,24},{24,32},{32,40},{40,48},{48,56},{56,64},{64,7... | collective-permute-start | bytes 430088 | tf_op jit(solution)/shard_map/ppermute | solution.py:117
  65.8 8.8 %copy-start.2 = (f32[4,16,4,128]{3,1,2,0:T(8,128)S(1)}, f32[4,16,4,128]{3,1,2,0:T(8,128)}, u32[]{:S(2)}) copy-start(f32[4,16,4,128]{3,1,2,0:T(8,128)} %copy.92) | copy-start | bytes 393220
  66.6 14.2 %copy-start.8 = (pred[65]{0:T(512)(128)(4,1)S(1)}, pred[65]{0:T(512)(128)(4,1)}, u32[]{:S(2)}) copy-start(pred[65]{0:T(512)(128)(4,1)} %constant.46.clone.1) | copy-start | bytes 199
  69.7 9.9 %all-to-all-start.2 = ((f32[8,1,256]{2,1,0:T(1,128)}), f32[8,1,256]{2,1,0:T(1,128)S(1)}, u32[]{:S(2)}, u32[]{:S(2)}) async-start(f32[8,1,256]{2,1,0:T(1,128)} %reshape.358), calls=%async_computation.2 | async-start | bytes 16384 | tf_op jit(solution)/shard_map/all_to_all | solution.py:198
  75.2 20.3 %collective-permute-start.1 = (f32[35840]{0:T(1024)}, f32[35840]{0:T(1024)}, u32[]{:S(2)}, u32[]{:S(2)}) collective-permute-start(f32[35840]{0:T(1024)} %pad_maximum_fusion.3), channel_id=1, source_target_pairs={{8,0},{16,8},{24,16},{32,24},{40,32},{48,40},{56,48},{64,56},{72,6... | collective-permute-start | bytes 430088 | tf_op jit(solution)/shard_map/ppermute | solution.py:118
  88.5 26.2 %all-to-all-start.3 = ((f32[64,1,640]{2,1,0:T(1,128)}), f32[64,1,640]{2,1,0:T(1,128)}, u32[]{:S(2)}, u32[]{:S(2)}) async-start(f32[64,1,640]{2,1,0:T(1,128)} %reshape.360), calls=%async_computation.3 | async-start | bytes 327680 | tf_op jit(solution)/shard_map/all_to_all | solution.py:214
  97.0 8.8 %collective-permute-start.2 = (f32[3,40,4]{2,1,0:T(8,128)}, f32[3,40,4]{2,1,0:T(8,128)}, u32[]{:S(2)}, u32[]{:S(2)}) collective-permute-start(f32[3,40,4]{2,1,0:T(8,128)} %get-tuple-element.27), channel_id=1, source_target_pairs={{0,1},{1,2},{2,3},{3,4},{4,5},{5,6},{6,7},{8,9},{9,10},{10,11},{11... | collective-permute-start | bytes 5768 | tf_op jit(solution)/shard_map/ppermute | solution.py:21
  99.8 6.0 %collective-permute-start.3 = (f32[3,40,4]{2,1,0:T(8,128)}, f32[3,40,4]{2,1,0:T(8,128)}, u32[]{:S(2)}, u32[]{:S(2)}) collective-permute-start(f32[3,40,4]{2,1,0:T(8,128)} %get-tuple-element.28), channel_id=1, source_target_pairs={{1,0},{2,1},{3,2},{4,3},{5,4},{6,5},{7,6},{9,8},{10,9},{11,10},{12... | collective-permute-start | bytes 5768 | tf_op jit(solution)/shard_map/ppermute | solution.py:24
  116.6 1.1 copy-start.9
  116.6 1.1 copy-start.10
  117.4 1.3 copy-start.1
  118.8 3.8 %copy-start.6 = (f32[2,4]{1,0:T(2,128)S(1)}, f32[2,4]{1,0:T(2,128)}, u32[]{:S(2)}) copy-start(f32[2,4]{1,0:T(2,128)} %param.14) | copy-start | bytes 100
  125.6 14.6 %copy-start.7 = (f32[2]{0:T(128)S(1)}, f32[2]{0:T(128)}, u32[]{:S(2)}) copy-start(f32[2]{0:T(128)} %param.15) | copy-start | bytes 28
  125.6 14.4 %all-to-all-start.4 = ((f32[8,165,128]{2,1,0:T(8,128)}), f32[8,165,128]{2,1,0:T(8,128)S(1)}, u32[]{:S(2)}, u32[]{:S(2)}) async-start(f32[8,165,128]{2,1,0:T(8,128)} %reshape.341), calls=%async_computation.4 | async-start | bytes 1376256 | tf_op jit(solution)/shard_map/all_to_all | solution.py:233
